TPU v7x, 512 devices: a whole 4x8x8 slice. The times are simulated.
512 devices in a mesh: seq: 16 (over y_lo, z), head: 8 (over x, core), dp: 4 (over y_hi).
Axes of the slice: x: 4, y: 8 (y_hi: 4, y_lo: 2; y = y_hi * 2 + y_lo), z: 8, core: 2. Of those that a mesh axis runs over, the one named last changes fastest.
Arguments:
- queries: bfloat16 [65536, 2048], P(('dp', 'seq', 'head')), parts along dimension 0, may hold values from -9 to 9
- keys: bfloat16 [65536, 2048], P(('dp', 'seq', 'head')), parts along dimension 0, may hold values from -9 to 9
- values: bfloat16 [65536, 2048], P(('dp', 'seq', 'head')), parts along dimension 0, may hold values from -6 to 6
- coords: int32 [3, 65536], P(None, ('dp', 'seq', 'head')), parts along dimension 1, may hold values from 0 to 511, as said below
- lengths: int32 [128], P('dp'), parts along dimension 0, may hold values from 1 to 1536, 16384 in all
Outputs:
- attention: bfloat16 [65536, 2048], P(('dp', 'seq', 'head')), parts along dimension 0
There are 4 independent parts, one for each index of `dp`. A program takes and returns all parts, laid end to end along the dimension named above; each array names one. Nothing has to cross between parts.
Inputs may be any that keep to these rules, and one draw needn't show every extreme that they name: `coords`: voxel coordinates of each token along x, y and z. `lengths`: the token counts of the 32 scenes of a pack in order; they sum to 16384 and the longest scene has exactly 1536 tokens.
All inputs are finite; a program needn't handle non-finite values.
Results may differ from a plain program's by a relative error of at most 0.012.
Values may be sent and summed in bfloat16 or wider, within the bound.
No kernel may reach another device: no remote copies, remote signals or barrier semaphores. Data moves between devices by JAX's collectives and lax.ppermute only.
A program may use at most 128 MiB of HBM per device.

v0:
```python
import jax
import jax.numpy as jnp
from jax import lax
from jax.sharding import PartitionSpec as P

HD = 64


score_scale = 0.125
neg_big = -1e30


def passed_along(block, axis, distance):
    devices = range(lax.axis_size(axis))
    route = [(i - distance, i) for i in devices if i - distance in devices]
    return lax.ppermute(block, axis, route)


def rotary_angles(coords):
    pair_count = HD // 2
    pair_id = jnp.arange(pair_count, dtype=jnp.int32)
    axis_of = 3 * pair_id // pair_count
    exponent = (3 * pair_id % pair_count).astype(jnp.float32) / pair_count
    frequency = jnp.power(jnp.float32(100.0), -exponent)
    position = coords.astype(jnp.float32)
    angles = jnp.zeros((coords.shape[1], pair_count), jnp.float32)
    for axis_id in range(3):
        picked = jnp.where(axis_of == axis_id, frequency, jnp.float32(0.0))
        angles = angles + position[axis_id][:, None] * picked[None, :]
    return angles


def rotate_rows(source, angles):
    row_count = source.shape[0]
    per_head = source.reshape(row_count, -1, HD).astype(jnp.float32)
    half_size = HD // 2
    front_half = per_head[..., :half_size]
    back_half = per_head[..., half_size:]
    cos_val = jnp.cos(angles)[:, None, :]
    sin_val = jnp.sin(angles)[:, None, :]
    turned = jnp.concatenate(
        [front_half * cos_val - back_half * sin_val, front_half * sin_val + back_half * cos_val],
        axis=-1,
    )
    return turned.reshape(row_count, -1)


def scene_of(positions, lengths):
    scene_end = jnp.cumsum(lengths)
    return jnp.sum((positions[:, None] >= scene_end[None, :]).astype(jnp.int32), axis=1)


def local(queries, keys, values, coords, lengths):
    tok_dev, all_cols = queries.shape
    head_count = lax.axis_size("head")
    seq_count = lax.axis_size("seq")
    head_cols = all_cols // head_count
    local_heads = head_cols // HD
    group_len = tok_dev * head_count
    total_len = group_len * seq_count
    reach = seq_count // 16 + 1
    angles = rotary_angles(coords)
    q_rot = (
        rotate_rows(queries, angles).astype(jnp.bfloat16).reshape(tok_dev, head_count, head_cols)
    )
    k_rot = rotate_rows(keys, angles).astype(jnp.bfloat16).reshape(tok_dev, head_count, head_cols)
    v_split = values.reshape(tok_dev, head_count, head_cols)
    q_blk, k_blk, v_blk = (
        lax.all_to_all(q_rot, "head", split_axis=1, concat_axis=0, tiled=True),
        lax.all_to_all(k_rot, "head", split_axis=1, concat_axis=0, tiled=True),
        lax.all_to_all(v_split, "head", split_axis=1, concat_axis=0, tiled=True),
    )
    q_heads = q_blk.reshape(group_len, local_heads, HD).transpose(1, 0, 2)
    k_local = k_blk.reshape(group_len, head_cols)
    v_local = v_blk.reshape(group_len, head_cols)
    own_start = lax.axis_index("seq") * group_len
    query_scene = scene_of(own_start + jnp.arange(group_len, dtype=jnp.int32), lengths)

    def attend(state_now, key_part, value_part, key_start):
        key_rows = key_part.shape[0]
        key_pos = key_start + jnp.arange(key_rows, dtype=jnp.int32)
        key_scene = scene_of(key_pos, lengths)
        valid_key = (key_pos >= 0) & (key_pos < total_len)
        allowed = (query_scene[:, None] == key_scene[None, :]) & valid_key[None, :]
        key_heads = key_part.reshape(key_rows, local_heads, HD).transpose(1, 0, 2)
        value_heads = value_part.reshape(key_rows, local_heads, HD).transpose(1, 0, 2)

        def one_head(operands):
            q_one, k_one, v_one, row_top, weight_sum, acc_rows = operands
            scores = jnp.dot(q_one, k_one.T, preferred_element_type=jnp.float32) * score_scale
            masked = jnp.where(allowed, scores, neg_big)
            new_top = jnp.maximum(row_top, jnp.max(masked, axis=1))
            raw_weights = jnp.where(allowed, jnp.exp(scores - new_top[:, None]), jnp.float32(0.0))
            shrink = jnp.exp(row_top - new_top)
            weight_sum = weight_sum * shrink + jnp.sum(raw_weights, axis=1)
            update = jnp.dot(
                raw_weights.astype(jnp.bfloat16), v_one, preferred_element_type=jnp.float32
            )
            acc_rows = acc_rows * shrink[:, None] + update
            return (new_top, weight_sum, acc_rows)

        return lax.map(one_head, (q_heads, key_heads, value_heads) + tuple(state_now))

    def visit(state_now, key_part, value_part, key_start):
        key_rows = key_part.shape[0]
        edge_pos = jnp.stack([key_start, key_start + key_rows - 1])
        edge_scene = scene_of(edge_pos, lengths)
        inside = (key_start + key_rows > 0) & (key_start < total_len)
        meets = inside & (edge_scene[0] <= query_scene[-1]) & (query_scene[0] <= edge_scene[1])
        return lax.cond(
            meets,
            lambda state: attend(state, key_part, value_part, key_start),
            lambda state: tuple(state),
            state_now,
        )

    state_now = (
        jnp.full((local_heads, group_len), neg_big, jnp.float32),
        jnp.zeros((local_heads, group_len), jnp.float32),
        jnp.zeros((local_heads, group_len, HD), jnp.float32),
    )
    state_now = visit(state_now, k_local, v_local, own_start)
    lower_k, lower_v = (k_local, v_local)
    upper_k, upper_v = (k_local, v_local)
    for distance in range(1, reach + 1):
        lower_k, lower_v = passed_along((lower_k, lower_v), "seq", 1)
        state_now = visit(state_now, lower_k, lower_v, own_start - distance * group_len)
        upper_k, upper_v = passed_along((upper_k, upper_v), "seq", -1)
        state_now = visit(state_now, upper_k, upper_v, own_start + distance * group_len)
    row_top, weight_sum, acc_rows = state_now
    finished = (
        (acc_rows / weight_sum[:, :, None])
        .transpose(1, 0, 2)
        .reshape(group_len, head_cols)
        .astype(jnp.bfloat16)
    )
    returned = lax.all_to_all(
        finished.reshape(group_len, 1, head_cols), "head", split_axis=0, concat_axis=1, tiled=True
    )
    return returned.reshape(tok_dev, all_cols)


def solution(mesh):
    in_specs = (
        P(("dp", "seq", "head"), None),
        P(("dp", "seq", "head"), None),
        P(("dp", "seq", "head"), None),
        P(None, ("dp", "seq", "head")),
        P("dp"),
    )
    out_specs = P(("dp", "seq", "head"), None)
    return jax.shard_map(local, mesh=mesh, in_specs=in_specs, out_specs=out_specs, check_vma=False)
```

profile of v0, /device:TPU:224, one launch (start us, length us, event | category | flops | bytes accessed | tf_op | source)
XLA Modules:
  0.0 323.7 jit_solution(11621187213473761469)
XLA Ops:
  5.0 4.3 %all-to-all-start = ((bf16[128,8,256]{0,2,1:T(8,128)(2,1)}), bf16[128,8,256]{0,2,1:T(8,128)(2,1)S(1)}, u32[]{:S(2)}, u32[]{:S(2)}) async-start(bf16[128,8,256]{0,2,1:T(8,128)(2,1)} %bitcast.51), calls=%async_computation | async-start | bytes 1048576 | tf_op jit(solution)/shard_map/all_to_all | solution.py:70
  10.3 9.3 %all-to-all-done = bf16[128,8,256]{0,2,1:T(8,128)(2,1)S(1)} async-done(((bf16[128,8,256]{0,2,1:T(8,128)(2,1)}), bf16[128,8,256]{0,2,1:T(8,128)(2,1)S(1)}, u32[]{:S(2)}, u32[]{:S(2)}) %all-to-all-start) | async-done | bytes 524320 | tf_op jit(solution)/shard_map/all_to_all | solution.py:70
  24.6 5.5 %collective-permute-start = (bf16[1024,256]{1,0:T(8,128)(2,1)S(1)}, bf16[1024,256]{1,0:T(8,128)(2,1)}, u32[]{:S(2)}, u32[]{:S(2)}) collective-permute-start(bf16[1024,256]{1,0:T(8,128)(2,1)S(1)} %bitcast.304), channel_id=1, source_target_pairs={{0,32},{32,64},{64,96},{96,128},{128,160},{160,192},{192,224},{224... | collective-permute-start | bytes 1572872 | tf_op jit(solution)/shard_map/ppermute | solution.py:16
  37.1 5.5 %collective-permute-start.1 = (bf16[1024,256]{1,0:T(8,128)(2,1)S(1)}, bf16[1024,256]{1,0:T(8,128)(2,1)}, u32[]{:S(2)}, u32[]{:S(2)}) collective-permute-start(bf16[1024,256]{1,0:T(8,128)(2,1)S(1)} %bitcast.307), channel_id=1, source_target_pairs={{0,32},{32,64},{64,96},{96,128},{128,160},{160,192},{192,224},{224... | collective-permute-start | bytes 1572872 | tf_op jit(solution)/shard_map/ppermute | solution.py:16
  44.8 5.1 %collective-permute-start.4 = (bf16[1024,256]{1,0:T(8,128)(2,1)}, bf16[1024,256]{1,0:T(8,128)(2,1)}, u32[]{:S(2)}, u32[]{:S(2)}) collective-permute-start(bf16[1024,256]{1,0:T(8,128)(2,1)} %collective-permute-done), channel_id=1, source_target_pairs={{0,32},{32,64},{64,96},{96,128},{128,160},{160,192},{192,224},{224... | collective-permute-start | bytes 1572872 | tf_op jit(solution)/shard_map/ppermute | solution.py:16
  50.0 4.9 %collective-permute-done.1 = bf16[1024,256]{1,0:T(8,128)(2,1)} collective-permute-done((bf16[1024,256]{1,0:T(8,128)(2,1)S(1)}, bf16[1024,256]{1,0:T(8,128)(2,1)}, u32[]{:S(2)}, u32[]{:S(2)}) %collective-permute-start.1) | collective-permute-done | bytes 524320 | tf_op jit(solution)/shard_map/ppermute | solution.py:16
  54.9 5.7 %collective-permute-start.5 = (bf16[1024,256]{1,0:T(8,128)(2,1)}, bf16[1024,256]{1,0:T(8,128)(2,1)}, u32[]{:S(2)}, u32[]{:S(2)}) collective-permute-start(bf16[1024,256]{1,0:T(8,128)(2,1)} %collective-permute-done.1), channel_id=1, source_target_pairs={{0,32},{32,64},{64,96},{96,128},{128,160},{160,192},{192,224},{224... | collective-permute-start | bytes 1572872 | tf_op jit(solution)/shard_map/ppermute | solution.py:16
  79.6 53.5 %conditional.5 = (f32[4,1024]{1,0:T(4,128)}, f32[4,1024]{1,0:T(4,128)}, f32[4,1024,64]{1,2,0:T(8,128)}) conditional(s32[]{:T(128)} %convert_element_type.131, () %tuple.58, (bf16[1024,1,256]{2,0,1:T(8,128)(2,1)S(1)}, bf16[1024,1,256]{2,0,1:T(8,128)(2,1)S(1)}, s32[1024]{0:T(1024)S(1)}, s32[]{:T(128)}, s32[32]{0:T(128)S(1)}, ...), branch_computations={%region_7.8_spmd, %region_8.15_spmd} | conditional | flops 286434272 | bytes 15441045 | solution.py:110
  81.2 51.9 %while.68 = (s32[]{:T(128)}, f32[4,1024]{1,0:T(4,128)}, f32[4,1024]{1,0:T(4,128)}, f32[4,1024,64]{1,2,0:T(8,128)}, bf16[4,1024,64]{1,2,0:T(8,128)(2,1)S(1)}, /*i...) while((s32[]{:T(128)}, f32[4,1024]{1,0:T(4,128)}, ...), condition=%wide.region_14.14_spmd.clone, body=%wide.region_11.13_spmd.clone.sunk | while | flops 286330880 | bytes 13329541 | solution.py:102
  89.9 4.3 %fusion.191 = f32[4,1024,64]{1,2,0:T(8,128)} fusion(f32[4,1024,64]{1,2,0:T(8,128)} %get-tuple-element.1916, s32[]{:T(128)S(6)} %copy.286, f32[1024,1024]{0,1:T(8,128)} %get-tuple-element.1722, s32[1024]{0:T(1024)S(1)} %get-tuple-element.1933, f32[1024]{0:T(1024)S(1)} %get-tuple-element.1721, s32[1024]{0:T(1024)S(1)} %get-tuple-element.1932, ...), kind=kOutput, calls=%fused_computation.13.clone.1 | convolution fusion | flops 140574720 | bytes 4605952 | tf_op jit(solution)/shard_map/cond/branch_1_fun/while/body/eval_jaxpr/dot_general | solution.py:96
  102.8 4.3 %fusion.191 = f32[4,1024,64]{1,2,0:T(8,128)} fusion(f32[4,1024,64]{1,2,0:T(8,128)} %get-tuple-element.1916, s32[]{:T(128)S(6)} %copy.286, f32[1024,1024]{0,1:T(8,128)} %get-tuple-element.1722, s32[1024]{0:T(1024)S(1)} %get-tuple-element.1933, f32[1024]{0:T(1024)S(1)} %get-tuple-element.1721, s32[1024]{0:T(1024)S(1)} %get-tuple-element.1932, ...), kind=kOutput, calls=%fused_computation.13.clone.1 | convolution fusion | flops 140574720 | bytes 4605952 | tf_op jit(solution)/shard_map/cond/branch_1_fun/while/body/eval_jaxpr/dot_general | solution.py:96
  115.8 4.3 %fusion.191 = f32[4,1024,64]{1,2,0:T(8,128)} fusion(f32[4,1024,64]{1,2,0:T(8,128)} %get-tuple-element.1916, s32[]{:T(128)S(6)} %copy.286, f32[1024,1024]{0,1:T(8,128)} %get-tuple-element.1722, s32[1024]{0:T(1024)S(1)} %get-tuple-element.1933, f32[1024]{0:T(1024)S(1)} %get-tuple-element.1721, s32[1024]{0:T(1024)S(1)} %get-tuple-element.1932, ...), kind=kOutput, calls=%fused_computation.13.clone.1 | convolution fusion | flops 140574720 | bytes 4605952 | tf_op jit(solution)/shard_map/cond/branch_1_fun/while/body/eval_jaxpr/dot_general | solution.py:96
  128.7 4.4 %fusion.191 = f32[4,1024,64]{1,2,0:T(8,128)} fusion(f32[4,1024,64]{1,2,0:T(8,128)} %get-tuple-element.1916, s32[]{:T(128)S(6)} %copy.286, f32[1024,1024]{0,1:T(8,128)} %get-tuple-element.1722, s32[1024]{0:T(1024)S(1)} %get-tuple-element.1933, f32[1024]{0:T(1024)S(1)} %get-tuple-element.1721, s32[1024]{0:T(1024)S(1)} %get-tuple-element.1932, ...), kind=kOutput, calls=%fused_computation.13.clone.1 | convolution fusion | flops 140574720 | bytes 4605952 | tf_op jit(solution)/shard_map/cond/branch_1_fun/while/body/eval_jaxpr/dot_general | solution.py:96
  133.1 43.7 %conditional.6 = ((f32[4,1024]{1,0:T(4,128)}, f32[4,1024]{1,0:T(4,128)}, f32[4,1024,64]{1,2,0:T(8,128)})) conditional(s32[]{:T(128)} %convert_element_type.129, (f32[4,1024]{1,0:T(4,128)}, f32[4,1024]{1,0:T(4,128)}, f32[4,1024,64]{1,2,0:T(8,128)}) %conditional.5, (bf16[1024,256]{1,0:T(8,128)(2,1)}, bf16[1024,256]{1,0:T(8,128)(2,1)}, ...), branch_computations={%region_15.16_spmd, %region_16.23_spmd} | conditional | flops 286499808 | bytes 34667760 | solution.py:110
  136.8 37.9 %while.69 = (s32[]{:T(128)}, f32[4,1024]{1,0:T(4,128)S(1)}, f32[4,1024]{1,0:T(4,128)S(1)}, f32[4,1024,64]{1,2,0:T(8,128)S(1)}, f32[4,1024]{1,0:T(4,128)}, /*inde...) while((s32[]{:T(128)}, f32[4,1024]{1,0:T(4,128)S(1)}, ...), condition=%wide.region_22.22_spmd.clone, body=%wide.region_19.21_spmd.clone.sunk | while | flops 286396416 | bytes 30393536 | solution.py:102
  142.6 3.6 %fusion.187 = f32[4,1024,64]{1,2,0:T(8,128)S(1)} fusion(f32[4,1024,64]{1,2,0:T(8,128)S(1)} %get-tuple-element.1874, s32[]{:T(128)S(6)} %copy.271, f32[1024,1024]{0,1:T(8,128)} %copy-done, s32[1024]{0:T(1024)S(1)} %get-tuple-element.1897, f32[1024]{0:T(1024)S(1)} %get-tuple-element.1706, s32[1024]{0:T(1024)S(1)} %get-tuple-element.1896, ...), kind=kOutput, calls=%fused_computation.36.clone.1 | convolution fusion | flops 140640256 | bytes 4868096 | tf_op jit(solution)/shard_map/cond/branch_1_fun/while/body/eval_jaxpr/dot_general | solution.py:96
  152.1 3.6 %fusion.187 = f32[4,1024,64]{1,2,0:T(8,128)S(1)} fusion(f32[4,1024,64]{1,2,0:T(8,128)S(1)} %get-tuple-element.1874, s32[]{:T(128)S(6)} %copy.271, f32[1024,1024]{0,1:T(8,128)} %copy-done, s32[1024]{0:T(1024)S(1)} %get-tuple-element.1897, f32[1024]{0:T(1024)S(1)} %get-tuple-element.1706, s32[1024]{0:T(1024)S(1)} %get-tuple-element.1896, ...), kind=kOutput, calls=%fused_computation.36.clone.1 | convolution fusion | flops 140640256 | bytes 4868096 | tf_op jit(solution)/shard_map/cond/branch_1_fun/while/body/eval_jaxpr/dot_general | solution.py:96
  161.5 3.6 %fusion.187 = f32[4,1024,64]{1,2,0:T(8,128)S(1)} fusion(f32[4,1024,64]{1,2,0:T(8,128)S(1)} %get-tuple-element.1874, s32[]{:T(128)S(6)} %copy.271, f32[1024,1024]{0,1:T(8,128)} %copy-done, s32[1024]{0:T(1024)S(1)} %get-tuple-element.1897, f32[1024]{0:T(1024)S(1)} %get-tuple-element.1706, s32[1024]{0:T(1024)S(1)} %get-tuple-element.1896, ...), kind=kOutput, calls=%fused_computation.36.clone.1 | convolution fusion | flops 140640256 | bytes 4868096 | tf_op jit(solution)/shard_map/cond/branch_1_fun/while/body/eval_jaxpr/dot_general | solution.py:96
  171.0 3.6 %fusion.187 = f32[4,1024,64]{1,2,0:T(8,128)S(1)} fusion(f32[4,1024,64]{1,2,0:T(8,128)S(1)} %get-tuple-element.1874, s32[]{:T(128)S(6)} %copy.271, f32[1024,1024]{0,1:T(8,128)} %copy-done, s32[1024]{0:T(1024)S(1)} %get-tuple-element.1897, f32[1024]{0:T(1024)S(1)} %get-tuple-element.1706, s32[1024]{0:T(1024)S(1)} %get-tuple-element.1896, ...), kind=kOutput, calls=%fused_computation.36.clone.1 | convolution fusion | flops 140640256 | bytes 4868096 | tf_op jit(solution)/shard_map/cond/branch_1_fun/while/body/eval_jaxpr/dot_general | solution.py:96
  176.8 43.8 %conditional.7 = ((f32[4,1024]{1,0:T(4,128)}, f32[4,1024]{1,0:T(4,128)}, f32[4,1024,64]{1,2,0:T(8,128)})) conditional(s32[]{:T(128)} %convert_element_type.127, (f32[4,1024]{1,0:T(4,128)}, f32[4,1024]{1,0:T(4,128)}, f32[4,1024,64]{1,2,0:T(8,128)}) %get-tuple-element.1965, (bf16[1024,256]{1,0:T(8,128)(2,1)}, bf16[1024,256]{1,0:T(8,128)(2,1)}, ...), branch_computations={%region_23.24_spmd, %region_24.31_spmd} | conditional | flops 286499808 | bytes 34667760 | solution.py:110
  180.5 37.9 %while.70 = (s32[]{:T(128)}, f32[4,1024]{1,0:T(4,128)S(1)}, f32[4,1024]{1,0:T(4,128)S(1)}, f32[4,1024,64]{1,2,0:T(8,128)S(1)}, f32[4,1024]{1,0:T(4,128)}, /*inde...) while((s32[]{:T(128)}, f32[4,1024]{1,0:T(4,128)S(1)}, ...), condition=%wide.region_30.30_spmd.clone, body=%wide.region_27.29_spmd.clone.sunk | while | flops 286396416 | bytes 30393536 | solution.py:102
  205.3 3.6 %fusion.183 = f32[4,1024,64]{1,2,0:T(8,128)S(1)} fusion(f32[4,1024,64]{1,2,0:T(8,128)S(1)} %get-tuple-element.1829, s32[]{:T(128)S(6)} %copy.256, f32[1024,1024]{0,1:T(8,128)} %copy-done.1, s32[1024]{0:T(1024)S(1)} %get-tuple-element.1852, f32[1024]{0:T(1024)S(1)} %get-tuple-element.1687, s32[1024]{0:T(1024)S(1)} %get-tuple-element.1851, ...), kind=kOutput, calls=%fused_computation.60.clone.1 | convolution fusion | flops 140640256 | bytes 4868096 | tf_op jit(solution)/shard_map/cond/branch_1_fun/while/body/eval_jaxpr/dot_general | solution.py:96
  214.8 3.6 %fusion.183 = f32[4,1024,64]{1,2,0:T(8,128)S(1)} fusion(f32[4,1024,64]{1,2,0:T(8,128)S(1)} %get-tuple-element.1829, s32[]{:T(128)S(6)} %copy.256, f32[1024,1024]{0,1:T(8,128)} %copy-done.1, s32[1024]{0:T(1024)S(1)} %get-tuple-element.1852, f32[1024]{0:T(1024)S(1)} %get-tuple-element.1687, s32[1024]{0:T(1024)S(1)} %get-tuple-element.1851, ...), kind=kOutput, calls=%fused_computation.60.clone.1 | convolution fusion | flops 140640256 | bytes 4868096 | tf_op jit(solution)/shard_map/cond/branch_1_fun/while/body/eval_jaxpr/dot_general | solution.py:96
  220.6 43.8 %conditional.8 = ((f32[4,1024]{1,0:T(4,128)}, f32[4,1024]{1,0:T(4,128)}, f32[4,1024,64]{1,2,0:T(8,128)})) conditional(s32[]{:T(128)} %convert_element_type.125, (f32[4,1024]{1,0:T(4,128)}, f32[4,1024]{1,0:T(4,128)}, f32[4,1024,64]{1,2,0:T(8,128)}) %get-tuple-element.1966, (bf16[1024,256]{1,0:T(8,128)(2,1)}, bf16[1024,256]{1,0:T(8,128)(2,1)}, ...), branch_computations={%region_31.32_spmd, %region_32.39_spmd} | conditional | flops 286499808 | bytes 34667760 | solution.py:110
  224.3 37.9 %while.71 = (s32[]{:T(128)}, f32[4,1024]{1,0:T(4,128)S(1)}, f32[4,1024]{1,0:T(4,128)S(1)}, f32[4,1024,64]{1,2,0:T(8,128)S(1)}, f32[4,1024]{1,0:T(4,128)}, /*inde...) while((s32[]{:T(128)}, f32[4,1024]{1,0:T(4,128)S(1)}, ...), condition=%wide.region_38.38_spmd.clone, body=%wide.region_35.37_spmd.clone.sunk | while | flops 286396416 | bytes 30393536 | solution.py:102
  230.2 3.6 %fusion.179 = f32[4,1024,64]{1,2,0:T(8,128)S(1)} fusion(f32[4,1024,64]{1,2,0:T(8,128)S(1)} %get-tuple-element.1784, s32[]{:T(128)S(6)} %copy.241, f32[1024,1024]{0,1:T(8,128)} %copy-done.2, s32[1024]{0:T(1024)S(1)} %get-tuple-element.1807, f32[1024]{0:T(1024)S(1)} %get-tuple-element.1668, s32[1024]{0:T(1024)S(1)} %get-tuple-element.1806, ...), kind=kOutput, calls=%fused_computation.84.clone.1 | convolution fusion | flops 140640256 | bytes 4868096 | tf_op jit(solution)/shard_map/cond/branch_1_fun/while/body/eval_jaxpr/dot_general | solution.py:96
  239.6 3.6 %fusion.179 = f32[4,1024,64]{1,2,0:T(8,128)S(1)} fusion(f32[4,1024,64]{1,2,0:T(8,128)S(1)} %get-tuple-element.1784, s32[]{:T(128)S(6)} %copy.241, f32[1024,1024]{0,1:T(8,128)} %copy-done.2, s32[1024]{0:T(1024)S(1)} %get-tuple-element.1807, f32[1024]{0:T(1024)S(1)} %get-tuple-element.1668, s32[1024]{0:T(1024)S(1)} %get-tuple-element.1806, ...), kind=kOutput, calls=%fused_computation.84.clone.1 | convolution fusion | flops 140640256 | bytes 4868096 | tf_op jit(solution)/shard_map/cond/branch_1_fun/while/body/eval_jaxpr/dot_general | solution.py:96
  249.1 3.6 %fusion.179 = f32[4,1024,64]{1,2,0:T(8,128)S(1)} fusion(f32[4,1024,64]{1,2,0:T(8,128)S(1)} %get-tuple-element.1784, s32[]{:T(128)S(6)} %copy.241, f32[1024,1024]{0,1:T(8,128)} %copy-done.2, s32[1024]{0:T(1024)S(1)} %get-tuple-element.1807, f32[1024]{0:T(1024)S(1)} %get-tuple-element.1668, s32[1024]{0:T(1024)S(1)} %get-tuple-element.1806, ...), kind=kOutput, calls=%fused_computation.84.clone.1 | convolution fusion | flops 140640256 | bytes 4868096 | tf_op jit(solution)/shard_map/cond/branch_1_fun/while/body/eval_jaxpr/dot_general | solution.py:96
  258.6 3.6 %fusion.179 = f32[4,1024,64]{1,2,0:T(8,128)S(1)} fusion(f32[4,1024,64]{1,2,0:T(8,128)S(1)} %get-tuple-element.1784, s32[]{:T(128)S(6)} %copy.241, f32[1024,1024]{0,1:T(8,128)} %copy-done.2, s32[1024]{0:T(1024)S(1)} %get-tuple-element.1807, f32[1024]{0:T(1024)S(1)} %get-tuple-element.1668, s32[1024]{0:T(1024)S(1)} %get-tuple-element.1806, ...), kind=kOutput, calls=%fused_computation.84.clone.1 | convolution fusion | flops 140640256 | bytes 4868096 | tf_op jit(solution)/shard_map/cond/branch_1_fun/while/body/eval_jaxpr/dot_general | solution.py:96
  264.4 39.3 %conditional.9 = ((f32[4,1024]{1,0:T(4,128)}, f32[4,1024,64]{1,2,0:T(8,128)})) conditional(s32[]{:T(128)} %convert_element_type.123, (f32[4,1024]{1,0:T(4,128)}, f32[4,1024,64]{1,2,0:T(8,128)}) %tuple.63, (bf16[1024,256]{1,0:T(8,128)(2,1)S(1)}, bf16[1024,256]{1,0:T(8,128)(2,1)S(1)}, s32[1024]{0:T(1024)S(1)}, s32[]{:T(128)}, s32[32]{0:T(128)S(1)}, ...), branch_computations={%region_39.40_spmd, %region_40.47_spmd} | conditional | flops 286499808 | bytes 34622676 | solution.py:110
  265.2 36.9 %while.72 = (s32[]{:T(128)}, f32[4,1024]{1,0:T(4,128)S(1)}, f32[4,1024,64]{1,2,0:T(8,128)S(1)}, f32[4,1024]{1,0:T(4,128)}, f32[4,1024]{1,0:T(4,128)}, /*index=5*...) while((s32[]{:T(128)}, f32[4,1024]{1,0:T(4,128)S(1)}, ...), condition=%wide.region_46.46_spmd.clone, body=%wide.region_43.45_spmd.clone.sunk | while | flops 286396416 | bytes 30381236 | solution.py:102
  306.9 14.9 %all_to_all.66 = bf16[8,2,16384]{2,1,0:T(2,128)(2,1)S(1)} all-to-all(bf16[8,2,16384]{2,1,0:T(2,128)(2,1)S(1)} %reshape.627), channel_id=1, replica_groups=mesh['seq'=16,'head'=8,'dp'=4] {'head'}, dimensions={0} | all-to-all | bytes 1048576 | tf_op jit(solution)/shard_map/all_to_all | solution.py:137
  (294 shorter events, 201.0 us)
Async XLA Ops:
  1.5 7.8 %copy-start.4 = (bf16[128,2048]{1,0:T(8,128)(2,1)S(1)}, bf16[128,2048]{1,0:T(8,128)(2,1)}, u32[]{:S(2)}) copy-start(bf16[128,2048]{1,0:T(8,128)(2,1)} %param.27) | copy-start | bytes 1572868
  3.6 19.6 %copy-start.5 = (s32[32]{0:T(128)S(1)}, s32[32]{0:T(128)}, u32[]{:S(2)}) copy-start(s32[32]{0:T(128)} %param.29) | copy-start | bytes 388
  5.0 14.6 %all-to-all-start = ((bf16[128,8,256]{0,2,1:T(8,128)(2,1)}), bf16[128,8,256]{0,2,1:T(8,128)(2,1)S(1)}, u32[]{:S(2)}, u32[]{:S(2)}) async-start(bf16[128,8,256]{0,2,1:T(8,128)(2,1)} %bitcast.51), calls=%async_computation | async-start | bytes 1048576 | tf_op jit(solution)/shard_map/all_to_all | solution.py:70
  19.6 13.7 %all-to-all-start.1 = ((bf16[128,8,256]{0,2,1:T(8,128)(2,1)}), bf16[128,8,256]{0,2,1:T(8,128)(2,1)S(1)}, u32[]{:S(2)}, u32[]{:S(2)}) async-start(bf16[128,8,256]{0,2,1:T(8,128)(2,1)} %bitcast.55), calls=%async_computation.1 | async-start | bytes 1048576 | tf_op jit(solution)/shard_map/all_to_all | solution.py:71
  24.6 20.3 %collective-permute-start = (bf16[1024,256]{1,0:T(8,128)(2,1)S(1)}, bf16[1024,256]{1,0:T(8,128)(2,1)}, u32[]{:S(2)}, u32[]{:S(2)}) collective-permute-start(bf16[1024,256]{1,0:T(8,128)(2,1)S(1)} %bitcast.304), channel_id=1, source_target_pairs={{0,32},{32,64},{64,96},{96,128},{128,160},{160,192},{192,224},{224... | collective-permute-start | bytes 1572872 | tf_op jit(solution)/shard_map/ppermute | solution.py:16
  30.1 30.5 %collective-permute-start.2 = (bf16[1024,256]{1,0:T(8,128)(2,1)S(1)}, bf16[1024,256]{1,0:T(8,128)(2,1)}, u32[]{:S(2)}, u32[]{:S(2)}) collective-permute-start(bf16[1024,256]{1,0:T(8,128)(2,1)S(1)} %bitcast.305), channel_id=1, source_target_pairs={{32,0},{64,32},{96,64},{128,96},{160,128},{192,160},{224,192},{256... | collective-permute-start | bytes 1572872 | tf_op jit(solution)/shard_map/ppermute | solution.py:16
  33.3 45.7 %all-to-all-start.2 = ((bf16[128,8,256]{0,2,1:T(8,128)(2,1)}), bf16[128,8,256]{0,2,1:T(8,128)(2,1)S(1)}, u32[]{:S(2)}, u32[]{:S(2)}) async-start(bf16[128,8,256]{0,2,1:T(8,128)(2,1)} %bitcast.61), calls=%async_computation.2 | async-start | bytes 1048576 | tf_op jit(solution)/shard_map/all_to_all | solution.py:69
  37.1 17.8 %collective-permute-start.1 = (bf16[1024,256]{1,0:T(8,128)(2,1)S(1)}, bf16[1024,256]{1,0:T(8,128)(2,1)}, u32[]{:S(2)}, u32[]{:S(2)}) collective-permute-start(bf16[1024,256]{1,0:T(8,128)(2,1)S(1)} %bitcast.307), channel_id=1, source_target_pairs={{0,32},{32,64},{64,96},{96,128},{128,160},{160,192},{192,224},{224... | collective-permute-start | bytes 1572872 | tf_op jit(solution)/shard_map/ppermute | solution.py:16
  42.6 19.9 %collective-permute-start.3 = (bf16[1024,256]{1,0:T(8,128)(2,1)S(1)}, bf16[1024,256]{1,0:T(8,128)(2,1)}, u32[]{:S(2)}, u32[]{:S(2)}) collective-permute-start(bf16[1024,256]{1,0:T(8,128)(2,1)S(1)} %bitcast.308), channel_id=1, source_target_pairs={{32,0},{64,32},{96,64},{128,96},{160,128},{192,160},{224,192},{256... | collective-permute-start | bytes 1572872 | tf_op jit(solution)/shard_map/ppermute | solution.py:16
  44.8 175.8 %collective-permute-start.4 = (bf16[1024,256]{1,0:T(8,128)(2,1)}, bf16[1024,256]{1,0:T(8,128)(2,1)}, u32[]{:S(2)}, u32[]{:S(2)}) collective-permute-start(bf16[1024,256]{1,0:T(8,128)(2,1)} %collective-permute-done), channel_id=1, source_target_pairs={{0,32},{32,64},{64,96},{96,128},{128,160},{160,192},{192,224},{224... | collective-permute-start | bytes 1572872 | tf_op jit(solution)/shard_map/ppermute | solution.py:16
  54.9 165.8 %collective-permute-start.5 = (bf16[1024,256]{1,0:T(8,128)(2,1)}, bf16[1024,256]{1,0:T(8,128)(2,1)}, u32[]{:S(2)}, u32[]{:S(2)}) collective-permute-start(bf16[1024,256]{1,0:T(8,128)(2,1)} %collective-permute-done.1), channel_id=1, source_target_pairs={{0,32},{32,64},{64,96},{96,128},{128,160},{160,192},{192,224},{224... | collective-permute-start | bytes 1572872 | tf_op jit(solution)/shard_map/ppermute | solution.py:16
  60.6 203.8 %collective-permute-start.6 = (bf16[1024,256]{1,0:T(8,128)(2,1)}, bf16[1024,256]{1,0:T(8,128)(2,1)S(1)}, u32[]{:S(2)}, u32[]{:S(2)}) collective-permute-start(bf16[1024,256]{1,0:T(8,128)(2,1)} %collective-permute-done.2), channel_id=1, source_target_pairs={{32,0},{64,32},{96,64},{128,96},{160,128},{192,160},{224,192},{256... | collective-permute-start | bytes 1572872 | tf_op jit(solution)/shard_map/ppermute | solution.py:16
  62.5 201.9 %collective-permute-start.7 = (bf16[1024,256]{1,0:T(8,128)(2,1)}, bf16[1024,256]{1,0:T(8,128)(2,1)S(1)}, u32[]{:S(2)}, u32[]{:S(2)}) collective-permute-start(bf16[1024,256]{1,0:T(8,128)(2,1)} %collective-permute-done.3), channel_id=1, source_target_pairs={{32,0},{64,32},{96,64},{128,96},{160,128},{192,160},{224,192},{256... | collective-permute-start | bytes 1572872 | tf_op jit(solution)/shard_map/ppermute | solution.py:16
  138.0 1.9 copy-start
  147.5 1.9 copy-start
  157.0 1.9 copy-start
  166.5 1.9 copy-start
  181.8 1.9 copy-start.1
  191.3 1.9 copy-start.1
  200.8 1.9 copy-start.1
  210.3 1.9 copy-start.1
  225.6 1.9 copy-start.2
  235.1 1.9 copy-start.2
  244.6 1.9 copy-start.2
  254.0 1.9 copy-start.2
  266.5 1.9 copy-start.3
  275.7 1.9 copy-start.3
  285.0 1.9 copy-start.3
  294.2 1.9 copy-start.3
where the time goes:
time: 329 us; the launch traced here: 324 us
  matrix products  106 us (32%)
  local copies, waits for them, and re-layouts  72.8 us (22%)
  other arithmetic  59.9 us (18%)
  starting transfers between devices  40.8 us (12%)
  waiting for transfers between devices  15.5 us (5%)
  blocking collectives  14.9 us (5%)
  between operations  12.6 us (4%)
    dot_general x20, matrix products, one_head(): jnp.dot(raw_weights.astype(jnp.bfloat16), v_one, preferred_element_type=j...  74.8 us
    reduce_sum x20, other arithmetic, one_head(): weight_sum = weight_sum * shrink + jnp.sum(raw_weights, axis=1)  39.7 us
    dot_general x20, matrix products, one_head(): jnp.dot(q_one, k_one.T, preferred_element_type=jnp.float32) * score_scale  31.2 us
    ppermute x8, starting transfers between devices, passed_along(): return lax.ppermute(block, axis, route)  29.5 us
    while x32, local copies, waits for them, and re-layouts  18.1 us
    all_to_all x1, blocking collectives, local(): lax.all_to_all(finished.reshape(group_len, 1, head_cols), 'head', split_a...  14.9 us
    dynamic_update_slice x36, local copies, waits for them, and re-layouts, attend(): lax.map(one_head, (q_heads, key_heads, value_heads) + tuple(state_now))  12.8 us
    dynamic_slice x16, local copies, waits for them, and re-layouts, attend(): lax.map(one_head, (q_heads, key_heads, value_heads) + tuple(state_now))  12.4 us
  transfers between devices with their start and end apart: 11, of which 3 were waited for; matrix products, arithmetic and copies ran while one was open for 54% of the time, Pallas kernels for 0%

commit v1 on v0

v1 whole, which is shorter than its diff:
```python
import functools

import jax
import jax.numpy as jnp
from jax import lax
from jax.experimental import pallas as pl
from jax.experimental.pallas import tpu as pltpu
from jax.sharding import PartitionSpec as P

HD = 64
MOST = 1536

score_scale = 0.125
neg_big = -1e30

TQ = 256
TK = 512


def shifted(block, axis, distance):
    devices = range(lax.axis_size(axis))
    route = [(i - distance, i) for i in devices if i - distance in devices]
    return lax.ppermute(block, axis, route)


def rotary_angles(coords):
    pair_count = HD // 2
    pair_id = jnp.arange(pair_count, dtype=jnp.int32)
    axis_of = 3 * pair_id // pair_count
    exponent = (3 * pair_id % pair_count).astype(jnp.float32) / pair_count
    frequency = jnp.power(jnp.float32(100.0), -exponent)
    position = coords.astype(jnp.float32)
    angles = jnp.zeros((coords.shape[1], pair_count), jnp.float32)
    for axis_id in range(3):
        picked = jnp.where(axis_of == axis_id, frequency, jnp.float32(0.0))
        angles = angles + position[axis_id][:, None] * picked[None, :]
    return angles


def rotate_rows(source, angles):
    row_count = source.shape[0]
    per_head = source.reshape(row_count, -1, HD).astype(jnp.float32)
    half_size = HD // 2
    front_half = per_head[..., :half_size]
    back_half = per_head[..., half_size:]
    cos_val = jnp.cos(angles)[:, None, :]
    sin_val = jnp.sin(angles)[:, None, :]
    turned = jnp.concatenate(
        [front_half * cos_val - back_half * sin_val, front_half * sin_val + back_half * cos_val],
        axis=-1,
    )
    return turned.reshape(row_count, -1)


def scene_of(positions, scene_end):
    return jnp.sum((positions[:, None] >= scene_end[None, :]).astype(jnp.int32), axis=1)


def flash_kernel(klo_ref, khi_ref, q_ref, k_ref, v_ref, qs_ref, ks_ref, o_ref):
    i = pl.program_id(1)
    q = q_ref[0]
    qs = qs_ref[...]
    tq = q.shape[0]

    def body(j, carry):
        m, l, acc = carry
        start = pl.multiple_of(j * TK, TK)
        k = k_ref[0, 0, pl.ds(start, TK), :]
        v = v_ref[0, 0, pl.ds(start, TK), :]
        ks = ks_ref[:, pl.ds(start, TK)]
        s = lax.dot_general(
            q, k, (((1,), (1,)), ((), ())), preferred_element_type=jnp.float32
        ) * score_scale
        s = jnp.where(qs == ks, s, neg_big)
        m_new = jnp.maximum(m, jnp.max(s, axis=1, keepdims=True))
        p = jnp.exp(s - m_new)
        alpha = jnp.exp(m - m_new)
        l = l * alpha + jnp.sum(p, axis=1, keepdims=True)
        acc = acc * alpha + jnp.dot(
            p.astype(jnp.bfloat16), v, preferred_element_type=jnp.float32
        )
        return m_new, l, acc

    init = (
        jnp.full((tq, 1), neg_big, jnp.float32),
        jnp.zeros((tq, 1), jnp.float32),
        jnp.zeros((tq, HD), jnp.float32),
    )
    m, l, acc = lax.fori_loop(klo_ref[i], khi_ref[i], body, init)
    o_ref[0] = (acc / l).astype(o_ref.dtype)


def flash(klo, khi, q_h, kv_win, q_scene, k_scene):
    heads, qlen, _ = q_h.shape
    wlen = kv_win.shape[2]
    grid = (heads, qlen // TQ)
    return pl.pallas_call(
        flash_kernel,
        out_shape=jax.ShapeDtypeStruct((heads, qlen, HD), jnp.bfloat16),
        grid_spec=pltpu.PrefetchScalarGridSpec(
            num_scalar_prefetch=2,
            grid=grid,
            in_specs=[
                pl.BlockSpec((1, TQ, HD), lambda h, i, *_: (h, i, 0)),
                pl.BlockSpec((1, 1, wlen, HD), lambda h, i, *_: (0, h, 0, 0)),
                pl.BlockSpec((1, 1, wlen, HD), lambda h, i, *_: (1, h, 0, 0)),
                pl.BlockSpec((TQ, 1), lambda h, i, *_: (i, 0)),
                pl.BlockSpec((1, wlen), lambda h, i, *_: (0, 0)),
            ],
            out_specs=pl.BlockSpec((1, TQ, HD), lambda h, i, *_: (h, i, 0)),
        ),
        compiler_params=pltpu.CompilerParams(
            dimension_semantics=("arbitrary", "arbitrary")
        ),
    )(klo, khi, q_h, kv_win, kv_win, q_scene, k_scene)


def local(queries, keys, values, coords, lengths):
    tok_dev, all_cols = queries.shape
    head_count = lax.axis_size("head")
    seq_count = lax.axis_size("seq")
    head_cols = all_cols // head_count
    local_heads = head_cols // HD
    group_len = tok_dev * head_count
    total_len = group_len * seq_count
    near = min(MOST, group_len)
    far = MOST - near
    angles = rotary_angles(coords)
    q_rot = rotate_rows(queries, angles).astype(jnp.bfloat16)
    k_rot = rotate_rows(keys, angles).astype(jnp.bfloat16)
    qkv = jnp.stack([q_rot, k_rot, values]).reshape(3, tok_dev, head_count, head_cols)
    blk = lax.all_to_all(qkv, "head", split_axis=2, concat_axis=1, tiled=True)
    blk = blk.reshape(3, group_len, local_heads, HD).transpose(0, 2, 1, 3)
    q_h = blk[0]
    kv = blk[1:]
    pieces = [kv]
    below = [shifted(kv, "seq", 1)]
    above = [shifted(kv, "seq", -1)]
    if far > 0:
        below.insert(0, shifted(kv[:, :, group_len - far:], "seq", 2))
        above.append(shifted(kv[:, :, :far], "seq", -2))
    kv_win = jnp.concatenate(below + pieces + above, axis=2)
    own_start = lax.axis_index("seq") * group_len
    win_start = own_start - group_len - far
    wlen = kv_win.shape[2]

    scene_end = jnp.cumsum(lengths).astype(jnp.int32)
    scene_begin = scene_end - lengths
    q_pos = own_start + jnp.arange(group_len, dtype=jnp.int32)
    q_scene = scene_of(q_pos, scene_end)
    k_pos = win_start + jnp.arange(wlen, dtype=jnp.int32)
    k_valid = (k_pos >= 0) & (k_pos < total_len)
    k_scene = jnp.where(k_valid, scene_of(k_pos, scene_end), -1)

    first_scene = q_scene[::TQ]
    last_scene = q_scene[TQ - 1 :: TQ]
    lo = jnp.take(scene_begin, first_scene) - win_start
    hi = jnp.take(scene_end, last_scene) - win_start
    lo = jnp.clip(lo, 0, wlen)
    hi = jnp.clip(hi, 0, wlen)
    klo = (lo // TK).astype(jnp.int32)
    khi = ((hi + TK - 1) // TK).astype(jnp.int32)

    out_h = flash(
        klo,
        khi,
        q_h,
        kv_win,
        q_scene.reshape(group_len, 1),
        k_scene.reshape(1, wlen).astype(jnp.int32),
    )
    finished = out_h.transpose(1, 0, 2).reshape(group_len, head_cols)
    returned = lax.all_to_all(
        finished.reshape(group_len, 1, head_cols), "head", split_axis=0, concat_axis=1, tiled=True
    )
    return returned.reshape(tok_dev, all_cols)


def solution(mesh):
    in_specs = (
        P(("dp", "seq", "head"), None),
        P(("dp", "seq", "head"), None),
        P(("dp", "seq", "head"), None),
        P(None, ("dp", "seq", "head")),
        P("dp"),
    )
    out_specs = P(("dp", "seq", "head"), None)
    return jax.shard_map(local, mesh=mesh, in_specs=in_specs, out_specs=out_specs, check_vma=False)
```

time: 329 us -> 177 us (0.54)
  the two profiles are of different devices: /device:TPU:224 before, /device:TPU:104 now
where the time goes in v1:
time: 177 us; the launch traced here: 176 us
  local copies, waits for them, and re-layouts  48.5 us (27%)
  waiting for transfers between devices  47.4 us (27%)
  Pallas kernels  39.1 us (22%)
  starting transfers between devices  22.8 us (13%)
  blocking collectives  12.8 us (7%)
  other arithmetic  4.87 us (3%)
    pallas_call x1, Pallas kernels, flash(): pl.pallas_call(flash_kernel, out_shape=jax.ShapeDtypeStruct((heads, qlen,...  39.1 us
    ppermute x4, waiting for transfers between devices, shifted(): return lax.ppermute(block, axis, route)  27.9 us
    all_to_all x1, waiting for transfers between devices, local(): blk = lax.all_to_all(qkv, 'head', split_axis=2, concat_axis=1, tiled=True)  19.6 us
    ppermute x4, starting transfers between devices, shifted(): return lax.ppermute(block, axis, route)  18.5 us
    unnamed x17, local copies, waits for them, and re-layouts  12.8 us
    all_to_all x1, blocking collectives, local(): lax.all_to_all(finished.reshape(group_len, 1, head_cols), 'head', split_a...  12.8 us
    ppermute x4, local copies, waits for them, and re-layouts, shifted(): return lax.ppermute(block, axis, route)  9.72 us
    reshape x2, local copies, waits for them, and re-layouts, local(): blk = blk.reshape(3, group_len, local_heads, HD).transpose(0, 2, 1, 3)  5.19 us
  transfers between devices with their start and end apart: 5, of which 2 were waited for; matrix products, arithmetic and copies ran while one was open for 15% of the time, Pallas kernels for 0%

profile of v1, /device:TPU:104, one launch (start us, length us, event | category | flops | bytes accessed | tf_op | source)
XLA Modules:
  0.0 175.7 jit_solution(583239898732294114)
XLA Ops:
  0.8 1.3 copy.48
  2.2 1.3 copy.49
  4.7 1.3 copy.51
  6.0 4.3 %all-to-all-start = ((bf16[3,128,8,256]{1,3,0,2:T(8,128)(2,1)}), bf16[3,128,8,256]{1,3,0,2:T(8,128)(2,1)S(1)}, u32[]{:S(2)}, u32[]{:S(2)}) async-start(bf16[3,128,8,256]{1,3,0,2:T(8,128)(2,1)} %copy.51), calls=%async_computation | async-start | bytes 3145728 | tf_op jit(solution)/shard_map/all_to_all | solution.py:132
  12.3 19.6 %all-to-all-done = bf16[3,128,8,256]{1,3,0,2:T(8,128)(2,1)S(1)} async-done(((bf16[3,128,8,256]{1,3,0,2:T(8,128)(2,1)}), bf16[3,128,8,256]{1,3,0,2:T(8,128)(2,1)S(1)}, u32[]{:S(2)}, u32[]{:S(2)}) %all-to-all-start) | async-done | bytes 1572896 | tf_op jit(solution)/shard_map/all_to_all | solution.py:132
  32.9 2.1 %reshape.308 = bf16[3,1024,4,64]{1,3,2,0:T(8,128)(2,1)} reshape(bf16[3,8,128,1,256]{2,1,4,0,3:T(8,128)(2,1)S(1)} %copy.52) | data formatting | bytes 3145728 | tf_op jit(solution)/shard_map/reshape | solution.py:133
  34.9 3.1 %copy.53 = bf16[3,1024,4,64]{3,1,2,0:T(8,128)(2,1)S(1)} copy(bf16[3,1024,4,64]{1,3,2,0:T(8,128)(2,1)} %reshape.308) | data formatting | bytes 3145728 | tf_op jit(solution)/shard_map/reshape | solution.py:133
  38.1 1.5 slice.64
  39.6 2.7 %copy.55 = bf16[2,4,1024,64]{2,3,1,0:T(8,128)(2,1)} copy(bf16[2,4,1024,64]{3,2,1,0:T(8,128)(2,1)} %slice.64) | data formatting | bytes 2097152 | tf_op jit(solution)/shard_map/slice | solution.py:135
  42.2 4.3 %collective-permute-start.1 = (bf16[2,4,1024,64]{2,3,1,0:T(8,128)(2,1)}, bf16[2,4,1024,64]{2,3,1,0:T(8,128)(2,1)}, u32[]{:S(2)}, u32[]{:S(2)}) collective-permute-start(bf16[2,4,1024,64]{2,3,1,0:T(8,128)(2,1)} %copy.55), channel_id=1, source_target_pairs={{0,32},{32,64},{64,96},{96,128},{128,160},{160,192},{192,224},{224... | collective-permute-start | bytes 3145736 | tf_op jit(solution)/shard_map/ppermute | solution.py:23
  46.5 1.6 fusion.6
  48.1 2.3 %copy.54 = bf16[2,4,512,64]{2,3,1,0:T(8,128)(2,1)} copy(bf16[2,4,512,64]{3,2,1,0:T(8,128)(2,1)} %get-tuple-element.7) | data formatting | bytes 1048576 | tf_op jit(solution)/shard_map/slice | solution.py:140
  50.4 7.3 %collective-permute-start = (bf16[2,4,512,64]{2,3,1,0:T(8,128)(2,1)}, bf16[2,4,512,64]{2,3,1,0:T(8,128)(2,1)}, u32[]{:S(2)}, u32[]{:S(2)}) collective-permute-start(bf16[2,4,512,64]{2,3,1,0:T(8,128)(2,1)} %copy.54), channel_id=1, source_target_pairs={{0,64},{32,96},{64,128},{96,160},{128,192},{160,224},{192,256},{22... | collective-permute-start | bytes 1572872 | tf_op jit(solution)/shard_map/ppermute | solution.py:23
  57.7 2.3 %copy.57 = bf16[2,4,512,64]{2,3,1,0:T(8,128)(2,1)} copy(bf16[2,4,512,64]{3,2,1,0:T(8,128)(2,1)} %get-tuple-element.6) | data formatting | bytes 1048576 | tf_op jit(solution)/shard_map/slice | solution.py:141
  60.0 3.1 %collective-permute-start.3 = (bf16[2,4,512,64]{2,3,1,0:T(8,128)(2,1)}, bf16[2,4,512,64]{2,3,1,0:T(8,128)(2,1)}, u32[]{:S(2)}, u32[]{:S(2)}) collective-permute-start(bf16[2,4,512,64]{2,3,1,0:T(8,128)(2,1)} %copy.57), channel_id=1, source_target_pairs={{64,0},{96,32},{128,64},{160,96},{192,128},{224,160},{256,192},{28... | collective-permute-start | bytes 1572872 | tf_op jit(solution)/shard_map/ppermute | solution.py:23
  63.7 1.0 copy.62.qs_ref
  65.4 3.9 %collective-permute-start.2 = (bf16[2,4,1024,64]{2,3,1,0:T(8,128)(2,1)}, bf16[2,4,1024,64]{2,3,1,0:T(8,128)(2,1)}, u32[]{:S(2)}, u32[]{:S(2)}) collective-permute-start(bf16[2,4,1024,64]{2,3,1,0:T(8,128)(2,1)} %copy.55), channel_id=1, source_target_pairs={{32,0},{64,32},{96,64},{128,96},{160,128},{192,160},{224,192},{256... | collective-permute-start | bytes 3145736 | tf_op jit(solution)/shard_map/ppermute | solution.py:23
  69.8 1.0 slice_bitcast_fusion.q_ref
  70.8 27.9 %collective-permute-done = bf16[2,4,512,64]{2,3,1,0:T(8,128)(2,1)} collective-permute-done((bf16[2,4,512,64]{2,3,1,0:T(8,128)(2,1)}, bf16[2,4,512,64]{2,3,1,0:T(8,128)(2,1)}, u32[]{:S(2)}, u32[]{:S(2)}) %collective-permute-start) | collective-permute-done | bytes 524320 | tf_op jit(solution)/shard_map/ppermute | solution.py:23
  98.7 2.5 %copy.58 = bf16[2,4,512,64]{3,2,1,0:T(8,128)(2,1)} copy(bf16[2,4,512,64]{2,3,1,0:T(8,128)(2,1)} %collective-permute-done) | data formatting | bytes 1048576 | tf_op jit(solution)/shard_map/ppermute | solution.py:23
  101.2 2.4 %copy.61 = bf16[2,4,512,64]{3,2,1,0:T(8,128)(2,1)} copy(bf16[2,4,512,64]{2,3,1,0:T(8,128)(2,1)} %collective-permute-done.3) | data formatting | bytes 1048576 | tf_op jit(solution)/shard_map/ppermute | solution.py:23
  103.5 2.4 %constant_dynamic-update-slice_fusion.4 = bf16[2,4,4096,64]{3,2,1,0:T(8,128)(2,1)} fusion(bf16[2,4,512,64]{3,2,1,0:T(8,128)(2,1)} %copy.58), kind=kLoop, calls=%fused_computation.21 | loop fusion | bytes 1572864
  105.9 2.8 %copy.59 = bf16[2,4,1024,64]{3,2,1,0:T(8,128)(2,1)} copy(bf16[2,4,1024,64]{2,3,1,0:T(8,128)(2,1)} %collective-permute-done.1) | data formatting | bytes 2097152 | tf_op jit(solution)/shard_map/ppermute | solution.py:23
  108.7 3.3 %constant_dynamic-update-slice_fusion.3 = bf16[2,4,4096,64]{3,2,1,0:T(8,128)(2,1)} fusion(bf16[2,4,4096,64]{3,2,1,0:T(8,128)(2,1)} %constant_dynamic-update-slice_fusion.4, bf16[2,4,1024,64]{3,2,1,0:T(8,128)(2,1)} %copy.59), kind=kLoop, calls=%fused_computation.20 | loop fusion | bytes 4194304
  112.0 1.6 constant_dynamic-update-slice_fusion.2
  113.6 2.1 %copy.60 = bf16[2,4,1024,64]{3,2,1,0:T(8,128)(2,1)S(1)} copy(bf16[2,4,1024,64]{2,3,1,0:T(8,128)(2,1)} %collective-permute-done.2) | data formatting | bytes 2097152 | tf_op jit(solution)/shard_map/ppermute | solution.py:23
  115.7 1.7 constant_dynamic-update-slice_fusion.1
  117.4 1.1 constant_dynamic-update-slice_fusion.k_ref.v_ref
  118.5 39.1 %shard_map.55 = bf16[4,1024,64]{2,1,0:T(8,128)(2,1)} custom-call(s32[4]{0:T(128)} %and_select_fusion.6.klo_ref, s32[4]{0:T(128)} %and_select_fusion.5.khi_ref, bf16[4,1024,64]{2,1,0:T(8,128)(2,1)} %slice_bitcast_fusion.q_ref, bf16[2,4,4096,64]{3,2,1,0:T(8,128)(2,1)} %constant_dynamic-update-slice_fusion.k_ref.v_ref, ...), custom_call_target="tpu_custom_call" | custom-call | tf_op jit(solution)/shard_map/pallas_call | solution.py:97
  157.6 1.5 copy.63
  159.7 1.0 reduce.1
  161.1 12.8 %all_to_all.30 = bf16[8,2,16384]{2,1,0:T(2,128)(2,1)S(1)} all-to-all(bf16[8,2,16384]{2,1,0:T(2,128)(2,1)S(1)} %reshape.336), channel_id=1, replica_groups=mesh['seq'=16,'head'=8,'dp'=4] {'head'}, dimensions={0} | all-to-all | bytes 1048576 | tf_op jit(solution)/shard_map/all_to_all | solution.py:173
  (47 shorter events, 9.4 us)
Async XLA Ops:
  0.0 3.7 %copy-start.1 = (bf16[128,2048]{1,0:T(8,128)(2,1)S(1)}, bf16[128,2048]{1,0:T(8,128)(2,1)}, u32[]{:S(2)}) copy-start(bf16[128,2048]{1,0:T(8,128)(2,1)} %param.9) | copy-start | bytes 1572868
  4.7 5.6 %copy-start.2 = (s32[32]{0:T(128)S(1)}, s32[32]{0:T(128)}, u32[]{:S(2)}) copy-start(s32[32]{0:T(128)} %param.11) | copy-start | bytes 388
  6.0 25.9 %all-to-all-start = ((bf16[3,128,8,256]{1,3,0,2:T(8,128)(2,1)}), bf16[3,128,8,256]{1,3,0,2:T(8,128)(2,1)S(1)}, u32[]{:S(2)}, u32[]{:S(2)}) async-start(bf16[3,128,8,256]{1,3,0,2:T(8,128)(2,1)} %copy.51), calls=%async_computation | async-start | bytes 3145728 | tf_op jit(solution)/shard_map/all_to_all | solution.py:132
  42.2 63.7 %collective-permute-start.1 = (bf16[2,4,1024,64]{2,3,1,0:T(8,128)(2,1)}, bf16[2,4,1024,64]{2,3,1,0:T(8,128)(2,1)}, u32[]{:S(2)}, u32[]{:S(2)}) collective-permute-start(bf16[2,4,1024,64]{2,3,1,0:T(8,128)(2,1)} %copy.55), channel_id=1, source_target_pairs={{0,32},{32,64},{64,96},{96,128},{128,160},{160,192},{192,224},{224... | collective-permute-start | bytes 3145736 | tf_op jit(solution)/shard_map/ppermute | solution.py:23
  50.4 48.3 %collective-permute-start = (bf16[2,4,512,64]{2,3,1,0:T(8,128)(2,1)}, bf16[2,4,512,64]{2,3,1,0:T(8,128)(2,1)}, u32[]{:S(2)}, u32[]{:S(2)}) collective-permute-start(bf16[2,4,512,64]{2,3,1,0:T(8,128)(2,1)} %copy.54), channel_id=1, source_target_pairs={{0,64},{32,96},{64,128},{96,160},{128,192},{160,224},{192,256},{22... | collective-permute-start | bytes 1572872 | tf_op jit(solution)/shard_map/ppermute | solution.py:23
  60.0 41.1 %collective-permute-start.3 = (bf16[2,4,512,64]{2,3,1,0:T(8,128)(2,1)}, bf16[2,4,512,64]{2,3,1,0:T(8,128)(2,1)}, u32[]{:S(2)}, u32[]{:S(2)}) collective-permute-start(bf16[2,4,512,64]{2,3,1,0:T(8,128)(2,1)} %copy.57), channel_id=1, source_target_pairs={{64,0},{96,32},{128,64},{160,96},{192,128},{224,160},{256,192},{28... | collective-permute-start | bytes 1572872 | tf_op jit(solution)/shard_map/ppermute | solution.py:23
  65.4 48.3 %collective-permute-start.2 = (bf16[2,4,1024,64]{2,3,1,0:T(8,128)(2,1)}, bf16[2,4,1024,64]{2,3,1,0:T(8,128)(2,1)}, u32[]{:S(2)}, u32[]{:S(2)}) collective-permute-start(bf16[2,4,1024,64]{2,3,1,0:T(8,128)(2,1)} %copy.55), channel_id=1, source_target_pairs={{32,0},{64,32},{96,64},{128,96},{160,128},{192,160},{224,192},{256... | collective-permute-start | bytes 3145736 | tf_op jit(solution)/shard_map/ppermute | solution.py:23
  113.6 3.8 %copy-start = (bf16[2,4,512,64]{3,2,1,0:T(8,128)(2,1)S(1)}, bf16[2,4,512,64]{3,2,1,0:T(8,128)(2,1)}, u32[]{:S(2)}) copy-start(bf16[2,4,512,64]{3,2,1,0:T(8,128)(2,1)} %copy.61) | copy-start | bytes 1572868

commit v2 on v1

v2 whole, which is shorter than its diff:
```python
import jax
import jax.numpy as jnp
from jax import lax
from jax.experimental import pallas as pl
from jax.experimental.pallas import tpu as pltpu
from jax.sharding import PartitionSpec as P

HD = 64
MOST = 1536

score_scale = 0.125
neg_big = -1e30

TQ = 256
TK = 256


def shifted(block, axis, distance):
    devices = range(lax.axis_size(axis))
    route = [(i - distance, i) for i in devices if i - distance in devices]
    return lax.ppermute(block, axis, route)


def rotary_angles(coords):
    pair_count = HD // 2
    pair_id = jnp.arange(pair_count, dtype=jnp.int32)
    axis_of = 3 * pair_id // pair_count
    exponent = (3 * pair_id % pair_count).astype(jnp.float32) / pair_count
    frequency = jnp.power(jnp.float32(100.0), -exponent)
    position = coords.astype(jnp.float32)
    angles = jnp.zeros((coords.shape[1], pair_count), jnp.float32)
    for axis_id in range(3):
        picked = jnp.where(axis_of == axis_id, frequency, jnp.float32(0.0))
        angles = angles + position[axis_id][:, None] * picked[None, :]
    return angles


def rotate_rows(source, angles, scale=None):
    row_count = source.shape[0]
    per_head = source.reshape(row_count, -1, HD).astype(jnp.float32)
    half_size = HD // 2
    front_half = per_head[..., :half_size]
    back_half = per_head[..., half_size:]
    cos_val = jnp.cos(angles)[:, None, :]
    sin_val = jnp.sin(angles)[:, None, :]
    turned = jnp.concatenate(
        [front_half * cos_val - back_half * sin_val, front_half * sin_val + back_half * cos_val],
        axis=-1,
    )
    if scale is not None:
        turned = turned * jnp.float32(scale)
    return turned


def scene_of(positions, scene_end):
    return jnp.sum((positions[:, None] >= scene_end[None, :]).astype(jnp.int32), axis=1)


def make_kernel(piece_rows, nq, has_state, finalize):
    n_pieces = len(piece_rows)
    ktmax = max(piece_rows) // TK

    def kernel(lo_ref, hi_ref, full_ref, q_ref, qs_ref, *rest):
        piece_refs = rest[: 3 * n_pieces]
        rest = rest[3 * n_pieces :]
        if has_state:
            m_in, l_in, acc_in = rest[:3]
            rest = rest[3:]
        outs = rest
        i = pl.program_id(1)
        q = q_ref[0, 0]
        qs = qs_ref[...]
        tq = q.shape[0]
        if has_state:
            carry = (m_in[0], l_in[0], acc_in[0])
        else:
            carry = (
                jnp.full((tq, 1), neg_big, jnp.float32),
                jnp.zeros((tq, 1), jnp.float32),
                jnp.zeros((tq, HD), jnp.float32),
            )
        for p in range(n_pieces):
            k_ref, v_ref, ks_ref = piece_refs[3 * p : 3 * p + 3]
            base = p * nq + i

            def update(start, carry, masked, k_ref=k_ref, v_ref=v_ref, ks_ref=ks_ref):
                m, l, acc = carry
                k = k_ref[0, 0, pl.ds(start, TK), :]
                v = v_ref[0, 0, pl.ds(start, TK), :]
                s = lax.dot_general(
                    q, k, (((1,), (1,)), ((), ())), preferred_element_type=jnp.float32
                )
                if masked:
                    ks = ks_ref[:, pl.ds(start, TK)]
                    s = jnp.where(qs == ks, s, neg_big)
                m_new = jnp.maximum(m, jnp.max(s, axis=1, keepdims=True))
                p_w = jnp.exp(s - m_new)
                alpha = jnp.exp(m - m_new)
                l = l * alpha + jnp.sum(p_w, axis=1, keepdims=True)
                acc = acc * alpha + jnp.dot(
                    p_w.astype(jnp.bfloat16), v, preferred_element_type=jnp.float32
                )
                return m_new, l, acc

            def body(j, carry, base=base, update=update):
                start = pl.multiple_of(j * TK, TK)
                full = full_ref[base * ktmax + j]
                return lax.cond(
                    full != 0,
                    lambda c: update(start, c, False),
                    lambda c: update(start, c, True),
                    carry,
                )

            carry = lax.fori_loop(lo_ref[base], hi_ref[base], body, carry)
        m, l, acc = carry
        if finalize:
            outs[0][0, 0] = (acc / l).astype(outs[0].dtype)
        else:
            outs[0][0] = m
            outs[1][0] = l
            outs[2][0] = acc

    return kernel


def attend(q_h, q_scene, pieces, lo, hi, full, state):
    heads, qlen, _ = q_h.shape[1:] if q_h.ndim == 4 else q_h.shape
    nq = qlen // TQ
    piece_rows = [kv.shape[2] for kv, _ in pieces]
    has_state = state is not None
    finalize = has_state
    kernel = make_kernel(piece_rows, nq, has_state, finalize)
    in_specs = [
        pl.BlockSpec((1, 1, TQ, HD), lambda h, i, *_: (0, h, i, 0)),
        pl.BlockSpec((TQ, 1), lambda h, i, *_: (i, 0)),
    ]
    args = [q_h, q_scene]
    for kv, ks in pieces:
        rows = kv.shape[2]
        in_specs.append(pl.BlockSpec((1, 1, rows, HD), lambda h, i, *_: (0, h, 0, 0)))
        in_specs.append(pl.BlockSpec((1, 1, rows, HD), lambda h, i, *_: (1, h, 0, 0)))
        in_specs.append(pl.BlockSpec((1, rows), lambda h, i, *_: (0, 0)))
        args += [kv, kv, ks]
    state_specs = [
        pl.BlockSpec((1, TQ, 1), lambda h, i, *_: (h, i, 0)),
        pl.BlockSpec((1, TQ, 1), lambda h, i, *_: (h, i, 0)),
        pl.BlockSpec((1, TQ, HD), lambda h, i, *_: (h, i, 0)),
    ]
    state_shapes = [
        jax.ShapeDtypeStruct((heads, qlen, 1), jnp.float32),
        jax.ShapeDtypeStruct((heads, qlen, 1), jnp.float32),
        jax.ShapeDtypeStruct((heads, qlen, HD), jnp.float32),
    ]
    if has_state:
        in_specs += state_specs
        args += list(state)
    if finalize:
        out_specs = [pl.BlockSpec((1, 1, TQ, HD), lambda h, i, *_: (0, h, i, 0))]
        out_shape = [jax.ShapeDtypeStruct((1, heads, qlen, HD), jnp.bfloat16)]
    else:
        out_specs = state_specs
        out_shape = state_shapes
    return pl.pallas_call(
        kernel,
        out_shape=out_shape,
        grid_spec=pltpu.PrefetchScalarGridSpec(
            num_scalar_prefetch=3,
            grid=(heads, nq),
            in_specs=in_specs,
            out_specs=out_specs,
        ),
        compiler_params=pltpu.CompilerParams(
            dimension_semantics=("arbitrary", "arbitrary")
        ),
    )(lo, hi, full, *args)


def local(queries, keys, values, coords, lengths):
    tok_dev, all_cols = queries.shape
    head_count = lax.axis_size("head")
    seq_count = lax.axis_size("seq")
    head_cols = all_cols // head_count
    local_heads = head_cols // HD
    group_len = tok_dev * head_count
    total_len = group_len * seq_count
    near = min(MOST, group_len)
    far = MOST - near
    nq = group_len // TQ

    def head_major(x):
        return x.reshape(tok_dev, head_count, local_heads, HD).transpose(1, 2, 0, 3)

    angles = rotary_angles(coords)
    q_rot = head_major(rotate_rows(queries, angles, score_scale).astype(jnp.bfloat16))
    k_rot = head_major(rotate_rows(keys, angles).astype(jnp.bfloat16))
    v_hm = head_major(values)
    kv_src = jnp.stack([k_rot, v_hm])
    kv = lax.all_to_all(kv_src, "head", split_axis=1, concat_axis=3, tiled=True)
    kv = kv.reshape(2, local_heads, group_len, HD)
    q_h = lax.all_to_all(q_rot, "head", split_axis=0, concat_axis=2, tiled=True)

    below1 = shifted(kv, "seq", 1)
    above1 = shifted(kv, "seq", -1)
    halo = [(below1, -group_len), (above1, group_len)]
    if far > 0:
        below2 = shifted(kv[:, :, group_len - far :], "seq", 2)
        above2 = shifted(kv[:, :, :far], "seq", -2)
        halo = [(below2, -group_len - far)] + halo + [(above2, 2 * group_len)]

    own_start = lax.axis_index("seq") * group_len
    scene_end = jnp.cumsum(lengths).astype(jnp.int32)
    scene_begin = scene_end - lengths
    q_pos = own_start + jnp.arange(group_len, dtype=jnp.int32)
    q_scene = scene_of(q_pos, scene_end)
    first_scene = q_scene[::TQ]
    last_scene = q_scene[TQ - 1 :: TQ]
    span_lo = jnp.take(scene_begin, first_scene)
    span_hi = jnp.take(scene_end, last_scene)
    q_single = first_scene == last_scene

    def tables(piece_list):
        ktmax = max(kvp.shape[2] for kvp, _ in piece_list) // TK
        los, his, fulls, prepared = [], [], [], []
        for kvp, offset in piece_list:
            rows = kvp.shape[2]
            p0 = own_start + offset
            k_pos = p0 + jnp.arange(rows, dtype=jnp.int32)
            k_valid = (k_pos >= 0) & (k_pos < total_len)
            k_scene = jnp.where(k_valid, scene_of(k_pos, scene_end), -1).astype(jnp.int32)
            lo = jnp.clip(span_lo - p0, 0, rows)
            hi = jnp.clip(span_hi - p0, 0, rows)
            klo = lo // TK
            khi = jnp.maximum((hi + TK - 1) // TK, klo)
            los.append(klo)
            his.append(khi)
            kt_first = k_scene[::TK]
            kt_last = k_scene[TK - 1 :: TK]
            kfull = (
                q_single[:, None]
                & (kt_first[None, :] == first_scene[:, None])
                & (kt_last[None, :] == first_scene[:, None])
            )
            kfull = jnp.pad(kfull, ((0, 0), (0, ktmax - kfull.shape[1])))
            fulls.append(kfull.reshape(-1))
            prepared.append((kvp, k_scene.reshape(1, rows)))
        return (
            jnp.concatenate(los).astype(jnp.int32),
            jnp.concatenate(his).astype(jnp.int32),
            jnp.concatenate(fulls).astype(jnp.int32),
            prepared,
        )

    q_scene_col = q_scene.reshape(group_len, 1).astype(jnp.int32)
    lo0, hi0, full0, prep0 = tables([(kv, 0)])
    state = attend(q_h, q_scene_col, prep0, lo0, hi0, full0, None)
    lo1, hi1, full1, prep1 = tables(halo)
    out_h = attend(q_h, q_scene_col, prep1, lo1, hi1, full1, state)[0]

    out_src = out_h.reshape(local_heads, head_count, tok_dev, HD)
    back = lax.all_to_all(out_src, "head", split_axis=1, concat_axis=0, tiled=True)
    back = back.reshape(head_count * local_heads, tok_dev, HD)
    return back.transpose(1, 0, 2).reshape(tok_dev, all_cols)


def solution(mesh):
    in_specs = (
        P(("dp", "seq", "head"), None),
        P(("dp", "seq", "head"), None),
        P(("dp", "seq", "head"), None),
        P(None, ("dp", "seq", "head")),
        P("dp"),
    )
    out_specs = P(("dp", "seq", "head"), None)
    return jax.shard_map(local, mesh=mesh, in_specs=in_specs, out_specs=out_specs, check_vma=False)
```

time: 177 us -> 185 us (1.045)
  the two profiles are of different devices: /device:TPU:104 before, /device:TPU:296 now
where the time goes in v2:
time: 185 us; the launch traced here: 184 us
  Pallas kernels  100 us (54%)
  local copies, waits for them, and re-layouts  28.3 us (15%)
  starting transfers between devices  23.4 us (13%)
  blocking collectives  14.8 us (8%)
  waiting for transfers between devices  10.3 us (6%)
  other arithmetic  6.72 us (4%)
    pallas_call x2, Pallas kernels, attend(): pl.pallas_call(kernel, out_shape=out_shape, grid_spec=pltpu.PrefetchScala...  100 us
    ppermute x4, starting transfers between devices, shifted(): return lax.ppermute(block, axis, route)  15 us
    all_to_all x1, blocking collectives, local(): lax.all_to_all(out_src, 'head', split_axis=1, concat_axis=0, tiled=True)  14.8 us
    all_to_all x1, waiting for transfers between devices, local(): kv = lax.all_to_all(kv_src, 'head', split_axis=1, concat_axis=3, tiled=True)  10.3 us
    ppermute x4, local copies, waits for them, and re-layouts, shifted(): return lax.ppermute(block, axis, route)  8.21 us
    all_to_all x1, starting transfers between devices, local(): kv = lax.all_to_all(kv_src, 'head', split_axis=1, concat_axis=3, tiled=True)  4.3 us
    all_to_all x1, starting transfers between devices, local(): q_h = lax.all_to_all(q_rot, 'head', split_axis=0, concat_axis=2, tiled=True)  4.14 us
    unnamed x13, local copies, waits for them, and re-layouts  3.79 us
  transfers between devices with their start and end apart: 6, of which 1 were waited for; matrix products, arithmetic and copies ran while one was open for 13% of the time, Pallas kernels for 17%

profile of v2, /device:TPU:296, one launch (start us, length us, event | category | flops | bytes accessed | tf_op | source)
XLA Modules:
  0.0 183.9 jit_solution(2987988260241769606)
XLA Ops:
  0.0 0.7 convert_element_type.73
  0.8 1.3 copy.42
  3.1 1.0 copy.45
  4.7 0.7 copy-done.1
  5.5 1.1 copy.46
  6.5 4.3 %all-to-all-start.1 = ((bf16[2,8,4,128,64]{3,4,2,0,1:T(8,128)(2,1)}), bf16[2,8,4,128,64]{3,4,2,0,1:T(8,128)(2,1)S(1)}, u32[]{:S(2)}, u32[]{:S(2)}) async-start(bf16[2,8,4,128,64]{3,4,2,0,1:T(8,128)(2,1)} %copy.46), calls=%async_computation.1 | async-start | bytes 2097152 | tf_op jit(solution)/shard_map/all_to_all | solution.py:199
  12.5 0.6 gather_fusion.1
  13.7 0.6 gather_fusion
  14.9 0.6 pad_add_fusion
  15.6 0.9 fusion.1
  16.5 10.3 %all-to-all-done.1 = bf16[2,8,4,128,64]{3,4,2,0,1:T(8,128)(2,1)S(1)} async-done(((bf16[2,8,4,128,64]{3,4,2,0,1:T(8,128)(2,1)}), bf16[2,8,4,128,64]{3,4,2,0,1:T(8,128)(2,1)S(1)}, u32[]{:S(2)}, u32[]{:S(2)}) %all-to-all-start.1) | async-done | bytes 1048608 | tf_op jit(solution)/shard_map/all_to_all | solution.py:199
  26.8 4.1 %all-to-all-start = ((bf16[8,4,128,64]{2,3,1,0:T(8,128)(2,1)}), bf16[8,4,128,64]{2,3,1,0:T(8,128)(2,1)}, u32[]{:S(2)}, u32[]{:S(2)}) async-start(bf16[8,4,128,64]{2,3,1,0:T(8,128)(2,1)} %fusion.1), calls=%async_computation | async-start | bytes 1048576 | tf_op jit(solution)/shard_map/all_to_all | solution.py:201
  30.9 1.1 copy.47
  32.0 1.7 copy.49
  33.7 3.4 %collective-permute-start.1 = (bf16[2,4,1024,64]{2,3,1,0:T(8,128)(2,1)}, bf16[2,4,1024,64]{2,3,1,0:T(8,128)(2,1)}, u32[]{:S(2)}, u32[]{:S(2)}) collective-permute-start(bf16[2,4,1024,64]{2,3,1,0:T(8,128)(2,1)} %copy.49), channel_id=1, source_target_pairs={{0,32},{32,64},{64,96},{96,128},{128,160},{160,192},{192,224},{224... | collective-permute-start | bytes 3145736 | tf_op jit(solution)/shard_map/ppermute | solution.py:21
  37.1 3.7 %collective-permute-start.2 = (bf16[2,4,1024,64]{2,3,1,0:T(8,128)(2,1)}, bf16[2,4,1024,64]{2,3,1,0:T(8,128)(2,1)}, u32[]{:S(2)}, u32[]{:S(2)}) collective-permute-start(bf16[2,4,1024,64]{2,3,1,0:T(8,128)(2,1)} %copy.49), channel_id=1, source_target_pairs={{32,0},{64,32},{96,64},{128,96},{160,128},{192,160},{224,192},{256... | collective-permute-start | bytes 3145736 | tf_op jit(solution)/shard_map/ppermute | solution.py:21
  41.4 1.1 fusion.13
  42.5 1.5 copy.48
  44.1 3.1 %collective-permute-start = (bf16[2,4,512,64]{2,3,1,0:T(8,128)(2,1)S(1)}, bf16[2,4,512,64]{2,3,1,0:T(8,128)(2,1)S(1)}, u32[]{:S(2)}, u32[]{:S(2)}) collective-permute-start(bf16[2,4,512,64]{2,3,1,0:T(8,128)(2,1)S(1)} %copy.48), channel_id=1, source_target_pairs={{0,64},{32,96},{64,128},{96,160},{128,192},{160,224},{192,256},{22... | collective-permute-start | bytes 1572872 | tf_op jit(solution)/shard_map/ppermute | solution.py:21
  47.5 4.9 %collective-permute-start.3 = (bf16[2,4,512,64]{2,3,1,0:T(8,128)(2,1)S(1)}, bf16[2,4,512,64]{2,3,1,0:T(8,128)(2,1)S(1)}, u32[]{:S(2)}, u32[]{:S(2)}) collective-permute-start(bf16[2,4,512,64]{2,3,1,0:T(8,128)(2,1)S(1)} %copy.51), channel_id=1, source_target_pairs={{64,0},{96,32},{128,64},{160,96},{192,128},{224,160},{256,192},{28... | collective-permute-start | bytes 1572872 | tf_op jit(solution)/shard_map/ppermute | solution.py:21
  53.6 1.0 copy.53.qs_ref
  55.2 0.6 and_select_fusion.1
  55.8 2.4 %copy.43 = bf16[1,4,8,128,64]{4,3,2,1,0:T(8,128)(2,1)} copy(bf16[1,4,8,128,64]{3,4,1,2,0:T(8,128)(2,1)} %bitcast.10) | data formatting | bytes 1048576 | tf_op jit(solution)/shard_map/all_to_all | solution.py:201
  58.2 31.9 %shard_map.55 = (f32[4,1024,1]{2,1,0:T(8,128)}, f32[4,1024,1]{2,1,0:T(8,128)}, f32[4,1024,64]{2,1,0:T(8,128)}) custom-call(s32[4]{0:T(128)} %get-tuple-element.18.lo_ref, s32[4]{0:T(128)} %get-tuple-element.17.hi_ref, s32[16]{0:T(128)} %reshape.462.full_ref, bf16[1,4,1024,64]{3,2,1,0:T(8,128)(2,1)} %bitcast.54, s32[1024,1]{1,0:T(8,128)} %copy.53.qs_ref, ...), custom_call_target="tpu_custom_call" | custom-call | tf_op jit(solution)/shard_map/pallas_call | solution.py:164
  90.1 1.4 copy.54.rest_0_.rest_1_
  91.4 1.3 copy.60.rest_9_.rest_10_
  92.8 2.8 %copy.56.rest_3_.rest_4_ = bf16[2,4,1024,64]{3,2,1,0:T(8,128)(2,1)} copy(bf16[2,4,1024,64]{2,3,1,0:T(8,128)(2,1)} %collective-permute-done.1) | data formatting | bytes 2097152 | tf_op jit(solution)/shard_map/ppermute | solution.py:21
  95.5 2.8 %copy.58.rest_6_.rest_7_ = bf16[2,4,1024,64]{3,2,1,0:T(8,128)(2,1)} copy(bf16[2,4,1024,64]{2,3,1,0:T(8,128)(2,1)} %collective-permute-done.2) | data formatting | bytes 2097152 | tf_op jit(solution)/shard_map/ppermute | solution.py:21
  98.3 68.1 %shard_map.56 = bf16[1,4,1024,64]{3,2,1,0:T(8,128)(2,1)} custom-call(s32[16]{0:T(128)} %get-tuple-element.55.lo_ref, s32[16]{0:T(128)} %get-tuple-element.56.hi_ref, s32[64]{0:T(128)} %add_convert_fusion.1.full_ref, bf16[1,4,1024,64]{3,2,1,0:T(8,128)(2,1)} %bitcast.55, s32[1024,1]{1,0:T(8,128)} %copy.53.qs_ref, ...), custom_call_target="tpu_custom_call" | custom-call | tf_op jit(solution)/shard_map/pallas_call | solution.py:164
  166.4 1.6 copy.62
  168.0 14.8 %all_to_all.48 = bf16[4,8,128,64]{2,3,0,1:T(8,128)(2,1)S(1)} all-to-all(bf16[4,8,128,64]{2,3,0,1:T(8,128)(2,1)S(1)} %copy.62), channel_id=1, replica_groups=mesh['seq'=16,'head'=8,'dp'=4] {'head'}, dimensions={1} | all-to-all | bytes 1048576 | tf_op jit(solution)/shard_map/all_to_all | solution.py:261
  182.9 1.0 copy.63
  (70 shorter events, 7.1 us)
Async XLA Ops:
  0.0 2.2 %copy-start.2 = (bf16[128,2048]{1,0:T(8,128)(2,1)S(1)}, bf16[128,2048]{1,0:T(8,128)(2,1)}, u32[]{:S(2)}) copy-start(bf16[128,2048]{1,0:T(8,128)(2,1)} %param.8) | copy-start | bytes 1572868
  2.1 1.0 copy-start.3
  4.3 1.0 copy-start.1
  5.4 5.4 %copy-start.4 = (s32[32]{0:T(128)S(1)}, s32[32]{0:T(128)}, u32[]{:S(2)}) copy-start(s32[32]{0:T(128)} %param.11) | copy-start | bytes 388
  6.5 20.2 %all-to-all-start.1 = ((bf16[2,8,4,128,64]{3,4,2,0,1:T(8,128)(2,1)}), bf16[2,8,4,128,64]{3,4,2,0,1:T(8,128)(2,1)S(1)}, u32[]{:S(2)}, u32[]{:S(2)}) async-start(bf16[2,8,4,128,64]{3,4,2,0,1:T(8,128)(2,1)} %copy.46), calls=%async_computation.1 | async-start | bytes 2097152 | tf_op jit(solution)/shard_map/all_to_all | solution.py:199
  26.8 29.0 %all-to-all-start = ((bf16[8,4,128,64]{2,3,1,0:T(8,128)(2,1)}), bf16[8,4,128,64]{2,3,1,0:T(8,128)(2,1)}, u32[]{:S(2)}, u32[]{:S(2)}) async-start(bf16[8,4,128,64]{2,3,1,0:T(8,128)(2,1)} %fusion.1), calls=%async_computation | async-start | bytes 1048576 | tf_op jit(solution)/shard_map/all_to_all | solution.py:201
  32.0 10.5 %copy-start = (bf16[2,1,4,8,128,64]{5,4,3,2,0,1:T(8,128)(2,1)}, bf16[2,1,4,8,128,64]{5,4,3,2,0,1:T(8,128)(2,1)S(1)}, u32[]{:S(2)}) copy-start(bf16[2,1,4,8,128,64]{5,4,3,2,0,1:T(8,128)(2,1)S(1)} %copy.47) | copy-start | bytes 3145732
  33.7 59.1 %collective-permute-start.1 = (bf16[2,4,1024,64]{2,3,1,0:T(8,128)(2,1)}, bf16[2,4,1024,64]{2,3,1,0:T(8,128)(2,1)}, u32[]{:S(2)}, u32[]{:S(2)}) collective-permute-start(bf16[2,4,1024,64]{2,3,1,0:T(8,128)(2,1)} %copy.49), channel_id=1, source_target_pairs={{0,32},{32,64},{64,96},{96,128},{128,160},{160,192},{192,224},{224... | collective-permute-start | bytes 3145736 | tf_op jit(solution)/shard_map/ppermute | solution.py:21
  37.1 58.5 %collective-permute-start.2 = (bf16[2,4,1024,64]{2,3,1,0:T(8,128)(2,1)}, bf16[2,4,1024,64]{2,3,1,0:T(8,128)(2,1)}, u32[]{:S(2)}, u32[]{:S(2)}) collective-permute-start(bf16[2,4,1024,64]{2,3,1,0:T(8,128)(2,1)} %copy.49), channel_id=1, source_target_pairs={{32,0},{64,32},{96,64},{128,96},{160,128},{192,160},{224,192},{256... | collective-permute-start | bytes 3145736 | tf_op jit(solution)/shard_map/ppermute | solution.py:21
  44.1 46.0 %collective-permute-start = (bf16[2,4,512,64]{2,3,1,0:T(8,128)(2,1)S(1)}, bf16[2,4,512,64]{2,3,1,0:T(8,128)(2,1)S(1)}, u32[]{:S(2)}, u32[]{:S(2)}) collective-permute-start(bf16[2,4,512,64]{2,3,1,0:T(8,128)(2,1)S(1)} %copy.48), channel_id=1, source_target_pairs={{0,64},{32,96},{64,128},{96,160},{128,192},{160,224},{192,256},{22... | collective-permute-start | bytes 1572872 | tf_op jit(solution)/shard_map/ppermute | solution.py:21
  47.5 44.0 %collective-permute-start.3 = (bf16[2,4,512,64]{2,3,1,0:T(8,128)(2,1)S(1)}, bf16[2,4,512,64]{2,3,1,0:T(8,128)(2,1)S(1)}, u32[]{:S(2)}, u32[]{:S(2)}) collective-permute-start(bf16[2,4,512,64]{2,3,1,0:T(8,128)(2,1)S(1)} %copy.51), channel_id=1, source_target_pairs={{64,0},{96,32},{128,64},{160,96},{192,128},{224,160},{256,192},{28... | collective-permute-start | bytes 1572872 | tf_op jit(solution)/shard_map/ppermute | solution.py:21

commit v3 on v2

--- a/solution.py
+++ b/solution.py
@@ -56,66 +56,58 @@
     return jnp.sum((positions[:, None] >= scene_end[None, :]).astype(jnp.int32), axis=1)
 
 
+LANES = 128
+
+
 def make_kernel(piece_rows, nq, has_state, finalize):
     n_pieces = len(piece_rows)
-    ktmax = max(piece_rows) // TK
-
-    def kernel(lo_ref, hi_ref, full_ref, q_ref, qs_ref, *rest):
-        piece_refs = rest[: 3 * n_pieces]
-        rest = rest[3 * n_pieces :]
+
+    def kernel(lo_ref, hi_ref, q_ref, qs_ref, *rest):
+        piece_refs = rest[: 2 * n_pieces]
+        rest = rest[2 * n_pieces :]
         if has_state:
             m_in, l_in, acc_in = rest[:3]
             rest = rest[3:]
         outs = rest
         i = pl.program_id(1)
         q = q_ref[0, 0]
-        qs = qs_ref[...]
+        qs = jnp.tile(qs_ref[...], (1, TK // LANES))
         tq = q.shape[0]
         if has_state:
             carry = (m_in[0], l_in[0], acc_in[0])
         else:
             carry = (
-                jnp.full((tq, 1), neg_big, jnp.float32),
-                jnp.zeros((tq, 1), jnp.float32),
+                jnp.full((tq, LANES), neg_big, jnp.float32),
+                jnp.zeros((tq, LANES), jnp.float32),
                 jnp.zeros((tq, HD), jnp.float32),
             )
         for p in range(n_pieces):
-            k_ref, v_ref, ks_ref = piece_refs[3 * p : 3 * p + 3]
+            kv_ref, ks_ref = piece_refs[2 * p : 2 * p + 2]
             base = p * nq + i
 
-            def update(start, carry, masked, k_ref=k_ref, v_ref=v_ref, ks_ref=ks_ref):
+            def body(j, carry, kv_ref=kv_ref, ks_ref=ks_ref):
                 m, l, acc = carry
-                k = k_ref[0, 0, pl.ds(start, TK), :]
-                v = v_ref[0, 0, pl.ds(start, TK), :]
+                start = pl.multiple_of(j * TK, TK)
+                k = kv_ref[0, 0, pl.ds(start, TK), :]
+                v = kv_ref[1, 0, pl.ds(start, TK), :]
+                ks = ks_ref[:, pl.ds(start, TK)]
                 s = lax.dot_general(
                     q, k, (((1,), (1,)), ((), ())), preferred_element_type=jnp.float32
                 )
-                if masked:
-                    ks = ks_ref[:, pl.ds(start, TK)]
-                    s = jnp.where(qs == ks, s, neg_big)
-                m_new = jnp.maximum(m, jnp.max(s, axis=1, keepdims=True))
-                p_w = jnp.exp(s - m_new)
+                s = jnp.where(qs == ks, s, neg_big)
+                m_new = jnp.maximum(m, jnp.max(s, axis=1)[:, None])
+                p_w = jnp.exp(s - jnp.tile(m_new, (1, TK // LANES)))
                 alpha = jnp.exp(m - m_new)
-                l = l * alpha + jnp.sum(p_w, axis=1, keepdims=True)
-                acc = acc * alpha + jnp.dot(
+                l = alpha * l + jnp.sum(p_w, axis=1)[:, None]
+                acc = acc * alpha[:, :HD] + jnp.dot(
                     p_w.astype(jnp.bfloat16), v, preferred_element_type=jnp.float32
                 )
                 return m_new, l, acc
 
-            def body(j, carry, base=base, update=update):
-                start = pl.multiple_of(j * TK, TK)
-                full = full_ref[base * ktmax + j]
-                return lax.cond(
-                    full != 0,
-                    lambda c: update(start, c, False),
-                    lambda c: update(start, c, True),
-                    carry,
-                )
-
             carry = lax.fori_loop(lo_ref[base], hi_ref[base], body, carry)
         m, l, acc = carry
         if finalize:
-            outs[0][0, 0] = (acc / l).astype(outs[0].dtype)
+            outs[0][0, 0] = (acc / l[:, :HD]).astype(outs[0].dtype)
         else:
             outs[0][0] = m
             outs[1][0] = l
@@ -124,8 +116,8 @@
     return kernel
 
 
-def attend(q_h, q_scene, pieces, lo, hi, full, state):
-    heads, qlen, _ = q_h.shape[1:] if q_h.ndim == 4 else q_h.shape
+def attend(q_h, q_scene, pieces, lo, hi, state):
+    heads, qlen, _ = q_h.shape[1:]
     nq = qlen // TQ
     piece_rows = [kv.shape[2] for kv, _ in pieces]
     has_state = state is not None
@@ -133,23 +125,22 @@
     kernel = make_kernel(piece_rows, nq, has_state, finalize)
     in_specs = [
         pl.BlockSpec((1, 1, TQ, HD), lambda h, i, *_: (0, h, i, 0)),
-        pl.BlockSpec((TQ, 1), lambda h, i, *_: (i, 0)),
+        pl.BlockSpec((TQ, LANES), lambda h, i, *_: (i, 0)),
     ]
     args = [q_h, q_scene]
     for kv, ks in pieces:
         rows = kv.shape[2]
-        in_specs.append(pl.BlockSpec((1, 1, rows, HD), lambda h, i, *_: (0, h, 0, 0)))
-        in_specs.append(pl.BlockSpec((1, 1, rows, HD), lambda h, i, *_: (1, h, 0, 0)))
+        in_specs.append(pl.BlockSpec((2, 1, rows, HD), lambda h, i, *_: (0, h, 0, 0)))
         in_specs.append(pl.BlockSpec((1, rows), lambda h, i, *_: (0, 0)))
-        args += [kv, kv, ks]
+        args += [kv, ks]
     state_specs = [
-        pl.BlockSpec((1, TQ, 1), lambda h, i, *_: (h, i, 0)),
-        pl.BlockSpec((1, TQ, 1), lambda h, i, *_: (h, i, 0)),
+        pl.BlockSpec((1, TQ, LANES), lambda h, i, *_: (h, i, 0)),
+        pl.BlockSpec((1, TQ, LANES), lambda h, i, *_: (h, i, 0)),
         pl.BlockSpec((1, TQ, HD), lambda h, i, *_: (h, i, 0)),
     ]
     state_shapes = [
-        jax.ShapeDtypeStruct((heads, qlen, 1), jnp.float32),
-        jax.ShapeDtypeStruct((heads, qlen, 1), jnp.float32),
+        jax.ShapeDtypeStruct((heads, qlen, LANES), jnp.float32),
+        jax.ShapeDtypeStruct((heads, qlen, LANES), jnp.float32),
         jax.ShapeDtypeStruct((heads, qlen, HD), jnp.float32),
     ]
     if has_state:
@@ -165,7 +156,7 @@
         kernel,
         out_shape=out_shape,
         grid_spec=pltpu.PrefetchScalarGridSpec(
-            num_scalar_prefetch=3,
+            num_scalar_prefetch=2,
             grid=(heads, nq),
             in_specs=in_specs,
             out_specs=out_specs,
@@ -173,7 +164,7 @@
         compiler_params=pltpu.CompilerParams(
             dimension_semantics=("arbitrary", "arbitrary")
         ),
-    )(lo, hi, full, *args)
+    )(lo, hi, *args)
 
 
 def local(queries, keys, values, coords, lengths):
@@ -217,11 +208,9 @@
     last_scene = q_scene[TQ - 1 :: TQ]
     span_lo = jnp.take(scene_begin, first_scene)
     span_hi = jnp.take(scene_end, last_scene)
-    q_single = first_scene == last_scene
 
     def tables(piece_list):
-        ktmax = max(kvp.shape[2] for kvp, _ in piece_list) // TK
-        los, his, fulls, prepared = [], [], [], []
+        los, his, prepared = [], [], []
         for kvp, offset in piece_list:
             rows = kvp.shape[2]
             p0 = own_start + offset
@@ -234,28 +223,18 @@
             khi = jnp.maximum((hi + TK - 1) // TK, klo)
             los.append(klo)
             his.append(khi)
-            kt_first = k_scene[::TK]
-            kt_last = k_scene[TK - 1 :: TK]
-            kfull = (
-                q_single[:, None]
-                & (kt_first[None, :] == first_scene[:, None])
-                & (kt_last[None, :] == first_scene[:, None])
-            )
-            kfull = jnp.pad(kfull, ((0, 0), (0, ktmax - kfull.shape[1])))
-            fulls.append(kfull.reshape(-1))
             prepared.append((kvp, k_scene.reshape(1, rows)))
         return (
             jnp.concatenate(los).astype(jnp.int32),
             jnp.concatenate(his).astype(jnp.int32),
-            jnp.concatenate(fulls).astype(jnp.int32),
             prepared,
         )
 
-    q_scene_col = q_scene.reshape(group_len, 1).astype(jnp.int32)
-    lo0, hi0, full0, prep0 = tables([(kv, 0)])
-    state = attend(q_h, q_scene_col, prep0, lo0, hi0, full0, None)
-    lo1, hi1, full1, prep1 = tables(halo)
-    out_h = attend(q_h, q_scene_col, prep1, lo1, hi1, full1, state)[0]
+    q_scene_col = jnp.broadcast_to(q_scene.astype(jnp.int32)[:, None], (group_len, LANES))
+    lo0, hi0, prep0 = tables([(kv, 0)])
+    state = attend(q_h, q_scene_col, prep0, lo0, hi0, None)
+    lo1, hi1, prep1 = tables(halo)
+    out_h = attend(q_h, q_scene_col, prep1, lo1, hi1, state)[0]
 
     out_src = out_h.reshape(local_heads, head_count, tok_dev, HD)
     back = lax.all_to_all(out_src, "head", split_axis=1, concat_axis=0, tiled=True)

time: 185 us -> 159 us (0.86)
  the two profiles are of different devices: /device:TPU:296 before, /device:TPU:160 now
where the time goes in v3:
time: 159 us; the launch traced here: 158 us
  Pallas kernels  73.6 us (46%)
  local copies, waits for them, and re-layouts  26.3 us (17%)
  starting transfers between devices  24.7 us (16%)
  blocking collectives  14.8 us (9%)
  waiting for transfers between devices  10.5 us (7%)
  other arithmetic  7.88 us (5%)
    pallas_call x2, Pallas kernels, attend(): pl.pallas_call(kernel, out_shape=out_shape, grid_spec=pltpu.PrefetchScala...  73.6 us
    ppermute x4, starting transfers between devices, shifted(): return lax.ppermute(block, axis, route)  16.3 us
    all_to_all x1, blocking collectives, local(): lax.all_to_all(out_src, 'head', split_axis=1, concat_axis=0, tiled=True)  14.8 us
    all_to_all x1, waiting for transfers between devices, local(): kv = lax.all_to_all(kv_src, 'head', split_axis=1, concat_axis=3, tiled=True)  10.5 us
    ppermute x4, local copies, waits for them, and re-layouts, shifted(): return lax.ppermute(block, axis, route)  8.17 us
    all_to_all x1, starting transfers between devices, local(): kv = lax.all_to_all(kv_src, 'head', split_axis=1, concat_axis=3, tiled=True)  4.3 us
    all_to_all x1, starting transfers between devices, local(): q_h = lax.all_to_all(q_rot, 'head', split_axis=0, concat_axis=2, tiled=True)  4.14 us
    unnamed x13, local copies, waits for them, and re-layouts  3.79 us
  transfers between devices with their start and end apart: 6, of which 1 were waited for; matrix products, arithmetic and copies ran while one was open for 14% of the time, Pallas kernels for 21%

profile of v3, /device:TPU:160, one launch (start us, length us, event | category | flops | bytes accessed | tf_op | source)
XLA Modules:
  0.0 158.0 jit_solution(4588529552004577265)
XLA Ops:
  0.0 0.7 convert_element_type.57
  0.8 1.3 copy.34
  3.1 1.0 copy.37
  4.7 0.7 copy-done.1
  5.5 1.1 copy.38
  6.5 4.3 %all-to-all-start.1 = ((bf16[2,8,4,128,64]{3,4,2,0,1:T(8,128)(2,1)}), bf16[2,8,4,128,64]{3,4,2,0,1:T(8,128)(2,1)S(1)}, u32[]{:S(2)}, u32[]{:S(2)}) async-start(bf16[2,8,4,128,64]{3,4,2,0,1:T(8,128)(2,1)} %copy.38), calls=%async_computation.1 | async-start | bytes 2097152 | tf_op jit(solution)/shard_map/all_to_all | solution.py:190
  11.5 0.6 gather_fusion.1
  12.1 0.6 gather_fusion
  13.4 0.7 pad_add_fusion.1.hi_ref
  14.2 0.9 fusion.1
  16.3 10.5 %all-to-all-done.1 = bf16[2,8,4,128,64]{3,4,2,0,1:T(8,128)(2,1)S(1)} async-done(((bf16[2,8,4,128,64]{3,4,2,0,1:T(8,128)(2,1)}), bf16[2,8,4,128,64]{3,4,2,0,1:T(8,128)(2,1)S(1)}, u32[]{:S(2)}, u32[]{:S(2)}) %all-to-all-start.1) | async-done | bytes 1048608 | tf_op jit(solution)/shard_map/all_to_all | solution.py:190
  26.8 4.1 %all-to-all-start = ((bf16[8,4,128,64]{2,3,1,0:T(8,128)(2,1)}), bf16[8,4,128,64]{2,3,1,0:T(8,128)(2,1)}, u32[]{:S(2)}, u32[]{:S(2)}) async-start(bf16[8,4,128,64]{2,3,1,0:T(8,128)(2,1)} %fusion.1), calls=%async_computation | async-start | bytes 1048576 | tf_op jit(solution)/shard_map/all_to_all | solution.py:192
  30.9 1.1 copy.39
  32.0 1.7 %copy.41 = bf16[2,4,1024,64]{2,3,1,0:T(8,128)(2,1)} copy(bf16[2,4,1024,64]{3,2,1,0:T(8,128)(2,1)S(1)} %bitcast.49) | data formatting | bytes 2097152 | tf_op jit(solution)/shard_map/reshape | solution.py:191
  33.7 4.3 %collective-permute-start.1 = (bf16[2,4,1024,64]{2,3,1,0:T(8,128)(2,1)}, bf16[2,4,1024,64]{2,3,1,0:T(8,128)(2,1)}, u32[]{:S(2)}, u32[]{:S(2)}) collective-permute-start(bf16[2,4,1024,64]{2,3,1,0:T(8,128)(2,1)} %copy.41), channel_id=1, source_target_pairs={{0,32},{32,64},{64,96},{96,128},{128,160},{160,192},{192,224},{224... | collective-permute-start | bytes 3145736 | tf_op jit(solution)/shard_map/ppermute | solution.py:21
  38.0 1.9 %collective-permute-start.2 = (bf16[2,4,1024,64]{2,3,1,0:T(8,128)(2,1)}, bf16[2,4,1024,64]{2,3,1,0:T(8,128)(2,1)}, u32[]{:S(2)}, u32[]{:S(2)}) collective-permute-start(bf16[2,4,1024,64]{2,3,1,0:T(8,128)(2,1)} %copy.41), channel_id=1, source_target_pairs={{32,0},{64,32},{96,64},{128,96},{160,128},{192,160},{224,192},{256... | collective-permute-start | bytes 3145736 | tf_op jit(solution)/shard_map/ppermute | solution.py:21
  40.5 1.1 fusion.13
  41.6 1.5 copy.40
  43.2 8.2 %collective-permute-start = (bf16[2,4,512,64]{2,3,1,0:T(8,128)(2,1)S(1)}, bf16[2,4,512,64]{2,3,1,0:T(8,128)(2,1)S(1)}, u32[]{:S(2)}, u32[]{:S(2)}) collective-permute-start(bf16[2,4,512,64]{2,3,1,0:T(8,128)(2,1)S(1)} %copy.40), channel_id=1, source_target_pairs={{0,64},{32,96},{64,128},{96,160},{128,192},{160,224},{192,256},{22... | collective-permute-start | bytes 1572872 | tf_op jit(solution)/shard_map/ppermute | solution.py:21
  51.6 1.9 %collective-permute-start.3 = (bf16[2,4,512,64]{2,3,1,0:T(8,128)(2,1)S(1)}, bf16[2,4,512,64]{2,3,1,0:T(8,128)(2,1)S(1)}, u32[]{:S(2)}, u32[]{:S(2)}) collective-permute-start(bf16[2,4,512,64]{2,3,1,0:T(8,128)(2,1)S(1)} %copy.43), channel_id=1, source_target_pairs={{64,0},{96,32},{128,64},{160,96},{192,128},{224,160},{256,192},{28... | collective-permute-start | bytes 1572872 | tf_op jit(solution)/shard_map/ppermute | solution.py:21
  53.6 0.7 pad_add_fusion.lo_ref
  55.4 2.4 %copy.35 = bf16[1,4,8,128,64]{4,3,2,1,0:T(8,128)(2,1)} copy(bf16[1,4,8,128,64]{3,4,1,2,0:T(8,128)(2,1)} %bitcast.10) | data formatting | bytes 1048576 | tf_op jit(solution)/shard_map/all_to_all | solution.py:192
  57.8 1.0 broadcast_in_dim.22.qs_ref
  58.8 33.5 %shard_map.55 = (f32[4,1024,128]{2,1,0:T(8,128)}, f32[4,1024,128]{2,1,0:T(8,128)}, f32[4,1024,64]{2,1,0:T(8,128)}) custom-call(s32[4]{0:T(128)} %get-tuple-element.18.lo_ref, s32[4]{0:T(128)} %get-tuple-element.17.hi_ref, bf16[1,4,1024,64]{3,2,1,0:T(8,128)(2,1)} %bitcast.52, s32[1024,128]{1,0:T(8,128)} %broadcast_in_dim.22.qs_ref, ...), custom_call_target="tpu_custom_call" | custom-call | tf_op jit(solution)/shard_map/pallas_call | solution.py:155
  92.3 1.4 copy.44.rest_0_
  93.7 1.3 copy.47.rest_6_
  95.0 2.7 %copy.45.rest_2_ = bf16[2,4,1024,64]{3,2,1,0:T(8,128)(2,1)} copy(bf16[2,4,1024,64]{2,3,1,0:T(8,128)(2,1)} %collective-permute-done.1) | data formatting | bytes 2097152 | tf_op jit(solution)/shard_map/ppermute | solution.py:21
  97.7 2.7 %copy.46.rest_4_ = bf16[2,4,1024,64]{3,2,1,0:T(8,128)(2,1)} copy(bf16[2,4,1024,64]{2,3,1,0:T(8,128)(2,1)} %collective-permute-done.2) | data formatting | bytes 2097152 | tf_op jit(solution)/shard_map/ppermute | solution.py:21
  100.5 40.1 %shard_map.56 = bf16[1,4,1024,64]{3,2,1,0:T(8,128)(2,1)} custom-call(s32[16]{0:T(128)} %pad_add_fusion.lo_ref, s32[16]{0:T(128)} %pad_add_fusion.1.hi_ref, bf16[1,4,1024,64]{3,2,1,0:T(8,128)(2,1)} %bitcast.53, s32[1024,128]{1,0:T(8,128)} %broadcast_in_dim.22.qs_ref, bf16[2,4,512,64]{3,2,1,0:T(8,128)(2,1)} %copy.44.rest_0_, ...), custom_call_target="tpu_custom_call" | custom-call | tf_op jit(solution)/shard_map/pallas_call | solution.py:155
  140.6 1.6 %copy.48 = bf16[4,8,128,64]{2,3,0,1:T(8,128)(2,1)S(1)} copy(bf16[4,8,128,64]{3,2,1,0:T(8,128)(2,1)} %bitcast.55) | data formatting | bytes 1048576 | tf_op jit(solution)/shard_map/reshape | solution.py:239
  142.2 14.8 %all_to_all.48 = bf16[4,8,128,64]{2,3,0,1:T(8,128)(2,1)S(1)} all-to-all(bf16[4,8,128,64]{2,3,0,1:T(8,128)(2,1)S(1)} %copy.48), channel_id=1, replica_groups=mesh['seq'=16,'head'=8,'dp'=4] {'head'}, dimensions={1} | all-to-all | bytes 1048576 | tf_op jit(solution)/shard_map/all_to_all | solution.py:240
  157.0 1.0 copy.49
  (47 shorter events, 6.3 us)
Async XLA Ops:
  0.0 2.2 %copy-start.2 = (bf16[128,2048]{1,0:T(8,128)(2,1)S(1)}, bf16[128,2048]{1,0:T(8,128)(2,1)}, u32[]{:S(2)}) copy-start(bf16[128,2048]{1,0:T(8,128)(2,1)} %param.8) | copy-start | bytes 1572868
  2.1 1.0 copy-start.3
  4.3 1.0 copy-start.1
  5.4 5.4 %copy-start.4 = (s32[32]{0:T(128)S(1)}, s32[32]{0:T(128)}, u32[]{:S(2)}) copy-start(s32[32]{0:T(128)} %param.11) | copy-start | bytes 388
  6.5 20.2 %all-to-all-start.1 = ((bf16[2,8,4,128,64]{3,4,2,0,1:T(8,128)(2,1)}), bf16[2,8,4,128,64]{3,4,2,0,1:T(8,128)(2,1)S(1)}, u32[]{:S(2)}, u32[]{:S(2)}) async-start(bf16[2,8,4,128,64]{3,4,2,0,1:T(8,128)(2,1)} %copy.38), calls=%async_computation.1 | async-start | bytes 2097152 | tf_op jit(solution)/shard_map/all_to_all | solution.py:190
  26.8 28.7 %all-to-all-start = ((bf16[8,4,128,64]{2,3,1,0:T(8,128)(2,1)}), bf16[8,4,128,64]{2,3,1,0:T(8,128)(2,1)}, u32[]{:S(2)}, u32[]{:S(2)}) async-start(bf16[8,4,128,64]{2,3,1,0:T(8,128)(2,1)} %fusion.1), calls=%async_computation | async-start | bytes 1048576 | tf_op jit(solution)/shard_map/all_to_all | solution.py:192
  32.0 9.6 %copy-start = (bf16[2,1,4,8,128,64]{5,4,3,2,0,1:T(8,128)(2,1)}, bf16[2,1,4,8,128,64]{5,4,3,2,0,1:T(8,128)(2,1)S(1)}, u32[]{:S(2)}) copy-start(bf16[2,1,4,8,128,64]{5,4,3,2,0,1:T(8,128)(2,1)S(1)} %copy.39) | copy-start | bytes 3145732
  33.7 61.3 %collective-permute-start.1 = (bf16[2,4,1024,64]{2,3,1,0:T(8,128)(2,1)}, bf16[2,4,1024,64]{2,3,1,0:T(8,128)(2,1)}, u32[]{:S(2)}, u32[]{:S(2)}) collective-permute-start(bf16[2,4,1024,64]{2,3,1,0:T(8,128)(2,1)} %copy.41), channel_id=1, source_target_pairs={{0,32},{32,64},{64,96},{96,128},{128,160},{160,192},{192,224},{224... | collective-permute-start | bytes 3145736 | tf_op jit(solution)/shard_map/ppermute | solution.py:21
  38.0 59.8 %collective-permute-start.2 = (bf16[2,4,1024,64]{2,3,1,0:T(8,128)(2,1)}, bf16[2,4,1024,64]{2,3,1,0:T(8,128)(2,1)}, u32[]{:S(2)}, u32[]{:S(2)}) collective-permute-start(bf16[2,4,1024,64]{2,3,1,0:T(8,128)(2,1)} %copy.41), channel_id=1, source_target_pairs={{32,0},{64,32},{96,64},{128,96},{160,128},{192,160},{224,192},{256... | collective-permute-start | bytes 3145736 | tf_op jit(solution)/shard_map/ppermute | solution.py:21
  43.2 49.1 %collective-permute-start = (bf16[2,4,512,64]{2,3,1,0:T(8,128)(2,1)S(1)}, bf16[2,4,512,64]{2,3,1,0:T(8,128)(2,1)S(1)}, u32[]{:S(2)}, u32[]{:S(2)}) collective-permute-start(bf16[2,4,512,64]{2,3,1,0:T(8,128)(2,1)S(1)} %copy.40), channel_id=1, source_target_pairs={{0,64},{32,96},{64,128},{96,160},{128,192},{160,224},{192,256},{22... | collective-permute-start | bytes 1572872 | tf_op jit(solution)/shard_map/ppermute | solution.py:21
  51.6 42.0 %collective-permute-start.3 = (bf16[2,4,512,64]{2,3,1,0:T(8,128)(2,1)S(1)}, bf16[2,4,512,64]{2,3,1,0:T(8,128)(2,1)S(1)}, u32[]{:S(2)}, u32[]{:S(2)}) collective-permute-start(bf16[2,4,512,64]{2,3,1,0:T(8,128)(2,1)S(1)} %copy.43), channel_id=1, source_target_pairs={{64,0},{96,32},{128,64},{160,96},{192,128},{224,160},{256,192},{28... | collective-permute-start | bytes 1572872 | tf_op jit(solution)/shard_map/ppermute | solution.py:21

commit v4 on v3

--- a/solution.py
+++ b/solution.py
@@ -12,7 +12,7 @@
 neg_big = -1e30
 
 TQ = 256
-TK = 256
+TK = 512
 
 
 def shifted(block, axis, distance):
@@ -59,96 +59,102 @@
 LANES = 128
 
 
-def make_kernel(piece_rows, nq, has_state, finalize):
+def make_kernel(piece_rows, heads, nq, has_state, finalize):
     n_pieces = len(piece_rows)
 
     def kernel(lo_ref, hi_ref, q_ref, qs_ref, *rest):
         piece_refs = rest[: 2 * n_pieces]
         rest = rest[2 * n_pieces :]
         if has_state:
-            m_in, l_in, acc_in = rest[:3]
-            rest = rest[3:]
+            m_in, acc_in = rest[:2]
+            rest = rest[2:]
         outs = rest
-        i = pl.program_id(1)
-        q = q_ref[0, 0]
+        i = pl.program_id(0)
+        tq = q_ref.shape[1]
+        pad = jnp.zeros((tq, LANES - HD), jnp.bfloat16)
+        qx = [jnp.concatenate([q_ref[h], pad], axis=1) for h in range(heads)]
         qs = jnp.tile(qs_ref[...], (1, TK // LANES))
-        tq = q.shape[0]
+        ones = jnp.ones((TK, LANES), jnp.bfloat16)
+        two = 2 * LANES
         if has_state:
-            carry = (m_in[0], l_in[0], acc_in[0])
+            carry = tuple((m_in[h], acc_in[h]) for h in range(heads))
         else:
-            carry = (
-                jnp.full((tq, LANES), neg_big, jnp.float32),
-                jnp.zeros((tq, LANES), jnp.float32),
-                jnp.zeros((tq, HD), jnp.float32),
+            carry = tuple(
+                (
+                    jnp.full((tq, LANES), neg_big, jnp.float32),
+                    jnp.zeros((tq, two), jnp.float32),
+                )
+                for h in range(heads)
             )
         for p in range(n_pieces):
             kv_ref, ks_ref = piece_refs[2 * p : 2 * p + 2]
             base = p * nq + i
 
             def body(j, carry, kv_ref=kv_ref, ks_ref=ks_ref):
-                m, l, acc = carry
                 start = pl.multiple_of(j * TK, TK)
-                k = kv_ref[0, 0, pl.ds(start, TK), :]
-                v = kv_ref[1, 0, pl.ds(start, TK), :]
-                ks = ks_ref[:, pl.ds(start, TK)]
-                s = lax.dot_general(
-                    q, k, (((1,), (1,)), ((), ())), preferred_element_type=jnp.float32
-                )
-                s = jnp.where(qs == ks, s, neg_big)
-                m_new = jnp.maximum(m, jnp.max(s, axis=1)[:, None])
-                p_w = jnp.exp(s - jnp.tile(m_new, (1, TK // LANES)))
-                alpha = jnp.exp(m - m_new)
-                l = alpha * l + jnp.sum(p_w, axis=1)[:, None]
-                acc = acc * alpha[:, :HD] + jnp.dot(
-                    p_w.astype(jnp.bfloat16), v, preferred_element_type=jnp.float32
-                )
-                return m_new, l, acc
+                allowed = qs == ks_ref[:, pl.ds(start, TK)]
+                new = []
+                for h in range(heads):
+                    m, acc = carry[h]
+                    kvt = kv_ref[h, pl.ds(start, TK), :]
+                    s = lax.dot_general(
+                        qx[h], kvt, (((1,), (1,)), ((), ())), preferred_element_type=jnp.float32
+                    )
+                    s = jnp.where(allowed, s, neg_big)
+                    m_new = jnp.maximum(m, jnp.max(s, axis=1)[:, None])
+                    p_w = jnp.exp(s - jnp.tile(m_new, (1, TK // LANES)))
+                    alpha = jnp.exp(m - m_new)
+                    pb = p_w.astype(jnp.bfloat16)
+                    rhs = jnp.concatenate([kvt, ones], axis=1)
+                    acc = jnp.tile(alpha, (1, 2)) * acc + jnp.dot(
+                        pb, rhs, preferred_element_type=jnp.float32
+                    )
+                    new.append((m_new, acc))
+                return tuple(new)
 
             carry = lax.fori_loop(lo_ref[base], hi_ref[base], body, carry)
-        m, l, acc = carry
         if finalize:
-            outs[0][0, 0] = (acc / l[:, :HD]).astype(outs[0].dtype)
+            for h in range(heads):
+                m, acc = carry[h]
+                outs[0][h] = (acc[:, HD:LANES] / acc[:, LANES + HD :]).astype(outs[0].dtype)
         else:
-            outs[0][0] = m
-            outs[1][0] = l
-            outs[2][0] = acc
+            for h in range(heads):
+                m, acc = carry[h]
+                outs[0][h] = m
+                outs[1][h] = acc
 
     return kernel
 
 
 def attend(q_h, q_scene, pieces, lo, hi, state):
-    heads, qlen, _ = q_h.shape[1:]
+    heads, qlen, _ = q_h.shape
     nq = qlen // TQ
-    piece_rows = [kv.shape[2] for kv, _ in pieces]
+    piece_rows = [kv.shape[1] for kv, _ in pieces]
     has_state = state is not None
     finalize = has_state
-    kernel = make_kernel(piece_rows, nq, has_state, finalize)
+    kernel = make_kernel(piece_rows, heads, nq, has_state, finalize)
     in_specs = [
-        pl.BlockSpec((1, 1, TQ, HD), lambda h, i, *_: (0, h, i, 0)),
-        pl.BlockSpec((TQ, LANES), lambda h, i, *_: (i, 0)),
+        pl.BlockSpec((heads, TQ, HD), lambda i, *_: (0, i, 0)),
+        pl.BlockSpec((TQ, LANES), lambda i, *_: (i, 0)),
     ]
     args = [q_h, q_scene]
     for kv, ks in pieces:
-        rows = kv.shape[2]
-        in_specs.append(pl.BlockSpec((2, 1, rows, HD), lambda h, i, *_: (0, h, 0, 0)))
-        in_specs.append(pl.BlockSpec((1, rows), lambda h, i, *_: (0, 0)))
+        rows = kv.shape[1]
+        in_specs.append(pl.BlockSpec((heads, rows, LANES), lambda i, *_: (0, 0, 0)))
+        in_specs.append(pl.BlockSpec((1, rows), lambda i, *_: (0, 0)))
         args += [kv, ks]
     state_specs = [
-        pl.BlockSpec((1, TQ, LANES), lambda h, i, *_: (h, i, 0)),
-        pl.BlockSpec((1, TQ, LANES), lambda h, i, *_: (h, i, 0)),
-        pl.BlockSpec((1, TQ, HD), lambda h, i, *_: (h, i, 0)),
+        pl.BlockSpec((heads, TQ, w), lambda i, *_: (0, i, 0)) for w in (LANES, 2 * LANES)
     ]
     state_shapes = [
-        jax.ShapeDtypeStruct((heads, qlen, LANES), jnp.float32),
-        jax.ShapeDtypeStruct((heads, qlen, LANES), jnp.float32),
-        jax.ShapeDtypeStruct((heads, qlen, HD), jnp.float32),
+        jax.ShapeDtypeStruct((heads, qlen, w), jnp.float32) for w in (LANES, 2 * LANES)
     ]
     if has_state:
         in_specs += state_specs
         args += list(state)
     if finalize:
-        out_specs = [pl.BlockSpec((1, 1, TQ, HD), lambda h, i, *_: (0, h, i, 0))]
-        out_shape = [jax.ShapeDtypeStruct((1, heads, qlen, HD), jnp.bfloat16)]
+        out_specs = [pl.BlockSpec((heads, TQ, HD), lambda i, *_: (0, i, 0))]
+        out_shape = [jax.ShapeDtypeStruct((heads, qlen, HD), jnp.bfloat16)]
     else:
         out_specs = state_specs
         out_shape = state_shapes
@@ -157,13 +163,11 @@
         out_shape=out_shape,
         grid_spec=pltpu.PrefetchScalarGridSpec(
             num_scalar_prefetch=2,
-            grid=(heads, nq),
+            grid=(nq,),
             in_specs=in_specs,
             out_specs=out_specs,
         ),
-        compiler_params=pltpu.CompilerParams(
-            dimension_semantics=("arbitrary", "arbitrary")
-        ),
+        compiler_params=pltpu.CompilerParams(dimension_semantics=("arbitrary",)),
     )(lo, hi, *args)
 
 
@@ -177,26 +181,27 @@
     total_len = group_len * seq_count
     near = min(MOST, group_len)
     far = MOST - near
-    nq = group_len // TQ
 
     def head_major(x):
-        return x.reshape(tok_dev, head_count, local_heads, HD).transpose(1, 2, 0, 3)
+        width = x.shape[-1]
+        return x.reshape(tok_dev, head_count, local_heads, width).transpose(1, 2, 0, 3)
 
     angles = rotary_angles(coords)
     q_rot = head_major(rotate_rows(queries, angles, score_scale).astype(jnp.bfloat16))
-    k_rot = head_major(rotate_rows(keys, angles).astype(jnp.bfloat16))
-    v_hm = head_major(values)
-    kv_src = jnp.stack([k_rot, v_hm])
-    kv = lax.all_to_all(kv_src, "head", split_axis=1, concat_axis=3, tiled=True)
-    kv = kv.reshape(2, local_heads, group_len, HD)
+    k_rot = rotate_rows(keys, angles).astype(jnp.bfloat16)
+    v_rows = values.reshape(tok_dev, -1, HD)
+    kv_src = head_major(jnp.concatenate([k_rot, v_rows], axis=-1))
+    kv = lax.all_to_all(kv_src, "head", split_axis=0, concat_axis=2, tiled=True)
+    kv = kv.reshape(local_heads, group_len, 2 * HD)
     q_h = lax.all_to_all(q_rot, "head", split_axis=0, concat_axis=2, tiled=True)
+    q_h = q_h.reshape(local_heads, group_len, HD)
 
     below1 = shifted(kv, "seq", 1)
     above1 = shifted(kv, "seq", -1)
     halo = [(below1, -group_len), (above1, group_len)]
     if far > 0:
-        below2 = shifted(kv[:, :, group_len - far :], "seq", 2)
-        above2 = shifted(kv[:, :, :far], "seq", -2)
+        below2 = shifted(kv[:, group_len - far :], "seq", 2)
+        above2 = shifted(kv[:, :far], "seq", -2)
         halo = [(below2, -group_len - far)] + halo + [(above2, 2 * group_len)]
 
     own_start = lax.axis_index("seq") * group_len
@@ -212,7 +217,7 @@
     def tables(piece_list):
         los, his, prepared = [], [], []
         for kvp, offset in piece_list:
-            rows = kvp.shape[2]
+            rows = kvp.shape[1]
             p0 = own_start + offset
             k_pos = p0 + jnp.arange(rows, dtype=jnp.int32)
             k_valid = (k_pos >= 0) & (k_pos < total_len)

time: 159 us -> 133 us (0.84)
  the two profiles are of different devices: /device:TPU:160 before, /device:TPU:104 now
where the time goes in v4:
time: 133 us; the launch traced here: 132 us
  Pallas kernels  36.4 us (27%)
  waiting for transfers between devices  30.9 us (23%)
  starting transfers between devices  28.7 us (22%)
  blocking collectives  14.6 us (11%)
  local copies, waits for them, and re-layouts  13 us (10%)
  other arithmetic  8.78 us (7%)
    pallas_call x2, Pallas kernels, attend(): pl.pallas_call(kernel, out_shape=out_shape, grid_spec=pltpu.PrefetchScala...  36.4 us
    ppermute x4, starting transfers between devices, shifted(): return lax.ppermute(block, axis, route)  20.9 us
    ppermute x4, waiting for transfers between devices, shifted(): return lax.ppermute(block, axis, route)  20.4 us
    all_to_all x1, blocking collectives, local(): lax.all_to_all(out_src, 'head', split_axis=1, concat_axis=0, tiled=True)  14.6 us
    all_to_all x1, waiting for transfers between devices, local(): kv = lax.all_to_all(kv_src, 'head', split_axis=0, concat_axis=2, tiled=True)  10.5 us
    unnamed x17, local copies, waits for them, and re-layouts  4.74 us
    all_to_all x1, starting transfers between devices, local(): kv = lax.all_to_all(kv_src, 'head', split_axis=0, concat_axis=2, tiled=True)  4.3 us
    all_to_all x1, starting transfers between devices, local(): q_h = lax.all_to_all(q_rot, 'head', split_axis=0, concat_axis=2, tiled=True)  3.49 us
  transfers between devices with their start and end apart: 6, of which 3 were waited for; matrix products, arithmetic and copies ran while one was open for 9% of the time, Pallas kernels for 12%

profile of v4, /device:TPU:104, one launch (start us, length us, event | category | flops | bytes accessed | tf_op | source)
XLA Modules:
  0.0 132.5 jit_solution(1307994858517416332)
XLA Ops:
  0.0 0.7 convert_element_type.57
  0.8 1.3 copy.17
  3.1 1.0 copy.20
  5.2 1.1 maximum_bitcast_fusion
  6.3 4.3 %all-to-all-start.1 = ((bf16[8,4,128,128]{2,3,1,0:T(8,128)(2,1)}), bf16[8,4,128,128]{2,3,1,0:T(8,128)(2,1)S(1)}, u32[]{:S(2)}, u32[]{:S(2)}) async-start(bf16[8,4,128,128]{2,3,1,0:T(8,128)(2,1)} %maximum_bitcast_fusion), calls=%async_computation.1 | async-start | bytes 2097152 | tf_op jit(solution)/shard_map/all_to_all | solution.py:194
  11.2 0.6 gather_fusion.1
  11.9 0.6 gather_fusion
  13.1 0.6 pad_add_fusion.1.hi_ref
  13.9 0.9 fusion.1
  14.8 0.6 and_select_fusion.3.rest_7_
  15.4 0.6 and_select_fusion.1.rest_5_
  16.0 10.5 %all-to-all-done.1 = bf16[8,4,128,128]{2,3,1,0:T(8,128)(2,1)S(1)} async-done(((bf16[8,4,128,128]{2,3,1,0:T(8,128)(2,1)}), bf16[8,4,128,128]{2,3,1,0:T(8,128)(2,1)S(1)}, u32[]{:S(2)}, u32[]{:S(2)}) %all-to-all-start.1) | async-done | bytes 1048608 | tf_op jit(solution)/shard_map/all_to_all | solution.py:194
  26.5 3.5 %all-to-all-start = ((bf16[8,4,128,64]{2,3,1,0:T(8,128)(2,1)}), bf16[8,4,128,64]{2,3,1,0:T(8,128)(2,1)S(1)}, u32[]{:S(2)}, u32[]{:S(2)}) async-start(bf16[8,4,128,64]{2,3,1,0:T(8,128)(2,1)} %fusion.1), calls=%async_computation | async-start | bytes 1048576 | tf_op jit(solution)/shard_map/all_to_all | solution.py:196
  30.0 0.7 copy.21
  30.7 1.9 %collective-permute-start.2 = (bf16[4,1024,128]{2,1,0:T(8,128)(2,1)S(1)}, bf16[4,1024,128]{2,1,0:T(8,128)(2,1)S(1)}, u32[]{:S(2)}, u32[]{:S(2)}) collective-permute-start(bf16[4,1024,128]{2,1,0:T(8,128)(2,1)S(1)} %bitcast.45), channel_id=1, source_target_pairs={{32,0},{64,32},{96,64},{128,96},{160,128},{192,160},{224,192},{256... | collective-permute-start | bytes 3145736 | tf_op jit(solution)/shard_map/ppermute | solution.py:21
  32.6 4.3 %collective-permute-start.1 = (bf16[4,1024,128]{2,1,0:T(8,128)(2,1)S(1)}, bf16[4,1024,128]{2,1,0:T(8,128)(2,1)}, u32[]{:S(2)}, u32[]{:S(2)}) collective-permute-start(bf16[4,1024,128]{2,1,0:T(8,128)(2,1)S(1)} %bitcast.46), channel_id=1, source_target_pairs={{0,32},{32,64},{64,96},{96,128},{128,160},{160,192},{192,224},{224... | collective-permute-start | bytes 3145736 | tf_op jit(solution)/shard_map/ppermute | solution.py:21
  37.5 1.0 fusion.13
  38.5 12.6 %collective-permute-start.3 = (bf16[4,512,128]{2,1,0:T(8,128)(2,1)}, bf16[4,512,128]{2,1,0:T(8,128)(2,1)S(1)}, u32[]{:S(2)}, u32[]{:S(2)}) collective-permute-start(bf16[4,512,128]{2,1,0:T(8,128)(2,1)} %get-tuple-element.31), channel_id=1, source_target_pairs={{64,0},{96,32},{128,64},{160,96},{192,128},{224,160},{256,192},{28... | collective-permute-start | bytes 1572872 | tf_op jit(solution)/shard_map/ppermute | solution.py:21
  51.1 2.1 %collective-permute-start = (bf16[4,512,128]{2,1,0:T(8,128)(2,1)}, bf16[4,512,128]{2,1,0:T(8,128)(2,1)}, u32[]{:S(2)}, u32[]{:S(2)}) collective-permute-start(bf16[4,512,128]{2,1,0:T(8,128)(2,1)} %get-tuple-element.32), channel_id=1, source_target_pairs={{0,64},{32,96},{64,128},{96,160},{128,192},{160,224},{192,256},{22... | collective-permute-start | bytes 1572872 | tf_op jit(solution)/shard_map/ppermute | solution.py:21
  53.2 0.7 pad_add_fusion.lo_ref
  53.9 0.6 and_select_fusion.2.rest_3_
  54.5 0.6 and_select_fusion.rest_1_
  55.1 1.4 %copy.18 = bf16[1,4,8,128,64]{4,3,2,1,0:T(8,128)(2,1)} copy(bf16[1,4,8,128,64]{3,4,1,2,0:T(8,128)(2,1)S(1)} %bitcast.53) | data formatting | bytes 1048576 | tf_op jit(solution)/shard_map/all_to_all | solution.py:196
  56.5 1.0 broadcast_in_dim.22.qs_ref
  57.5 15.4 %shard_map.55 = (f32[4,1024,128]{2,1,0:T(8,128)}, f32[4,1024,256]{2,1,0:T(8,128)}) custom-call(s32[4]{0:T(128)} %get-tuple-element.16.lo_ref, s32[4]{0:T(128)} %get-tuple-element.15.hi_ref, bf16[4,1024,64]{2,1,0:T(8,128)(2,1)} %bitcast.43, s32[1024,128]{1,0:T(8,128)} %broadcast_in_dim.22.qs_ref, bf16[4,1024,128]{2,1,0:T(8,128)(2,1)} %bitcast.48, ...), custom_call_target="tpu_custom_call" | custom-call | tf_op jit(solution)/shard_map/pallas_call | solution.py:161
  72.9 1.1 collective-permute-done.3.rest_6_
  74.0 19.3 %collective-permute-done.rest_0_ = bf16[4,512,128]{2,1,0:T(8,128)(2,1)} collective-permute-done((bf16[4,512,128]{2,1,0:T(8,128)(2,1)}, bf16[4,512,128]{2,1,0:T(8,128)(2,1)}, u32[]{:S(2)}, u32[]{:S(2)}) %collective-permute-start) | collective-permute-done | bytes 524320 | tf_op jit(solution)/shard_map/ppermute | solution.py:21
  93.3 1.0 copy-done.2
  94.3 20.9 %shard_map.56 = bf16[4,1024,64]{2,1,0:T(8,128)(2,1)} custom-call(s32[16]{0:T(128)} %pad_add_fusion.lo_ref, s32[16]{0:T(128)} %pad_add_fusion.1.hi_ref, bf16[4,1024,64]{2,1,0:T(8,128)(2,1)} %bitcast.44, s32[1024,128]{1,0:T(8,128)} %broadcast_in_dim.22.qs_ref, bf16[4,512,128]{2,1,0:T(8,128)(2,1)} %collective-permute-done.rest_0_, ...), custom_call_target="tpu_custom_call" | custom-call | tf_op jit(solution)/shard_map/pallas_call | solution.py:161
  115.3 1.6 %copy.22 = bf16[4,8,128,64]{2,3,0,1:T(8,128)(2,1)S(1)} copy(bf16[4,8,128,64]{3,2,1,0:T(8,128)(2,1)} %bitcast.49) | data formatting | bytes 1048576 | tf_op jit(solution)/shard_map/reshape | solution.py:244
  116.9 14.6 %all_to_all.45 = bf16[4,8,128,64]{2,3,0,1:T(8,128)(2,1)S(1)} all-to-all(bf16[4,8,128,64]{2,3,0,1:T(8,128)(2,1)S(1)} %copy.22), channel_id=1, replica_groups=mesh['seq'=16,'head'=8,'dp'=4] {'head'}, dimensions={1} | all-to-all | bytes 1048576 | tf_op jit(solution)/shard_map/all_to_all | solution.py:245
  131.5 1.0 copy.23
  (42 shorter events, 4.0 us)
Async XLA Ops:
  0.0 2.2 %copy-start.4 = (bf16[128,2048]{1,0:T(8,128)(2,1)S(1)}, bf16[128,2048]{1,0:T(8,128)(2,1)}, u32[]{:S(2)}) copy-start(bf16[128,2048]{1,0:T(8,128)(2,1)} %param.8) | copy-start | bytes 1572868
  2.1 1.0 copy-start.5
  4.1 1.0 copy-start.1
  5.2 5.4 %copy-start.6 = (s32[32]{0:T(128)S(1)}, s32[32]{0:T(128)}, u32[]{:S(2)}) copy-start(s32[32]{0:T(128)} %param.11) | copy-start | bytes 388
  6.3 20.2 %all-to-all-start.1 = ((bf16[8,4,128,128]{2,3,1,0:T(8,128)(2,1)}), bf16[8,4,128,128]{2,3,1,0:T(8,128)(2,1)S(1)}, u32[]{:S(2)}, u32[]{:S(2)}) async-start(bf16[8,4,128,128]{2,3,1,0:T(8,128)(2,1)} %maximum_bitcast_fusion), calls=%async_computation.1 | async-start | bytes 2097152 | tf_op jit(solution)/shard_map/all_to_all | solution.py:194
  26.5 28.6 %all-to-all-start = ((bf16[8,4,128,64]{2,3,1,0:T(8,128)(2,1)}), bf16[8,4,128,64]{2,3,1,0:T(8,128)(2,1)S(1)}, u32[]{:S(2)}, u32[]{:S(2)}) async-start(bf16[8,4,128,64]{2,3,1,0:T(8,128)(2,1)} %fusion.1), calls=%async_computation | async-start | bytes 1048576 | tf_op jit(solution)/shard_map/all_to_all | solution.py:196
  30.7 26.8 %copy-start = (bf16[1,4,8,128,128]{4,3,2,1,0:T(8,128)(2,1)}, bf16[1,4,8,128,128]{4,3,2,1,0:T(8,128)(2,1)S(1)}, u32[]{:S(2)}) copy-start(bf16[1,4,8,128,128]{4,3,2,1,0:T(8,128)(2,1)S(1)} %copy.21) | copy-start | bytes 3145732
  30.7 62.6 %collective-permute-start.2 = (bf16[4,1024,128]{2,1,0:T(8,128)(2,1)S(1)}, bf16[4,1024,128]{2,1,0:T(8,128)(2,1)S(1)}, u32[]{:S(2)}, u32[]{:S(2)}) collective-permute-start(bf16[4,1024,128]{2,1,0:T(8,128)(2,1)S(1)} %bitcast.45), channel_id=1, source_target_pairs={{32,0},{64,32},{96,64},{128,96},{160,128},{192,160},{224,192},{256... | collective-permute-start | bytes 3145736 | tf_op jit(solution)/shard_map/ppermute | solution.py:21
  32.6 60.7 %collective-permute-start.1 = (bf16[4,1024,128]{2,1,0:T(8,128)(2,1)S(1)}, bf16[4,1024,128]{2,1,0:T(8,128)(2,1)}, u32[]{:S(2)}, u32[]{:S(2)}) collective-permute-start(bf16[4,1024,128]{2,1,0:T(8,128)(2,1)S(1)} %bitcast.46), channel_id=1, source_target_pairs={{0,32},{32,64},{64,96},{96,128},{128,160},{160,192},{192,224},{224... | collective-permute-start | bytes 3145736 | tf_op jit(solution)/shard_map/ppermute | solution.py:21
  38.5 35.4 %collective-permute-start.3 = (bf16[4,512,128]{2,1,0:T(8,128)(2,1)}, bf16[4,512,128]{2,1,0:T(8,128)(2,1)S(1)}, u32[]{:S(2)}, u32[]{:S(2)}) collective-permute-start(bf16[4,512,128]{2,1,0:T(8,128)(2,1)} %get-tuple-element.31), channel_id=1, source_target_pairs={{64,0},{96,32},{128,64},{160,96},{192,128},{224,160},{256,192},{28... | collective-permute-start | bytes 1572872 | tf_op jit(solution)/shard_map/ppermute | solution.py:21
  51.1 42.2 %collective-permute-start = (bf16[4,512,128]{2,1,0:T(8,128)(2,1)}, bf16[4,512,128]{2,1,0:T(8,128)(2,1)}, u32[]{:S(2)}, u32[]{:S(2)}) collective-permute-start(bf16[4,512,128]{2,1,0:T(8,128)(2,1)} %get-tuple-element.32), channel_id=1, source_target_pairs={{0,64},{32,96},{64,128},{96,160},{128,192},{160,224},{192,256},{22... | collective-permute-start | bytes 1572872 | tf_op jit(solution)/shard_map/ppermute | solution.py:21
  74.0 19.3 %copy-start.3 = (bf16[4,512,128]{2,1,0:T(8,128)(2,1)}, bf16[4,512,128]{2,1,0:T(8,128)(2,1)S(1)}, u32[]{:S(2)}) copy-start(bf16[4,512,128]{2,1,0:T(8,128)(2,1)S(1)} %collective-permute-done.3.rest_6_) | copy-start | bytes 1572868
  93.3 1.1 copy-start.2

commit v5 on v4

--- a/solution.py
+++ b/solution.py
@@ -126,12 +126,11 @@
     return kernel
 
 
-def attend(q_h, q_scene, pieces, lo, hi, state):
+def attend(q_h, q_scene, pieces, lo, hi, state, finalize):
     heads, qlen, _ = q_h.shape
     nq = qlen // TQ
     piece_rows = [kv.shape[1] for kv, _ in pieces]
     has_state = state is not None
-    finalize = has_state
     kernel = make_kernel(piece_rows, heads, nq, has_state, finalize)
     in_specs = [
         pl.BlockSpec((heads, TQ, HD), lambda i, *_: (0, i, 0)),
@@ -196,13 +195,22 @@
     q_h = lax.all_to_all(q_rot, "head", split_axis=0, concat_axis=2, tiled=True)
     q_h = q_h.reshape(local_heads, group_len, HD)
 
-    below1 = shifted(kv, "seq", 1)
-    above1 = shifted(kv, "seq", -1)
-    halo = [(below1, -group_len), (above1, group_len)]
+    half = group_len - far
+    below_hi = shifted(kv[:, half:], "seq", 1)
+    below_lo = shifted(kv[:, :half], "seq", 1)
+    above_lo = shifted(kv[:, :far], "seq", -1)
+    above_hi = shifted(kv[:, far:], "seq", -1)
+    near_pieces = [
+        (below_lo, -group_len),
+        (below_hi, -far),
+        (above_lo, group_len),
+        (above_hi, group_len + far),
+    ]
+    far_pieces = []
     if far > 0:
-        below2 = shifted(kv[:, group_len - far :], "seq", 2)
-        above2 = shifted(kv[:, :far], "seq", -2)
-        halo = [(below2, -group_len - far)] + halo + [(above2, 2 * group_len)]
+        below2 = shifted(below_hi, "seq", 1)
+        above2 = shifted(above_lo, "seq", -1)
+        far_pieces = [(below2, -group_len - far), (above2, 2 * group_len)]
 
     own_start = lax.axis_index("seq") * group_len
     scene_end = jnp.cumsum(lengths).astype(jnp.int32)
@@ -237,9 +245,15 @@
 
     q_scene_col = jnp.broadcast_to(q_scene.astype(jnp.int32)[:, None], (group_len, LANES))
     lo0, hi0, prep0 = tables([(kv, 0)])
-    state = attend(q_h, q_scene_col, prep0, lo0, hi0, None)
-    lo1, hi1, prep1 = tables(halo)
-    out_h = attend(q_h, q_scene_col, prep1, lo1, hi1, state)[0]
+    state = attend(q_h, q_scene_col, prep0, lo0, hi0, None, False)
+    if far_pieces:
+        lo1, hi1, prep1 = tables(near_pieces)
+        state = attend(q_h, q_scene_col, prep1, lo1, hi1, state, False)
+        lo2, hi2, prep2 = tables(far_pieces)
+        out_h = attend(q_h, q_scene_col, prep2, lo2, hi2, state, True)[0]
+    else:
+        lo1, hi1, prep1 = tables(near_pieces)
+        out_h = attend(q_h, q_scene_col, prep1, lo1, hi1, state, True)[0]
 
     out_src = out_h.reshape(local_heads, head_count, tok_dev, HD)
     back = lax.all_to_all(out_src, "head", split_axis=1, concat_axis=0, tiled=True)

time: 133 us -> 128 us (0.962)
  waiting for transfers between devices: 30.9 us -> 11 us
  Pallas kernels: 36.4 us -> 44.2 us
  starting transfers between devices: 28.7 us -> 33.8 us
    ppermute x4 -> x6, waiting for transfers between devices: 20.4 us -> 0.38 us  [shifted(): return lax.ppermute(block, axis, route)]
    pallas_call x2 -> x3, Pallas kernels: 36.4 us -> 44.2 us  [attend(): pl.pallas_call(kernel, out_shape=out_shape, grid_spec=pltpu.PrefetchScala...]
    ppermute x4 -> x6, starting transfers between devices: 20.9 us -> 26 us  [shifted(): return lax.ppermute(block, axis, route)]
    select_n x5 -> x7, other arithmetic: 2.99 us -> 3.96 us  [tables(): jnp.where(k_valid, scene_of(k_pos, scene_end), -1).astype(jnp.int32)]
    unnamed x17 -> x19, local copies, waits for them, and re-layouts: 4.74 us -> 4.47 us
  transfers between devices with their start and end apart: 6 -> 8, of which waited for: 3 -> 2; matrix products, arithmetic and copies ran while one was open for 9% -> 10% of each run, Pallas kernels for 12% -> 29%
where the time goes in v5:
time: 128 us; the launch traced here: 127 us
  Pallas kernels  44.2 us (35%)
  starting transfers between devices  33.8 us (26%)
  blocking collectives  14.9 us (12%)
  local copies, waits for them, and re-layouts  12.8 us (10%)
  waiting for transfers between devices  11 us (9%)
  other arithmetic  9.78 us (8%)
    pallas_call x3, Pallas kernels, attend(): pl.pallas_call(kernel, out_shape=out_shape, grid_spec=pltpu.PrefetchScala...  44.2 us
    ppermute x6, starting transfers between devices, shifted(): return lax.ppermute(block, axis, route)  26 us
    all_to_all x1, blocking collectives, local(): lax.all_to_all(out_src, 'head', split_axis=1, concat_axis=0, tiled=True)  14.9 us
    all_to_all x1, waiting for transfers between devices, local(): kv = lax.all_to_all(kv_src, 'head', split_axis=0, concat_axis=2, tiled=True)  10.6 us
    unnamed x19, local copies, waits for them, and re-layouts  4.47 us
    all_to_all x1, starting transfers between devices, local(): kv = lax.all_to_all(kv_src, 'head', split_axis=0, concat_axis=2, tiled=True)  4.3 us
    select_n x7, other arithmetic, tables(): jnp.where(k_valid, scene_of(k_pos, scene_end), -1).astype(jnp.int32)  3.96 us
    all_to_all x1, starting transfers between devices, local(): q_h = lax.all_to_all(q_rot, 'head', split_axis=0, concat_axis=2, tiled=True)  3.49 us
  transfers between devices with their start and end apart: 8, of which 2 were waited for; matrix products, arithmetic and copies ran while one was open for 10% of the time, Pallas kernels for 29%

profile of v5, /device:TPU:104, one launch (start us, length us, event | category | flops | bytes accessed | tf_op | source)
XLA Modules:
  0.0 126.8 jit_solution(4708450611394500403)
XLA Ops:
  0.0 0.7 convert_element_type.63
  0.8 1.3 %copy.17 = bf16[128,2048]{0,1:T(8,128)(2,1)S(1)} copy(bf16[128,2048]{1,0:T(8,128)(2,1)} %param.7) | data formatting | bytes 1048576 | tf_op args[0]
  3.1 1.0 copy.20
  5.2 1.1 maximum_bitcast_fusion
  6.3 4.3 %all-to-all-start.1 = ((bf16[8,4,128,128]{2,3,1,0:T(8,128)(2,1)}), bf16[8,4,128,128]{2,3,1,0:T(8,128)(2,1)S(1)}, u32[]{:S(2)}, u32[]{:S(2)}) async-start(bf16[8,4,128,128]{2,3,1,0:T(8,128)(2,1)} %maximum_bitcast_fusion), calls=%async_computation.1 | async-start | bytes 2097152 | tf_op jit(solution)/shard_map/all_to_all | solution.py:193
  11.9 0.9 fusion.1
  12.8 0.6 gather_fusion.1
  13.5 0.6 gather_fusion
  14.1 0.6 and_select_fusion.2.rest_5_
  14.7 0.6 and_select_fusion.3.rest_3_
  15.9 10.6 %all-to-all-done.1 = bf16[8,4,128,128]{2,3,1,0:T(8,128)(2,1)S(1)} async-done(((bf16[8,4,128,128]{2,3,1,0:T(8,128)(2,1)}), bf16[8,4,128,128]{2,3,1,0:T(8,128)(2,1)S(1)}, u32[]{:S(2)}, u32[]{:S(2)}) %all-to-all-start.1) | async-done | bytes 1048608 | tf_op jit(solution)/shard_map/all_to_all | solution.py:193
  26.5 3.5 %all-to-all-start = ((bf16[8,4,128,64]{2,3,1,0:T(8,128)(2,1)}), bf16[8,4,128,64]{2,3,1,0:T(8,128)(2,1)S(1)}, u32[]{:S(2)}, u32[]{:S(2)}) async-start(bf16[8,4,128,64]{2,3,1,0:T(8,128)(2,1)} %fusion.1), calls=%async_computation | async-start | bytes 1048576 | tf_op jit(solution)/shard_map/all_to_all | solution.py:195
  30.0 0.7 copy.21
  30.7 1.2 fusion.15
  31.9 4.3 %collective-permute-start = (bf16[4,512,128]{2,1,0:T(8,128)(2,1)}, bf16[4,512,128]{2,1,0:T(8,128)(2,1)S(1)}, u32[]{:S(2)}, u32[]{:S(2)}) collective-permute-start(bf16[4,512,128]{2,1,0:T(8,128)(2,1)} %get-tuple-element.41), channel_id=1, source_target_pairs={{0,32},{32,64},{64,96},{96,128},{128,160},{160,192},{192,224},{224... | collective-permute-start | bytes 1572872 | tf_op jit(solution)/shard_map/ppermute | solution.py:21
  36.1 1.9 %collective-permute-start.2 = (bf16[4,512,128]{2,1,0:T(8,128)(2,1)}, bf16[4,512,128]{2,1,0:T(8,128)(2,1)S(1)}, u32[]{:S(2)}, u32[]{:S(2)}) collective-permute-start(bf16[4,512,128]{2,1,0:T(8,128)(2,1)} %get-tuple-element.40), channel_id=1, source_target_pairs={{32,0},{64,32},{96,64},{128,96},{160,128},{192,160},{224,192},{256... | collective-permute-start | bytes 1572872 | tf_op jit(solution)/shard_map/ppermute | solution.py:21
  38.1 0.7 pad_add_fusion
  39.8 4.3 %collective-permute-start.4 = (bf16[4,512,128]{2,1,0:T(8,128)(2,1)}, bf16[4,512,128]{2,1,0:T(8,128)(2,1)}, u32[]{:S(2)}, u32[]{:S(2)}) collective-permute-start(bf16[4,512,128]{2,1,0:T(8,128)(2,1)} %get-tuple-element.40), channel_id=1, source_target_pairs={{0,32},{32,64},{64,96},{96,128},{128,160},{160,192},{192,224},{224... | collective-permute-start | bytes 1572872 | tf_op jit(solution)/shard_map/ppermute | solution.py:21
  44.1 6.7 %collective-permute-start.5 = (bf16[4,512,128]{2,1,0:T(8,128)(2,1)}, bf16[4,512,128]{2,1,0:T(8,128)(2,1)}, u32[]{:S(2)}, u32[]{:S(2)}) collective-permute-start(bf16[4,512,128]{2,1,0:T(8,128)(2,1)} %get-tuple-element.41), channel_id=1, source_target_pairs={{32,0},{64,32},{96,64},{128,96},{160,128},{192,160},{224,192},{256... | collective-permute-start | bytes 1572872 | tf_op jit(solution)/shard_map/ppermute | solution.py:21
  50.7 2.3 %collective-permute-start.1 = (bf16[4,512,128]{2,1,0:T(8,128)(2,1)S(1)}, bf16[4,512,128]{2,1,0:T(8,128)(2,1)S(1)}, u32[]{:S(2)}, u32[]{:S(2)}) collective-permute-start(bf16[4,512,128]{2,1,0:T(8,128)(2,1)S(1)} %collective-permute-done.rest_2_), channel_id=1, source_target_pairs={{0,32},{32,64},{64,96},{96,128},{128,160},{160,192},{192,224},{224... | collective-permute-start | bytes 1572872 | tf_op jit(solution)/shard_map/ppermute | solution.py:21
  53.4 6.7 %collective-permute-start.3 = (bf16[4,512,128]{2,1,0:T(8,128)(2,1)S(1)}, bf16[4,512,128]{2,1,0:T(8,128)(2,1)}, u32[]{:S(2)}, u32[]{:S(2)}) collective-permute-start(bf16[4,512,128]{2,1,0:T(8,128)(2,1)S(1)} %collective-permute-done.2.rest_4_), channel_id=1, source_target_pairs={{32,0},{64,32},{96,64},{128,96},{160,128},{192,160},{224,192},{256... | collective-permute-start | bytes 1572872 | tf_op jit(solution)/shard_map/ppermute | solution.py:21
  60.1 0.7 pad_add_fusion.2
  61.3 0.6 and_select_fusion.rest_1_
  61.9 1.4 %copy.18 = bf16[1,4,8,128,64]{4,3,2,1,0:T(8,128)(2,1)} copy(bf16[1,4,8,128,64]{3,4,1,2,0:T(8,128)(2,1)S(1)} %bitcast.54) | data formatting | bytes 1048576 | tf_op jit(solution)/shard_map/all_to_all | solution.py:195
  63.3 1.0 broadcast_in_dim.25.qs_ref
  64.3 15.6 %shard_map.55 = (f32[4,1024,128]{2,1,0:T(8,128)}, f32[4,1024,256]{2,1,0:T(8,128)}) custom-call(s32[4]{0:T(128)} %get-tuple-element.21.lo_ref, s32[4]{0:T(128)} %get-tuple-element.20.hi_ref, bf16[4,1024,64]{2,1,0:T(8,128)(2,1)} %bitcast.45, s32[1024,128]{1,0:T(8,128)} %broadcast_in_dim.25.qs_ref, bf16[4,1024,128]{2,1,0:T(8,128)(2,1)} %bitcast.49, ...), custom_call_target="tpu_custom_call" | custom-call | tf_op jit(solution)/shard_map/pallas_call | solution.py:160
  79.9 21.6 %shard_map.56 = (f32[4,1024,128]{2,1,0:T(8,128)}, f32[4,1024,256]{2,1,0:T(8,128)}) custom-call(s32[16]{0:T(128)} %get-tuple-element.61.lo_ref, s32[16]{0:T(128)} %get-tuple-element.62.hi_ref, bf16[4,1024,64]{2,1,0:T(8,128)(2,1)} %bitcast.46, s32[1024,128]{1,0:T(8,128)} %broadcast_in_dim.25.qs_ref, bf16[4,512,128]{2,1,0:T(8,128)(2,1)} %collective-permute-done.4.rest_0_, ...), custom_call_target="tpu_custom_call" | custom-call | tf_op jit(solution)/shard_map/pallas_call | solution.py:160
  101.6 0.8 copy-done.4
  102.3 7.0 %shard_map.57 = bf16[4,1024,64]{2,1,0:T(8,128)(2,1)} custom-call(s32[8]{0:T(128)} %get-tuple-element.59.lo_ref, s32[8]{0:T(128)} %get-tuple-element.60.hi_ref, bf16[4,1024,64]{2,1,0:T(8,128)(2,1)} %bitcast.47, s32[1024,128]{1,0:T(8,128)} %broadcast_in_dim.25.qs_ref, bf16[4,512,128]{2,1,0:T(8,128)(2,1)} %copy-done.4, s32[1,512]{1,0:T(1,128)} %and_select_fusion.6.rest_1_, ...), custom_call_target="tpu_custom_call" | custom-call | tf_op jit(solution)/shard_map/pallas_call | solution.py:160
  109.3 1.6 %copy.22 = bf16[4,8,128,64]{2,3,0,1:T(8,128)(2,1)S(1)} copy(bf16[4,8,128,64]{3,2,1,0:T(8,128)(2,1)} %bitcast.50) | data formatting | bytes 1048576 | tf_op jit(solution)/shard_map/reshape | solution.py:258
  110.9 14.9 %all_to_all.45 = bf16[4,8,128,64]{2,3,0,1:T(8,128)(2,1)S(1)} all-to-all(bf16[4,8,128,64]{2,3,0,1:T(8,128)(2,1)S(1)} %copy.22), channel_id=1, replica_groups=mesh['seq'=16,'head'=8,'dp'=4] {'head'}, dimensions={1} | all-to-all | bytes 1048576 | tf_op jit(solution)/shard_map/all_to_all | solution.py:259
  125.8 1.0 copy.23
  (52 shorter events, 6.0 us)
Async XLA Ops:
  0.0 2.2 %copy-start.5 = (bf16[128,2048]{1,0:T(8,128)(2,1)S(1)}, bf16[128,2048]{1,0:T(8,128)(2,1)}, u32[]{:S(2)}) copy-start(bf16[128,2048]{1,0:T(8,128)(2,1)} %param.8) | copy-start | bytes 1572868
  2.1 1.0 copy-start.6
  4.1 1.0 copy-start.1
  5.2 5.4 %copy-start.7 = (s32[32]{0:T(128)S(1)}, s32[32]{0:T(128)}, u32[]{:S(2)}) copy-start(s32[32]{0:T(128)} %param.11) | copy-start | bytes 388
  6.3 20.2 %all-to-all-start.1 = ((bf16[8,4,128,128]{2,3,1,0:T(8,128)(2,1)}), bf16[8,4,128,128]{2,3,1,0:T(8,128)(2,1)S(1)}, u32[]{:S(2)}, u32[]{:S(2)}) async-start(bf16[8,4,128,128]{2,3,1,0:T(8,128)(2,1)} %maximum_bitcast_fusion), calls=%async_computation.1 | async-start | bytes 2097152 | tf_op jit(solution)/shard_map/all_to_all | solution.py:193
  26.5 35.4 %all-to-all-start = ((bf16[8,4,128,64]{2,3,1,0:T(8,128)(2,1)}), bf16[8,4,128,64]{2,3,1,0:T(8,128)(2,1)S(1)}, u32[]{:S(2)}, u32[]{:S(2)}) async-start(bf16[8,4,128,64]{2,3,1,0:T(8,128)(2,1)} %fusion.1), calls=%async_computation | async-start | bytes 1048576 | tf_op jit(solution)/shard_map/all_to_all | solution.py:195
  30.7 33.6 %copy-start = (bf16[1,4,8,128,128]{4,3,2,1,0:T(8,128)(2,1)}, bf16[1,4,8,128,128]{4,3,2,1,0:T(8,128)(2,1)S(1)}, u32[]{:S(2)}) copy-start(bf16[1,4,8,128,128]{4,3,2,1,0:T(8,128)(2,1)S(1)} %copy.21) | copy-start | bytes 3145732
  31.9 18.9 %collective-permute-start = (bf16[4,512,128]{2,1,0:T(8,128)(2,1)}, bf16[4,512,128]{2,1,0:T(8,128)(2,1)S(1)}, u32[]{:S(2)}, u32[]{:S(2)}) collective-permute-start(bf16[4,512,128]{2,1,0:T(8,128)(2,1)} %get-tuple-element.41), channel_id=1, source_target_pairs={{0,32},{32,64},{64,96},{96,128},{128,160},{160,192},{192,224},{224... | collective-permute-start | bytes 1572872 | tf_op jit(solution)/shard_map/ppermute | solution.py:21
  36.1 17.3 %collective-permute-start.2 = (bf16[4,512,128]{2,1,0:T(8,128)(2,1)}, bf16[4,512,128]{2,1,0:T(8,128)(2,1)S(1)}, u32[]{:S(2)}, u32[]{:S(2)}) collective-permute-start(bf16[4,512,128]{2,1,0:T(8,128)(2,1)} %get-tuple-element.40), channel_id=1, source_target_pairs={{32,0},{64,32},{96,64},{128,96},{160,128},{192,160},{224,192},{256... | collective-permute-start | bytes 1572872 | tf_op jit(solution)/shard_map/ppermute | solution.py:21
  39.8 40.1 %collective-permute-start.4 = (bf16[4,512,128]{2,1,0:T(8,128)(2,1)}, bf16[4,512,128]{2,1,0:T(8,128)(2,1)}, u32[]{:S(2)}, u32[]{:S(2)}) collective-permute-start(bf16[4,512,128]{2,1,0:T(8,128)(2,1)} %get-tuple-element.40), channel_id=1, source_target_pairs={{0,32},{32,64},{64,96},{96,128},{128,160},{160,192},{192,224},{224... | collective-permute-start | bytes 1572872 | tf_op jit(solution)/shard_map/ppermute | solution.py:21
  44.1 35.9 %collective-permute-start.5 = (bf16[4,512,128]{2,1,0:T(8,128)(2,1)}, bf16[4,512,128]{2,1,0:T(8,128)(2,1)}, u32[]{:S(2)}, u32[]{:S(2)}) collective-permute-start(bf16[4,512,128]{2,1,0:T(8,128)(2,1)} %get-tuple-element.41), channel_id=1, source_target_pairs={{32,0},{64,32},{96,64},{128,96},{160,128},{192,160},{224,192},{256... | collective-permute-start | bytes 1572872 | tf_op jit(solution)/shard_map/ppermute | solution.py:21
  50.7 29.2 %copy-start.2 = (bf16[4,512,128]{2,1,0:T(8,128)(2,1)}, bf16[4,512,128]{2,1,0:T(8,128)(2,1)S(1)}, u32[]{:S(2)}) copy-start(bf16[4,512,128]{2,1,0:T(8,128)(2,1)S(1)} %collective-permute-done.rest_2_) | copy-start | bytes 1572868
  50.7 50.8 %collective-permute-start.1 = (bf16[4,512,128]{2,1,0:T(8,128)(2,1)S(1)}, bf16[4,512,128]{2,1,0:T(8,128)(2,1)S(1)}, u32[]{:S(2)}, u32[]{:S(2)}) collective-permute-start(bf16[4,512,128]{2,1,0:T(8,128)(2,1)S(1)} %collective-permute-done.rest_2_), channel_id=1, source_target_pairs={{0,32},{32,64},{64,96},{96,128},{128,160},{160,192},{192,224},{224... | collective-permute-start | bytes 1572872 | tf_op jit(solution)/shard_map/ppermute | solution.py:21
  53.4 26.5 %copy-start.3 = (bf16[4,512,128]{2,1,0:T(8,128)(2,1)}, bf16[4,512,128]{2,1,0:T(8,128)(2,1)S(1)}, u32[]{:S(2)}) copy-start(bf16[4,512,128]{2,1,0:T(8,128)(2,1)S(1)} %collective-permute-done.2.rest_4_) | copy-start | bytes 1572868
  53.4 48.2 %collective-permute-start.3 = (bf16[4,512,128]{2,1,0:T(8,128)(2,1)S(1)}, bf16[4,512,128]{2,1,0:T(8,128)(2,1)}, u32[]{:S(2)}, u32[]{:S(2)}) collective-permute-start(bf16[4,512,128]{2,1,0:T(8,128)(2,1)S(1)} %collective-permute-done.2.rest_4_), channel_id=1, source_target_pairs={{32,0},{64,32},{96,64},{128,96},{160,128},{192,160},{224,192},{256... | collective-permute-start | bytes 1572872 | tf_op jit(solution)/shard_map/ppermute | solution.py:21
  101.6 0.8 copy-start.4

commit v6 on v5

--- a/solution.py
+++ b/solution.py
@@ -126,30 +126,36 @@
     return kernel
 
 
-def attend(q_h, q_scene, pieces, lo, hi, state, finalize):
+def attend(q_h, q_scene, pieces, lo, hi, state, finalize, group=None):
     heads, qlen, _ = q_h.shape
+    g = 0
+    if group is not None:
+        g, heads = group
     nq = qlen // TQ
     piece_rows = [kv.shape[1] for kv, _ in pieces]
     has_state = state is not None
     kernel = make_kernel(piece_rows, heads, nq, has_state, finalize)
     in_specs = [
-        pl.BlockSpec((heads, TQ, HD), lambda i, *_: (0, i, 0)),
+        pl.BlockSpec((heads, TQ, HD), lambda i, *_: (g, i, 0)),
         pl.BlockSpec((TQ, LANES), lambda i, *_: (i, 0)),
     ]
     args = [q_h, q_scene]
     for kv, ks in pieces:
         rows = kv.shape[1]
-        in_specs.append(pl.BlockSpec((heads, rows, LANES), lambda i, *_: (0, 0, 0)))
+        in_specs.append(pl.BlockSpec((heads, rows, LANES), lambda i, *_: (g, 0, 0)))
         in_specs.append(pl.BlockSpec((1, rows), lambda i, *_: (0, 0)))
         args += [kv, ks]
     state_specs = [
         pl.BlockSpec((heads, TQ, w), lambda i, *_: (0, i, 0)) for w in (LANES, 2 * LANES)
     ]
+    in_state_specs = [
+        pl.BlockSpec((heads, TQ, w), lambda i, *_: (g, i, 0)) for w in (LANES, 2 * LANES)
+    ]
     state_shapes = [
         jax.ShapeDtypeStruct((heads, qlen, w), jnp.float32) for w in (LANES, 2 * LANES)
     ]
     if has_state:
-        in_specs += state_specs
+        in_specs += in_state_specs
         args += list(state)
     if finalize:
         out_specs = [pl.BlockSpec((heads, TQ, HD), lambda i, *_: (0, i, 0))]
@@ -246,18 +252,22 @@
     q_scene_col = jnp.broadcast_to(q_scene.astype(jnp.int32)[:, None], (group_len, LANES))
     lo0, hi0, prep0 = tables([(kv, 0)])
     state = attend(q_h, q_scene_col, prep0, lo0, hi0, None, False)
+    lo1, hi1, prep1 = tables(near_pieces)
     if far_pieces:
-        lo1, hi1, prep1 = tables(near_pieces)
         state = attend(q_h, q_scene_col, prep1, lo1, hi1, state, False)
         lo2, hi2, prep2 = tables(far_pieces)
-        out_h = attend(q_h, q_scene_col, prep2, lo2, hi2, state, True)[0]
+        last = (lo2, hi2, prep2)
     else:
-        lo1, hi1, prep1 = tables(near_pieces)
-        out_h = attend(q_h, q_scene_col, prep1, lo1, hi1, state, True)[0]
-
-    out_src = out_h.reshape(local_heads, head_count, tok_dev, HD)
-    back = lax.all_to_all(out_src, "head", split_axis=1, concat_axis=0, tiled=True)
-    back = back.reshape(head_count * local_heads, tok_dev, HD)
+        last = (lo1, hi1, prep1)
+    split = 2 if local_heads % 2 == 0 else 1
+    part_heads = local_heads // split
+    returned = []
+    for g in range(split):
+        out_g = attend(q_h, q_scene_col, last[2], last[0], last[1], state, True, (g, part_heads))[0]
+        out_src = out_g.reshape(part_heads, head_count, tok_dev, HD)
+        back = lax.all_to_all(out_src, "head", split_axis=1, concat_axis=0, tiled=True)
+        returned.append(back.reshape(head_count, part_heads, tok_dev, HD))
+    back = jnp.stack(returned, axis=1).reshape(head_count * local_heads, tok_dev, HD)
     return back.transpose(1, 0, 2).reshape(tok_dev, all_cols)
 
 

time: 128 us -> 137 us (1.070)
  the two profiles are of different devices: /device:TPU:104 before, /device:TPU:40 now
where the time goes in v6:
time: 137 us; the launch traced here: 136 us
  Pallas kernels  45 us (33%)
  starting transfers between devices  42.3 us (31%)
  local copies, waits for them, and re-layouts  14.6 us (11%)
  waiting for transfers between devices  12.9 us (9%)
  blocking collectives  11.3 us (8%)
  other arithmetic  9.61 us (7%)
    pallas_call x4, Pallas kernels, attend(): pl.pallas_call(kernel, out_shape=out_shape, grid_spec=pltpu.PrefetchScala...  45 us
    ppermute x6, starting transfers between devices, shifted(): return lax.ppermute(block, axis, route)  29.8 us
    all_to_all x1, blocking collectives, local(): lax.all_to_all(out_src, 'head', split_axis=1, concat_axis=0, tiled=True)  11.3 us
    all_to_all x1, waiting for transfers between devices, local(): kv = lax.all_to_all(kv_src, 'head', split_axis=0, concat_axis=2, tiled=True)  10.7 us
    all_to_all x1, starting transfers between devices, local(): lax.all_to_all(out_src, 'head', split_axis=1, concat_axis=0, tiled=True)  4.71 us
    unnamed x19, local copies, waits for them, and re-layouts  4.66 us
    all_to_all x1, starting transfers between devices, local(): kv = lax.all_to_all(kv_src, 'head', split_axis=0, concat_axis=2, tiled=True)  4.3 us
    select_n x7, other arithmetic, tables(): jnp.where(k_valid, scene_of(k_pos, scene_end), -1).astype(jnp.int32)  3.93 us
  transfers between devices with their start and end apart: 9, of which 3 were waited for; matrix products, arithmetic and copies ran while one was open for 10% of the time, Pallas kernels for 29%

profile of v6, /device:TPU:40, one launch (start us, length us, event | category | flops | bytes accessed | tf_op | source)
XLA Modules:
  0.0 135.9 jit_solution(12496429397056061402)
XLA Ops:
  0.0 0.7 convert_element_type.63
  0.8 1.3 copy.18
  3.1 1.0 copy.21
  5.2 1.1 maximum_bitcast_fusion
  6.3 4.3 %all-to-all-start.1 = ((bf16[8,4,128,128]{2,3,1,0:T(8,128)(2,1)}), bf16[8,4,128,128]{2,3,1,0:T(8,128)(2,1)S(1)}, u32[]{:S(2)}, u32[]{:S(2)}) async-start(bf16[8,4,128,128]{2,3,1,0:T(8,128)(2,1)} %maximum_bitcast_fusion), calls=%async_computation.1 | async-start | bytes 2097152 | tf_op jit(solution)/shard_map/all_to_all | solution.py:199
  11.9 0.9 fusion.1
  12.8 0.6 gather_fusion.1
  13.5 0.6 gather_fusion
  15.8 10.7 %all-to-all-done.1 = bf16[8,4,128,128]{2,3,1,0:T(8,128)(2,1)S(1)} async-done(((bf16[8,4,128,128]{2,3,1,0:T(8,128)(2,1)}), bf16[8,4,128,128]{2,3,1,0:T(8,128)(2,1)S(1)}, u32[]{:S(2)}, u32[]{:S(2)}) %all-to-all-start.1) | async-done | bytes 1048608 | tf_op jit(solution)/shard_map/all_to_all | solution.py:199
  26.5 3.5 %all-to-all-start = ((bf16[8,4,128,64]{2,3,1,0:T(8,128)(2,1)}), bf16[8,4,128,64]{2,3,1,0:T(8,128)(2,1)S(1)}, u32[]{:S(2)}, u32[]{:S(2)}) async-start(bf16[8,4,128,64]{2,3,1,0:T(8,128)(2,1)} %fusion.1), calls=%async_computation | async-start | bytes 1048576 | tf_op jit(solution)/shard_map/all_to_all | solution.py:201
  30.0 0.7 copy.22
  30.7 1.1 fusion.15
  31.8 4.3 %collective-permute-start = (bf16[4,512,128]{2,1,0:T(8,128)(2,1)}, bf16[4,512,128]{2,1,0:T(8,128)(2,1)S(1)}, u32[]{:S(2)}, u32[]{:S(2)}) collective-permute-start(bf16[4,512,128]{2,1,0:T(8,128)(2,1)} %get-tuple-element.41), channel_id=1, source_target_pairs={{0,32},{32,64},{64,96},{96,128},{128,160},{160,192},{192,224},{224... | collective-permute-start | bytes 1572872 | tf_op jit(solution)/shard_map/ppermute | solution.py:21
  36.1 9.4 %collective-permute-start.2 = (bf16[4,512,128]{2,1,0:T(8,128)(2,1)}, bf16[4,512,128]{2,1,0:T(8,128)(2,1)}, u32[]{:S(2)}, u32[]{:S(2)}) collective-permute-start(bf16[4,512,128]{2,1,0:T(8,128)(2,1)} %get-tuple-element.40), channel_id=1, source_target_pairs={{32,0},{64,32},{96,64},{128,96},{160,128},{192,160},{224,192},{256... | collective-permute-start | bytes 1572872 | tf_op jit(solution)/shard_map/ppermute | solution.py:21
  47.2 1.9 %collective-permute-start.4 = (bf16[4,512,128]{2,1,0:T(8,128)(2,1)}, bf16[4,512,128]{2,1,0:T(8,128)(2,1)}, u32[]{:S(2)}, u32[]{:S(2)}) collective-permute-start(bf16[4,512,128]{2,1,0:T(8,128)(2,1)} %get-tuple-element.40), channel_id=1, source_target_pairs={{0,32},{32,64},{64,96},{96,128},{128,160},{160,192},{192,224},{224... | collective-permute-start | bytes 1572872 | tf_op jit(solution)/shard_map/ppermute | solution.py:21
  49.1 6.0 %collective-permute-start.5 = (bf16[4,512,128]{2,1,0:T(8,128)(2,1)}, bf16[4,512,128]{2,1,0:T(8,128)(2,1)}, u32[]{:S(2)}, u32[]{:S(2)}) collective-permute-start(bf16[4,512,128]{2,1,0:T(8,128)(2,1)} %get-tuple-element.41), channel_id=1, source_target_pairs={{32,0},{64,32},{96,64},{128,96},{160,128},{192,160},{224,192},{256... | collective-permute-start | bytes 1572872 | tf_op jit(solution)/shard_map/ppermute | solution.py:21
  55.1 1.4 %collective-permute-done.rest_2_ = bf16[4,512,128]{2,1,0:T(8,128)(2,1)S(1)} collective-permute-done((bf16[4,512,128]{2,1,0:T(8,128)(2,1)}, bf16[4,512,128]{2,1,0:T(8,128)(2,1)S(1)}, u32[]{:S(2)}, u32[]{:S(2)}) %collective-permute-start) | collective-permute-done | bytes 524320 | tf_op jit(solution)/shard_map/ppermute | solution.py:21
  56.5 1.9 %collective-permute-start.1 = (bf16[4,512,128]{2,1,0:T(8,128)(2,1)S(1)}, bf16[4,512,128]{2,1,0:T(8,128)(2,1)S(1)}, u32[]{:S(2)}, u32[]{:S(2)}) collective-permute-start(bf16[4,512,128]{2,1,0:T(8,128)(2,1)S(1)} %collective-permute-done.rest_2_), channel_id=1, source_target_pairs={{0,32},{32,64},{64,96},{96,128},{128,160},{160,192},{192,224},{224... | collective-permute-start | bytes 1572872 | tf_op jit(solution)/shard_map/ppermute | solution.py:21
  58.5 6.3 %collective-permute-start.3 = (bf16[4,512,128]{2,1,0:T(8,128)(2,1)}, bf16[4,512,128]{2,1,0:T(8,128)(2,1)S(1)}, u32[]{:S(2)}, u32[]{:S(2)}) collective-permute-start(bf16[4,512,128]{2,1,0:T(8,128)(2,1)} %collective-permute-done.2.rest_4_), channel_id=1, source_target_pairs={{32,0},{64,32},{96,64},{128,96},{160,128},{192,160},{224,192},{256... | collective-permute-start | bytes 1572872 | tf_op jit(solution)/shard_map/ppermute | solution.py:21
  66.5 1.4 %copy.19 = bf16[1,4,8,128,64]{4,3,2,1,0:T(8,128)(2,1)} copy(bf16[1,4,8,128,64]{3,4,1,2,0:T(8,128)(2,1)S(1)} %bitcast.61) | data formatting | bytes 1048576 | tf_op jit(solution)/shard_map/all_to_all | solution.py:201
  67.9 1.0 broadcast_in_dim.25.qs_ref
  68.9 14.2 %shard_map.55 = (f32[4,1024,128]{2,1,0:T(8,128)}, f32[4,1024,256]{2,1,0:T(8,128)}) custom-call(s32[4]{0:T(128)} %get-tuple-element.21.lo_ref, s32[4]{0:T(128)} %get-tuple-element.20.hi_ref, bf16[4,1024,64]{2,1,0:T(8,128)(2,1)} %bitcast.52, s32[1024,128]{1,0:T(8,128)} %broadcast_in_dim.25.qs_ref, bf16[4,1024,128]{2,1,0:T(8,128)(2,1)} %bitcast.57, ...), custom_call_target="tpu_custom_call" | custom-call | tf_op jit(solution)/shard_map/pallas_call | solution.py:166
  83.1 20.0 %shard_map.56 = (f32[4,1024,128]{2,1,0:T(8,128)}, f32[4,1024,256]{2,1,0:T(8,128)}) custom-call(s32[16]{0:T(128)} %get-tuple-element.61.lo_ref, s32[16]{0:T(128)} %get-tuple-element.62.hi_ref, bf16[4,1024,64]{2,1,0:T(8,128)(2,1)} %bitcast.53, s32[1024,128]{1,0:T(8,128)} %broadcast_in_dim.25.qs_ref, bf16[4,512,128]{2,1,0:T(8,128)(2,1)} %collective-permute-done.4.rest_0_, ...), custom_call_target="tpu_custom_call" | custom-call | tf_op jit(solution)/shard_map/pallas_call | solution.py:166
  103.1 0.8 copy-done.1
  104.0 5.4 %shard_map.57 = bf16[2,1024,64]{2,1,0:T(8,128)(2,1)} custom-call(s32[8]{0:T(128)} %get-tuple-element.59.lo_ref, s32[8]{0:T(128)} %get-tuple-element.60.hi_ref, bf16[4,1024,64]{2,1,0:T(8,128)(2,1)} %bitcast.54, s32[1024,128]{1,0:T(8,128)} %broadcast_in_dim.25.qs_ref, bf16[4,512,128]{2,1,0:T(8,128)(2,1)} %copy-done.1, s32[1,512]{1,0:T(1,128)} %and_select_fusion.6.rest_1_, ...), custom_call_target="tpu_custom_call" | custom-call | tf_op jit(solution)/shard_map/pallas_call | solution.py:166
  109.4 1.9 %copy.23 = bf16[2,8,128,64]{2,3,0,1:T(8,128)(2,1)} copy(bf16[2,8,128,64]{3,2,1,0:T(8,128)(2,1)} %bitcast.65) | data formatting | bytes 524288 | tf_op jit(solution)/shard_map/reshape | solution.py:267
  111.4 4.7 %all-to-all-start.2 = ((bf16[2,8,128,64]{2,3,0,1:T(8,128)(2,1)}), bf16[2,8,128,64]{2,3,0,1:T(8,128)(2,1)S(1)}, u32[]{:S(2)}, u32[]{:S(2)}) async-start(bf16[2,8,128,64]{2,3,0,1:T(8,128)(2,1)} %copy.23), calls=%async_computation.2 | async-start | bytes 524288 | tf_op jit(solution)/shard_map/all_to_all | solution.py:268
  116.1 5.4 %shard_map.58 = bf16[2,1024,64]{2,1,0:T(8,128)(2,1)} custom-call(s32[8]{0:T(128)} %get-tuple-element.59.lo_ref, s32[8]{0:T(128)} %get-tuple-element.60.hi_ref, bf16[4,1024,64]{2,1,0:T(8,128)(2,1)} %bitcast.55, s32[1024,128]{1,0:T(8,128)} %broadcast_in_dim.25.qs_ref, bf16[4,512,128]{2,1,0:T(8,128)(2,1)} %copy-done.1, s32[1,512]{1,0:T(1,128)} %and_select_fusion.6.rest_1_, ...), custom_call_target="tpu_custom_call" | custom-call | tf_op jit(solution)/shard_map/pallas_call | solution.py:166
  121.5 1.2 copy.24
  122.7 0.9 all-to-all-done.2
  123.6 11.3 %all_to_all.60 = bf16[2,8,128,64]{2,3,0,1:T(8,128)(2,1)S(1)} all-to-all(bf16[2,8,128,64]{2,3,0,1:T(8,128)(2,1)S(1)} %copy.24), channel_id=1, replica_groups=mesh['seq'=16,'head'=8,'dp'=4] {'head'}, dimensions={1} | all-to-all | bytes 524288 | tf_op jit(solution)/shard_map/all_to_all | solution.py:268
  134.9 1.0 copy.25
  (57 shorter events, 8.7 us)
Async XLA Ops:
  0.0 2.2 %copy-start.5 = (bf16[128,2048]{1,0:T(8,128)(2,1)S(1)}, bf16[128,2048]{1,0:T(8,128)(2,1)}, u32[]{:S(2)}) copy-start(bf16[128,2048]{1,0:T(8,128)(2,1)} %param.8) | copy-start | bytes 1572868
  2.1 1.0 copy-start.6
  4.1 1.0 copy-start.3
  5.2 5.4 %copy-start.7 = (s32[32]{0:T(128)S(1)}, s32[32]{0:T(128)}, u32[]{:S(2)}) copy-start(s32[32]{0:T(128)} %param.11) | copy-start | bytes 388
  6.3 20.2 %all-to-all-start.1 = ((bf16[8,4,128,128]{2,3,1,0:T(8,128)(2,1)}), bf16[8,4,128,128]{2,3,1,0:T(8,128)(2,1)S(1)}, u32[]{:S(2)}, u32[]{:S(2)}) async-start(bf16[8,4,128,128]{2,3,1,0:T(8,128)(2,1)} %maximum_bitcast_fusion), calls=%async_computation.1 | async-start | bytes 2097152 | tf_op jit(solution)/shard_map/all_to_all | solution.py:199
  26.5 40.0 %all-to-all-start = ((bf16[8,4,128,64]{2,3,1,0:T(8,128)(2,1)}), bf16[8,4,128,64]{2,3,1,0:T(8,128)(2,1)S(1)}, u32[]{:S(2)}, u32[]{:S(2)}) async-start(bf16[8,4,128,64]{2,3,1,0:T(8,128)(2,1)} %fusion.1), calls=%async_computation | async-start | bytes 1048576 | tf_op jit(solution)/shard_map/all_to_all | solution.py:201
  30.7 38.2 %copy-start = (bf16[1,4,8,128,128]{4,3,2,1,0:T(8,128)(2,1)}, bf16[1,4,8,128,128]{4,3,2,1,0:T(8,128)(2,1)S(1)}, u32[]{:S(2)}) copy-start(bf16[1,4,8,128,128]{4,3,2,1,0:T(8,128)(2,1)S(1)} %copy.22) | copy-start | bytes 3145732
  31.8 24.7 %collective-permute-start = (bf16[4,512,128]{2,1,0:T(8,128)(2,1)}, bf16[4,512,128]{2,1,0:T(8,128)(2,1)S(1)}, u32[]{:S(2)}, u32[]{:S(2)}) collective-permute-start(bf16[4,512,128]{2,1,0:T(8,128)(2,1)} %get-tuple-element.41), channel_id=1, source_target_pairs={{0,32},{32,64},{64,96},{96,128},{128,160},{160,192},{192,224},{224... | collective-permute-start | bytes 1572872 | tf_op jit(solution)/shard_map/ppermute | solution.py:21
  36.1 22.3 %collective-permute-start.2 = (bf16[4,512,128]{2,1,0:T(8,128)(2,1)}, bf16[4,512,128]{2,1,0:T(8,128)(2,1)}, u32[]{:S(2)}, u32[]{:S(2)}) collective-permute-start(bf16[4,512,128]{2,1,0:T(8,128)(2,1)} %get-tuple-element.40), channel_id=1, source_target_pairs={{32,0},{64,32},{96,64},{128,96},{160,128},{192,160},{224,192},{256... | collective-permute-start | bytes 1572872 | tf_op jit(solution)/shard_map/ppermute | solution.py:21
  47.2 35.9 %collective-permute-start.4 = (bf16[4,512,128]{2,1,0:T(8,128)(2,1)}, bf16[4,512,128]{2,1,0:T(8,128)(2,1)}, u32[]{:S(2)}, u32[]{:S(2)}) collective-permute-start(bf16[4,512,128]{2,1,0:T(8,128)(2,1)} %get-tuple-element.40), channel_id=1, source_target_pairs={{0,32},{32,64},{64,96},{96,128},{128,160},{160,192},{192,224},{224... | collective-permute-start | bytes 1572872 | tf_op jit(solution)/shard_map/ppermute | solution.py:21
  49.1 34.0 %collective-permute-start.5 = (bf16[4,512,128]{2,1,0:T(8,128)(2,1)}, bf16[4,512,128]{2,1,0:T(8,128)(2,1)}, u32[]{:S(2)}, u32[]{:S(2)}) collective-permute-start(bf16[4,512,128]{2,1,0:T(8,128)(2,1)} %get-tuple-element.41), channel_id=1, source_target_pairs={{32,0},{64,32},{96,64},{128,96},{160,128},{192,160},{224,192},{256... | collective-permute-start | bytes 1572872 | tf_op jit(solution)/shard_map/ppermute | solution.py:21
  56.5 26.6 %copy-start.4 = (bf16[4,512,128]{2,1,0:T(8,128)(2,1)}, bf16[4,512,128]{2,1,0:T(8,128)(2,1)S(1)}, u32[]{:S(2)}) copy-start(bf16[4,512,128]{2,1,0:T(8,128)(2,1)S(1)} %collective-permute-done.rest_2_) | copy-start | bytes 1572868
  56.5 46.5 %collective-permute-start.1 = (bf16[4,512,128]{2,1,0:T(8,128)(2,1)S(1)}, bf16[4,512,128]{2,1,0:T(8,128)(2,1)S(1)}, u32[]{:S(2)}, u32[]{:S(2)}) collective-permute-start(bf16[4,512,128]{2,1,0:T(8,128)(2,1)S(1)} %collective-permute-done.rest_2_), channel_id=1, source_target_pairs={{0,32},{32,64},{64,96},{96,128},{128,160},{160,192},{192,224},{224... | collective-permute-start | bytes 1572872 | tf_op jit(solution)/shard_map/ppermute | solution.py:21
  58.5 44.6 %collective-permute-start.3 = (bf16[4,512,128]{2,1,0:T(8,128)(2,1)}, bf16[4,512,128]{2,1,0:T(8,128)(2,1)S(1)}, u32[]{:S(2)}, u32[]{:S(2)}) collective-permute-start(bf16[4,512,128]{2,1,0:T(8,128)(2,1)} %collective-permute-done.2.rest_4_), channel_id=1, source_target_pairs={{32,0},{64,32},{96,64},{128,96},{160,128},{192,160},{224,192},{256... | collective-permute-start | bytes 1572872 | tf_op jit(solution)/shard_map/ppermute | solution.py:21
  103.1 0.8 copy-start.1
  103.1 1.0 copy-start.2
  111.4 12.2 %all-to-all-start.2 = ((bf16[2,8,128,64]{2,3,0,1:T(8,128)(2,1)}), bf16[2,8,128,64]{2,3,0,1:T(8,128)(2,1)S(1)}, u32[]{:S(2)}, u32[]{:S(2)}) async-start(bf16[2,8,128,64]{2,3,0,1:T(8,128)(2,1)} %copy.23), calls=%async_computation.2 | async-start | bytes 524288 | tf_op jit(solution)/shard_map/all_to_all | solution.py:268

commit v7 on v5

--- a/solution.py
+++ b/solution.py
@@ -244,16 +244,16 @@
         )
 
     q_scene_col = jnp.broadcast_to(q_scene.astype(jnp.int32)[:, None], (group_len, LANES))
-    lo0, hi0, prep0 = tables([(kv, 0)])
+    if far_pieces:
+        first = [(kv, 0), (below_hi, -far), (above_lo, group_len)]
+        second = [(below_lo, -group_len), (above_hi, group_len + far)] + far_pieces
+    else:
+        first = [(kv, 0)]
+        second = near_pieces
+    lo0, hi0, prep0 = tables(first)
     state = attend(q_h, q_scene_col, prep0, lo0, hi0, None, False)
-    if far_pieces:
-        lo1, hi1, prep1 = tables(near_pieces)
-        state = attend(q_h, q_scene_col, prep1, lo1, hi1, state, False)
-        lo2, hi2, prep2 = tables(far_pieces)
-        out_h = attend(q_h, q_scene_col, prep2, lo2, hi2, state, True)[0]
-    else:
-        lo1, hi1, prep1 = tables(near_pieces)
-        out_h = attend(q_h, q_scene_col, prep1, lo1, hi1, state, True)[0]
+    lo1, hi1, prep1 = tables(second)
+    out_h = attend(q_h, q_scene_col, prep1, lo1, hi1, state, True)[0]
 
     out_src = out_h.reshape(local_heads, head_count, tok_dev, HD)
     back = lax.all_to_all(out_src, "head", split_axis=1, concat_axis=0, tiled=True)

time: 128 us -> 126 us (0.984)
  the two profiles are of different devices: /device:TPU:104 before, /device:TPU:8 now
where the time goes in v7:
time: 126 us; the launch traced here: 125 us
  Pallas kernels  38.8 us (31%)
  starting transfers between devices  36.4 us (29%)
  blocking collectives  14.9 us (12%)
  local copies, waits for them, and re-layouts  13.1 us (10%)
  waiting for transfers between devices  12.6 us (10%)
  other arithmetic  9.21 us (7%)
    pallas_call x2, Pallas kernels, attend(): pl.pallas_call(kernel, out_shape=out_shape, grid_spec=pltpu.PrefetchScala...  38.8 us
    ppermute x6, starting transfers between devices, shifted(): return lax.ppermute(block, axis, route)  28.6 us
    all_to_all x1, blocking collectives, local(): lax.all_to_all(out_src, 'head', split_axis=1, concat_axis=0, tiled=True)  14.9 us
    all_to_all x1, waiting for transfers between devices, local(): kv = lax.all_to_all(kv_src, 'head', split_axis=0, concat_axis=2, tiled=True)  11.2 us
    unnamed x19, local copies, waits for them, and re-layouts  4.79 us
    all_to_all x1, starting transfers between devices, local(): kv = lax.all_to_all(kv_src, 'head', split_axis=0, concat_axis=2, tiled=True)  4.3 us
    select_n x7, other arithmetic, tables(): jnp.where(k_valid, scene_of(k_pos, scene_end), -1).astype(jnp.int32)  3.99 us
    all_to_all x1, starting transfers between devices, local(): q_h = lax.all_to_all(q_rot, 'head', split_axis=0, concat_axis=2, tiled=True)  3.49 us
  transfers between devices with their start and end apart: 8, of which 2 were waited for; matrix products, arithmetic and copies ran while one was open for 10% of the time, Pallas kernels for 19%

profile of v7, /device:TPU:8, one launch (start us, length us, event | category | flops | bytes accessed | tf_op | source)
XLA Modules:
  0.0 125.4 jit_solution(11358258087158665667)
XLA Ops:
  0.0 0.7 convert_element_type.63
  0.8 1.3 %copy.17 = bf16[128,2048]{0,1:T(8,128)(2,1)S(1)} copy(bf16[128,2048]{1,0:T(8,128)(2,1)} %param.7) | data formatting | bytes 1048576 | tf_op args[0]
  3.1 1.0 copy.20
  5.2 1.1 maximum_bitcast_fusion
  6.3 4.3 %all-to-all-start.1 = ((bf16[8,4,128,128]{2,3,1,0:T(8,128)(2,1)}), bf16[8,4,128,128]{2,3,1,0:T(8,128)(2,1)S(1)}, u32[]{:S(2)}, u32[]{:S(2)}) async-start(bf16[8,4,128,128]{2,3,1,0:T(8,128)(2,1)} %maximum_bitcast_fusion), calls=%async_computation.1 | async-start | bytes 2097152 | tf_op jit(solution)/shard_map/all_to_all | solution.py:193
  11.9 0.9 fusion.1
  12.8 0.6 gather_fusion.1
  13.5 0.6 gather_fusion
  15.3 11.2 %all-to-all-done.1 = bf16[8,4,128,128]{2,3,1,0:T(8,128)(2,1)S(1)} async-done(((bf16[8,4,128,128]{2,3,1,0:T(8,128)(2,1)}), bf16[8,4,128,128]{2,3,1,0:T(8,128)(2,1)S(1)}, u32[]{:S(2)}, u32[]{:S(2)}) %all-to-all-start.1) | async-done | bytes 1048608 | tf_op jit(solution)/shard_map/all_to_all | solution.py:193
  26.5 3.5 %all-to-all-start = ((bf16[8,4,128,64]{2,3,1,0:T(8,128)(2,1)}), bf16[8,4,128,64]{2,3,1,0:T(8,128)(2,1)S(1)}, u32[]{:S(2)}, u32[]{:S(2)}) async-start(bf16[8,4,128,64]{2,3,1,0:T(8,128)(2,1)} %fusion.1), calls=%async_computation | async-start | bytes 1048576 | tf_op jit(solution)/shard_map/all_to_all | solution.py:195
  30.0 0.7 copy.21
  30.7 1.2 fusion.15
  31.9 4.3 %collective-permute-start.2 = (bf16[4,512,128]{2,1,0:T(8,128)(2,1)}, bf16[4,512,128]{2,1,0:T(8,128)(2,1)}, u32[]{:S(2)}, u32[]{:S(2)}) collective-permute-start(bf16[4,512,128]{2,1,0:T(8,128)(2,1)} %get-tuple-element.36), channel_id=1, source_target_pairs={{0,32},{32,64},{64,96},{96,128},{128,160},{160,192},{192,224},{224... | collective-permute-start | bytes 1572872 | tf_op jit(solution)/shard_map/ppermute | solution.py:21
  36.1 8.5 %collective-permute-start.4 = (bf16[4,512,128]{2,1,0:T(8,128)(2,1)}, bf16[4,512,128]{2,1,0:T(8,128)(2,1)}, u32[]{:S(2)}, u32[]{:S(2)}) collective-permute-start(bf16[4,512,128]{2,1,0:T(8,128)(2,1)} %get-tuple-element.37), channel_id=1, source_target_pairs={{32,0},{64,32},{96,64},{128,96},{160,128},{192,160},{224,192},{256... | collective-permute-start | bytes 1572872 | tf_op jit(solution)/shard_map/ppermute | solution.py:21
  44.6 0.7 pad_add_fusion.2
  45.8 0.6 and_select_fusion.5.rest_3_
  46.4 1.9 %collective-permute-start = (bf16[4,512,128]{2,1,0:T(8,128)(2,1)}, bf16[4,512,128]{2,1,0:T(8,128)(2,1)S(1)}, u32[]{:S(2)}, u32[]{:S(2)}) collective-permute-start(bf16[4,512,128]{2,1,0:T(8,128)(2,1)} %get-tuple-element.37), channel_id=1, source_target_pairs={{0,32},{32,64},{64,96},{96,128},{128,160},{160,192},{192,224},{224... | collective-permute-start | bytes 1572872 | tf_op jit(solution)/shard_map/ppermute | solution.py:21
  48.3 6.0 %collective-permute-start.1 = (bf16[4,512,128]{2,1,0:T(8,128)(2,1)}, bf16[4,512,128]{2,1,0:T(8,128)(2,1)S(1)}, u32[]{:S(2)}, u32[]{:S(2)}) collective-permute-start(bf16[4,512,128]{2,1,0:T(8,128)(2,1)} %get-tuple-element.36), channel_id=1, source_target_pairs={{32,0},{64,32},{96,64},{128,96},{160,128},{192,160},{224,192},{256... | collective-permute-start | bytes 1572872 | tf_op jit(solution)/shard_map/ppermute | solution.py:21
  54.4 1.4 %collective-permute-done.2.rest_2_ = bf16[4,512,128]{2,1,0:T(8,128)(2,1)} collective-permute-done((bf16[4,512,128]{2,1,0:T(8,128)(2,1)}, bf16[4,512,128]{2,1,0:T(8,128)(2,1)}, u32[]{:S(2)}, u32[]{:S(2)}) %collective-permute-start.2) | collective-permute-done | bytes 524320 | tf_op jit(solution)/shard_map/ppermute | solution.py:21
  55.8 1.9 %collective-permute-start.3 = (bf16[4,512,128]{2,1,0:T(8,128)(2,1)}, bf16[4,512,128]{2,1,0:T(8,128)(2,1)S(1)}, u32[]{:S(2)}, u32[]{:S(2)}) collective-permute-start(bf16[4,512,128]{2,1,0:T(8,128)(2,1)} %collective-permute-done.2.rest_2_), channel_id=1, source_target_pairs={{0,32},{32,64},{64,96},{96,128},{128,160},{160,192},{192,224},{224... | collective-permute-start | bytes 1572872 | tf_op jit(solution)/shard_map/ppermute | solution.py:21
  57.7 6.0 %collective-permute-start.5 = (bf16[4,512,128]{2,1,0:T(8,128)(2,1)}, bf16[4,512,128]{2,1,0:T(8,128)(2,1)}, u32[]{:S(2)}, u32[]{:S(2)}) collective-permute-start(bf16[4,512,128]{2,1,0:T(8,128)(2,1)} %collective-permute-done.4.rest_4_), channel_id=1, source_target_pairs={{32,0},{64,32},{96,64},{128,96},{160,128},{192,160},{224,192},{256... | collective-permute-start | bytes 1572872 | tf_op jit(solution)/shard_map/ppermute | solution.py:21
  63.7 0.6 pad_add_fusion
  64.4 0.6 and_select_fusion.6.rest_1_
  65.0 0.6 and_select_fusion.rest_1_
  65.6 1.3 %copy.18 = bf16[1,4,8,128,64]{4,3,2,1,0:T(8,128)(2,1)} copy(bf16[1,4,8,128,64]{3,4,1,2,0:T(8,128)(2,1)S(1)} %bitcast.53) | data formatting | bytes 1048576 | tf_op jit(solution)/shard_map/all_to_all | solution.py:195
  66.9 1.0 broadcast_in_dim.25.qs_ref
  67.9 23.6 %shard_map.55 = (f32[4,1024,128]{2,1,0:T(8,128)}, f32[4,1024,256]{2,1,0:T(8,128)}) custom-call(s32[12]{0:T(128)} %get-tuple-element.55.lo_ref, s32[12]{0:T(128)} %get-tuple-element.56.hi_ref, bf16[4,1024,64]{2,1,0:T(8,128)(2,1)} %bitcast.45, s32[1024,128]{1,0:T(8,128)} %broadcast_in_dim.25.qs_ref, bf16[4,1024,128]{2,1,0:T(8,128)(2,1)} %bitcast.48, ...), custom_call_target="tpu_custom_call" | custom-call | tf_op jit(solution)/shard_map/pallas_call | solution.py:160
  91.6 0.8 copy-done.2
  92.7 15.2 %shard_map.56 = bf16[4,1024,64]{2,1,0:T(8,128)(2,1)} custom-call(s32[16]{0:T(128)} %get-tuple-element.57.lo_ref, s32[16]{0:T(128)} %get-tuple-element.58.hi_ref, bf16[4,1024,64]{2,1,0:T(8,128)(2,1)} %bitcast.46, s32[1024,128]{1,0:T(8,128)} %broadcast_in_dim.25.qs_ref, bf16[4,512,128]{2,1,0:T(8,128)(2,1)} %copy-done.2, s32[1,512]{1,0:T(1,128)} %and_select_fusion.6.rest_1_, ...), custom_call_target="tpu_custom_call" | custom-call | tf_op jit(solution)/shard_map/pallas_call | solution.py:160
  107.9 1.6 %copy.22 = bf16[4,8,128,64]{2,3,0,1:T(8,128)(2,1)S(1)} copy(bf16[4,8,128,64]{3,2,1,0:T(8,128)(2,1)} %bitcast.49) | data formatting | bytes 1048576 | tf_op jit(solution)/shard_map/reshape | solution.py:258
  109.5 14.9 %all_to_all.45 = bf16[4,8,128,64]{2,3,0,1:T(8,128)(2,1)S(1)} all-to-all(bf16[4,8,128,64]{2,3,0,1:T(8,128)(2,1)S(1)} %copy.22), channel_id=1, replica_groups=mesh['seq'=16,'head'=8,'dp'=4] {'head'}, dimensions={1} | all-to-all | bytes 1048576 | tf_op jit(solution)/shard_map/all_to_all | solution.py:259
  124.4 1.0 copy.23
  (51 shorter events, 5.4 us)
Async XLA Ops:
  0.0 2.2 %copy-start.5 = (bf16[128,2048]{1,0:T(8,128)(2,1)S(1)}, bf16[128,2048]{1,0:T(8,128)(2,1)}, u32[]{:S(2)}) copy-start(bf16[128,2048]{1,0:T(8,128)(2,1)} %param.8) | copy-start | bytes 1572868
  2.1 1.0 copy-start.6
  4.1 1.0 copy-start.1
  5.2 5.4 %copy-start.7 = (s32[32]{0:T(128)S(1)}, s32[32]{0:T(128)}, u32[]{:S(2)}) copy-start(s32[32]{0:T(128)} %param.11) | copy-start | bytes 388
  6.3 20.2 %all-to-all-start.1 = ((bf16[8,4,128,128]{2,3,1,0:T(8,128)(2,1)}), bf16[8,4,128,128]{2,3,1,0:T(8,128)(2,1)S(1)}, u32[]{:S(2)}, u32[]{:S(2)}) async-start(bf16[8,4,128,128]{2,3,1,0:T(8,128)(2,1)} %maximum_bitcast_fusion), calls=%async_computation.1 | async-start | bytes 2097152 | tf_op jit(solution)/shard_map/all_to_all | solution.py:193
  26.5 39.0 %all-to-all-start = ((bf16[8,4,128,64]{2,3,1,0:T(8,128)(2,1)}), bf16[8,4,128,64]{2,3,1,0:T(8,128)(2,1)S(1)}, u32[]{:S(2)}, u32[]{:S(2)}) async-start(bf16[8,4,128,64]{2,3,1,0:T(8,128)(2,1)} %fusion.1), calls=%async_computation | async-start | bytes 1048576 | tf_op jit(solution)/shard_map/all_to_all | solution.py:195
  30.7 37.2 %copy-start = (bf16[1,4,8,128,128]{4,3,2,1,0:T(8,128)(2,1)}, bf16[1,4,8,128,128]{4,3,2,1,0:T(8,128)(2,1)S(1)}, u32[]{:S(2)}) copy-start(bf16[1,4,8,128,128]{4,3,2,1,0:T(8,128)(2,1)S(1)} %copy.21) | copy-start | bytes 3145732
  31.9 23.9 %collective-permute-start.2 = (bf16[4,512,128]{2,1,0:T(8,128)(2,1)}, bf16[4,512,128]{2,1,0:T(8,128)(2,1)}, u32[]{:S(2)}, u32[]{:S(2)}) collective-permute-start(bf16[4,512,128]{2,1,0:T(8,128)(2,1)} %get-tuple-element.36), channel_id=1, source_target_pairs={{0,32},{32,64},{64,96},{96,128},{128,160},{160,192},{192,224},{224... | collective-permute-start | bytes 1572872 | tf_op jit(solution)/shard_map/ppermute | solution.py:21
  36.1 21.5 %collective-permute-start.4 = (bf16[4,512,128]{2,1,0:T(8,128)(2,1)}, bf16[4,512,128]{2,1,0:T(8,128)(2,1)}, u32[]{:S(2)}, u32[]{:S(2)}) collective-permute-start(bf16[4,512,128]{2,1,0:T(8,128)(2,1)} %get-tuple-element.37), channel_id=1, source_target_pairs={{32,0},{64,32},{96,64},{128,96},{160,128},{192,160},{224,192},{256... | collective-permute-start | bytes 1572872 | tf_op jit(solution)/shard_map/ppermute | solution.py:21
  46.4 45.1 %collective-permute-start = (bf16[4,512,128]{2,1,0:T(8,128)(2,1)}, bf16[4,512,128]{2,1,0:T(8,128)(2,1)S(1)}, u32[]{:S(2)}, u32[]{:S(2)}) collective-permute-start(bf16[4,512,128]{2,1,0:T(8,128)(2,1)} %get-tuple-element.37), channel_id=1, source_target_pairs={{0,32},{32,64},{64,96},{96,128},{128,160},{160,192},{192,224},{224... | collective-permute-start | bytes 1572872 | tf_op jit(solution)/shard_map/ppermute | solution.py:21
  48.3 43.2 %collective-permute-start.1 = (bf16[4,512,128]{2,1,0:T(8,128)(2,1)}, bf16[4,512,128]{2,1,0:T(8,128)(2,1)S(1)}, u32[]{:S(2)}, u32[]{:S(2)}) collective-permute-start(bf16[4,512,128]{2,1,0:T(8,128)(2,1)} %get-tuple-element.36), channel_id=1, source_target_pairs={{32,0},{64,32},{96,64},{128,96},{160,128},{192,160},{224,192},{256... | collective-permute-start | bytes 1572872 | tf_op jit(solution)/shard_map/ppermute | solution.py:21
  55.8 35.8 %collective-permute-start.3 = (bf16[4,512,128]{2,1,0:T(8,128)(2,1)}, bf16[4,512,128]{2,1,0:T(8,128)(2,1)S(1)}, u32[]{:S(2)}, u32[]{:S(2)}) collective-permute-start(bf16[4,512,128]{2,1,0:T(8,128)(2,1)} %collective-permute-done.2.rest_2_), channel_id=1, source_target_pairs={{0,32},{32,64},{64,96},{96,128},{128,160},{160,192},{192,224},{224... | collective-permute-start | bytes 1572872 | tf_op jit(solution)/shard_map/ppermute | solution.py:21
  57.7 33.9 %collective-permute-start.5 = (bf16[4,512,128]{2,1,0:T(8,128)(2,1)}, bf16[4,512,128]{2,1,0:T(8,128)(2,1)}, u32[]{:S(2)}, u32[]{:S(2)}) collective-permute-start(bf16[4,512,128]{2,1,0:T(8,128)(2,1)} %collective-permute-done.4.rest_4_), channel_id=1, source_target_pairs={{32,0},{64,32},{96,64},{128,96},{160,128},{192,160},{224,192},{256... | collective-permute-start | bytes 1572872 | tf_op jit(solution)/shard_map/ppermute | solution.py:21
  91.5 0.8 copy-start.2
  91.6 1.0 copy-start.3
  91.6 1.1 copy-start.4

commit v8 on v7

--- a/solution.py
+++ b/solution.py
@@ -13,6 +13,7 @@
 
 TQ = 256
 TK = 512
+TK_HALO = 256
 
 
 def shifted(block, axis, distance):
@@ -59,7 +60,7 @@
 LANES = 128
 
 
-def make_kernel(piece_rows, heads, nq, has_state, finalize):
+def make_kernel(piece_rows, heads, nq, has_state, finalize, TK):
     n_pieces = len(piece_rows)
 
     def kernel(lo_ref, hi_ref, q_ref, qs_ref, *rest):
@@ -126,12 +127,12 @@
     return kernel
 
 
-def attend(q_h, q_scene, pieces, lo, hi, state, finalize):
+def attend(q_h, q_scene, pieces, lo, hi, state, finalize, tk):
     heads, qlen, _ = q_h.shape
     nq = qlen // TQ
     piece_rows = [kv.shape[1] for kv, _ in pieces]
     has_state = state is not None
-    kernel = make_kernel(piece_rows, heads, nq, has_state, finalize)
+    kernel = make_kernel(piece_rows, heads, nq, has_state, finalize, tk)
     in_specs = [
         pl.BlockSpec((heads, TQ, HD), lambda i, *_: (0, i, 0)),
         pl.BlockSpec((TQ, LANES), lambda i, *_: (i, 0)),
@@ -222,7 +223,7 @@
     span_lo = jnp.take(scene_begin, first_scene)
     span_hi = jnp.take(scene_end, last_scene)
 
-    def tables(piece_list):
+    def tables(piece_list, TK):
         los, his, prepared = [], [], []
         for kvp, offset in piece_list:
             rows = kvp.shape[1]
@@ -250,10 +251,10 @@
     else:
         first = [(kv, 0)]
         second = near_pieces
-    lo0, hi0, prep0 = tables(first)
-    state = attend(q_h, q_scene_col, prep0, lo0, hi0, None, False)
-    lo1, hi1, prep1 = tables(second)
-    out_h = attend(q_h, q_scene_col, prep1, lo1, hi1, state, True)[0]
+    lo0, hi0, prep0 = tables(first, TK)
+    state = attend(q_h, q_scene_col, prep0, lo0, hi0, None, False, TK)
+    lo1, hi1, prep1 = tables(second, TK_HALO)
+    out_h = attend(q_h, q_scene_col, prep1, lo1, hi1, state, True, TK_HALO)[0]
 
     out_src = out_h.reshape(local_heads, head_count, tok_dev, HD)
     back = lax.all_to_all(out_src, "head", split_axis=1, concat_axis=0, tiled=True)

time: 126 us -> 126 us (level)
  the two profiles are of different devices: /device:TPU:8 before, /device:TPU:56 now
where the time goes in v8:
time: 126 us; the launch traced here: 125 us
  Pallas kernels  37.6 us (30%)
  starting transfers between devices  37.5 us (30%)
  blocking collectives  14.9 us (12%)
  local copies, waits for them, and re-layouts  13.1 us (10%)
  waiting for transfers between devices  12.6 us (10%)
  other arithmetic  9.21 us (7%)
    pallas_call x2, Pallas kernels, attend(): pl.pallas_call(kernel, out_shape=out_shape, grid_spec=pltpu.PrefetchScala...  37.6 us
    ppermute x6, starting transfers between devices, shifted(): return lax.ppermute(block, axis, route)  29.7 us
    all_to_all x1, blocking collectives, local(): lax.all_to_all(out_src, 'head', split_axis=1, concat_axis=0, tiled=True)  14.9 us
    all_to_all x1, waiting for transfers between devices, local(): kv = lax.all_to_all(kv_src, 'head', split_axis=0, concat_axis=2, tiled=True)  11.2 us
    unnamed x19, local copies, waits for them, and re-layouts  4.79 us
    all_to_all x1, starting transfers between devices, local(): kv = lax.all_to_all(kv_src, 'head', split_axis=0, concat_axis=2, tiled=True)  4.3 us
    select_n x7, other arithmetic, tables(): jnp.where(k_valid, scene_of(k_pos, scene_end), -1).astype(jnp.int32)  3.99 us
    all_to_all x1, starting transfers between devices, local(): q_h = lax.all_to_all(q_rot, 'head', split_axis=0, concat_axis=2, tiled=True)  3.49 us
  transfers between devices with their start and end apart: 8, of which 2 were waited for; matrix products, arithmetic and copies ran while one was open for 10% of the time, Pallas kernels for 23%

profile of v8, /device:TPU:56, one launch (start us, length us, event | category | flops | bytes accessed | tf_op | source)
XLA Modules:
  0.0 125.2 jit_solution(8927937612968069465)
XLA Ops:
  0.0 0.7 convert_element_type.63
  0.8 1.3 %copy.17 = bf16[128,2048]{0,1:T(8,128)(2,1)S(1)} copy(bf16[128,2048]{1,0:T(8,128)(2,1)} %param.7) | data formatting | bytes 1048576 | tf_op args[0]
  3.1 1.0 copy.20
  5.2 1.1 maximum_bitcast_fusion
  6.3 4.3 %all-to-all-start.1 = ((bf16[8,4,128,128]{2,3,1,0:T(8,128)(2,1)}), bf16[8,4,128,128]{2,3,1,0:T(8,128)(2,1)S(1)}, u32[]{:S(2)}, u32[]{:S(2)}) async-start(bf16[8,4,128,128]{2,3,1,0:T(8,128)(2,1)} %maximum_bitcast_fusion), calls=%async_computation.1 | async-start | bytes 2097152 | tf_op jit(solution)/shard_map/all_to_all | solution.py:194
  11.9 0.9 fusion.1
  12.8 0.6 gather_fusion.1
  13.5 0.6 gather_fusion
  15.3 11.2 %all-to-all-done.1 = bf16[8,4,128,128]{2,3,1,0:T(8,128)(2,1)S(1)} async-done(((bf16[8,4,128,128]{2,3,1,0:T(8,128)(2,1)}), bf16[8,4,128,128]{2,3,1,0:T(8,128)(2,1)S(1)}, u32[]{:S(2)}, u32[]{:S(2)}) %all-to-all-start.1) | async-done | bytes 1048608 | tf_op jit(solution)/shard_map/all_to_all | solution.py:194
  26.5 3.5 %all-to-all-start = ((bf16[8,4,128,64]{2,3,1,0:T(8,128)(2,1)}), bf16[8,4,128,64]{2,3,1,0:T(8,128)(2,1)S(1)}, u32[]{:S(2)}, u32[]{:S(2)}) async-start(bf16[8,4,128,64]{2,3,1,0:T(8,128)(2,1)} %fusion.1), calls=%async_computation | async-start | bytes 1048576 | tf_op jit(solution)/shard_map/all_to_all | solution.py:196
  30.0 0.7 copy.21
  30.7 1.2 fusion.15
  31.9 4.3 %collective-permute-start.2 = (bf16[4,512,128]{2,1,0:T(8,128)(2,1)}, bf16[4,512,128]{2,1,0:T(8,128)(2,1)}, u32[]{:S(2)}, u32[]{:S(2)}) collective-permute-start(bf16[4,512,128]{2,1,0:T(8,128)(2,1)} %get-tuple-element.36), channel_id=1, source_target_pairs={{0,32},{32,64},{64,96},{96,128},{128,160},{160,192},{192,224},{224... | collective-permute-start | bytes 1572872 | tf_op jit(solution)/shard_map/ppermute | solution.py:22
  36.1 9.4 %collective-permute-start.4 = (bf16[4,512,128]{2,1,0:T(8,128)(2,1)}, bf16[4,512,128]{2,1,0:T(8,128)(2,1)}, u32[]{:S(2)}, u32[]{:S(2)}) collective-permute-start(bf16[4,512,128]{2,1,0:T(8,128)(2,1)} %get-tuple-element.37), channel_id=1, source_target_pairs={{32,0},{64,32},{96,64},{128,96},{160,128},{192,160},{224,192},{256... | collective-permute-start | bytes 1572872 | tf_op jit(solution)/shard_map/ppermute | solution.py:22
  45.5 0.7 pad_add_fusion.2
  46.7 0.6 and_select_fusion.5.rest_3_
  47.3 1.9 %collective-permute-start = (bf16[4,512,128]{2,1,0:T(8,128)(2,1)}, bf16[4,512,128]{2,1,0:T(8,128)(2,1)S(1)}, u32[]{:S(2)}, u32[]{:S(2)}) collective-permute-start(bf16[4,512,128]{2,1,0:T(8,128)(2,1)} %get-tuple-element.37), channel_id=1, source_target_pairs={{0,32},{32,64},{64,96},{96,128},{128,160},{160,192},{192,224},{224... | collective-permute-start | bytes 1572872 | tf_op jit(solution)/shard_map/ppermute | solution.py:22
  49.2 6.0 %collective-permute-start.1 = (bf16[4,512,128]{2,1,0:T(8,128)(2,1)}, bf16[4,512,128]{2,1,0:T(8,128)(2,1)S(1)}, u32[]{:S(2)}, u32[]{:S(2)}) collective-permute-start(bf16[4,512,128]{2,1,0:T(8,128)(2,1)} %get-tuple-element.36), channel_id=1, source_target_pairs={{32,0},{64,32},{96,64},{128,96},{160,128},{192,160},{224,192},{256... | collective-permute-start | bytes 1572872 | tf_op jit(solution)/shard_map/ppermute | solution.py:22
  55.3 1.4 %collective-permute-done.2.rest_2_ = bf16[4,512,128]{2,1,0:T(8,128)(2,1)} collective-permute-done((bf16[4,512,128]{2,1,0:T(8,128)(2,1)}, bf16[4,512,128]{2,1,0:T(8,128)(2,1)}, u32[]{:S(2)}, u32[]{:S(2)}) %collective-permute-start.2) | collective-permute-done | bytes 524320 | tf_op jit(solution)/shard_map/ppermute | solution.py:22
  56.7 1.9 %collective-permute-start.3 = (bf16[4,512,128]{2,1,0:T(8,128)(2,1)}, bf16[4,512,128]{2,1,0:T(8,128)(2,1)S(1)}, u32[]{:S(2)}, u32[]{:S(2)}) collective-permute-start(bf16[4,512,128]{2,1,0:T(8,128)(2,1)} %collective-permute-done.2.rest_2_), channel_id=1, source_target_pairs={{0,32},{32,64},{64,96},{96,128},{128,160},{160,192},{192,224},{224... | collective-permute-start | bytes 1572872 | tf_op jit(solution)/shard_map/ppermute | solution.py:22
  58.6 6.2 %collective-permute-start.5 = (bf16[4,512,128]{2,1,0:T(8,128)(2,1)}, bf16[4,512,128]{2,1,0:T(8,128)(2,1)}, u32[]{:S(2)}, u32[]{:S(2)}) collective-permute-start(bf16[4,512,128]{2,1,0:T(8,128)(2,1)} %collective-permute-done.4.rest_4_), channel_id=1, source_target_pairs={{32,0},{64,32},{96,64},{128,96},{160,128},{192,160},{224,192},{256... | collective-permute-start | bytes 1572872 | tf_op jit(solution)/shard_map/ppermute | solution.py:22
  64.8 0.6 pad_add_fusion
  65.4 0.6 and_select_fusion.6.rest_1_
  66.0 0.6 and_select_fusion.rest_1_
  66.6 1.3 %copy.18 = bf16[1,4,8,128,64]{4,3,2,1,0:T(8,128)(2,1)} copy(bf16[1,4,8,128,64]{3,4,1,2,0:T(8,128)(2,1)S(1)} %bitcast.53) | data formatting | bytes 1048576 | tf_op jit(solution)/shard_map/all_to_all | solution.py:196
  68.0 1.0 broadcast_in_dim.25.qs_ref
  69.0 29.2 %shard_map.55 = (f32[4,1024,128]{2,1,0:T(8,128)}, f32[4,1024,256]{2,1,0:T(8,128)}) custom-call(s32[12]{0:T(128)} %get-tuple-element.55.lo_ref, s32[12]{0:T(128)} %get-tuple-element.56.hi_ref, bf16[4,1024,64]{2,1,0:T(8,128)(2,1)} %bitcast.45, s32[1024,128]{1,0:T(8,128)} %broadcast_in_dim.25.qs_ref, bf16[4,1024,128]{2,1,0:T(8,128)(2,1)} %bitcast.48, ...), custom_call_target="tpu_custom_call" | custom-call | tf_op jit(solution)/shard_map/pallas_call | solution.py:161
  98.3 0.8 copy-done.2
  99.4 8.4 %shard_map.56 = bf16[4,1024,64]{2,1,0:T(8,128)(2,1)} custom-call(s32[16]{0:T(128)} %get-tuple-element.57.lo_ref, s32[16]{0:T(128)} %get-tuple-element.58.hi_ref, bf16[4,1024,64]{2,1,0:T(8,128)(2,1)} %bitcast.46, s32[1024,128]{1,0:T(8,128)} %broadcast_in_dim.25.qs_ref, bf16[4,512,128]{2,1,0:T(8,128)(2,1)} %copy-done.2, s32[1,512]{1,0:T(1,128)} %and_select_fusion.6.rest_1_, ...), custom_call_target="tpu_custom_call" | custom-call | tf_op jit(solution)/shard_map/pallas_call | solution.py:161
  107.8 1.6 %copy.22 = bf16[4,8,128,64]{2,3,0,1:T(8,128)(2,1)S(1)} copy(bf16[4,8,128,64]{3,2,1,0:T(8,128)(2,1)} %bitcast.49) | data formatting | bytes 1048576 | tf_op jit(solution)/shard_map/reshape | solution.py:259
  109.4 14.9 %all_to_all.45 = bf16[4,8,128,64]{2,3,0,1:T(8,128)(2,1)S(1)} all-to-all(bf16[4,8,128,64]{2,3,0,1:T(8,128)(2,1)S(1)} %copy.22), channel_id=1, replica_groups=mesh['seq'=16,'head'=8,'dp'=4] {'head'}, dimensions={1} | all-to-all | bytes 1048576 | tf_op jit(solution)/shard_map/all_to_all | solution.py:260
  124.2 1.0 copy.23
  (51 shorter events, 5.4 us)
Async XLA Ops:
  0.0 2.2 %copy-start.5 = (bf16[128,2048]{1,0:T(8,128)(2,1)S(1)}, bf16[128,2048]{1,0:T(8,128)(2,1)}, u32[]{:S(2)}) copy-start(bf16[128,2048]{1,0:T(8,128)(2,1)} %param.8) | copy-start | bytes 1572868
  2.1 1.0 copy-start.6
  4.1 1.0 copy-start.1
  5.2 5.4 %copy-start.7 = (s32[32]{0:T(128)S(1)}, s32[32]{0:T(128)}, u32[]{:S(2)}) copy-start(s32[32]{0:T(128)} %param.11) | copy-start | bytes 388
  6.3 20.2 %all-to-all-start.1 = ((bf16[8,4,128,128]{2,3,1,0:T(8,128)(2,1)}), bf16[8,4,128,128]{2,3,1,0:T(8,128)(2,1)S(1)}, u32[]{:S(2)}, u32[]{:S(2)}) async-start(bf16[8,4,128,128]{2,3,1,0:T(8,128)(2,1)} %maximum_bitcast_fusion), calls=%async_computation.1 | async-start | bytes 2097152 | tf_op jit(solution)/shard_map/all_to_all | solution.py:194
  26.5 40.1 %all-to-all-start = ((bf16[8,4,128,64]{2,3,1,0:T(8,128)(2,1)}), bf16[8,4,128,64]{2,3,1,0:T(8,128)(2,1)S(1)}, u32[]{:S(2)}, u32[]{:S(2)}) async-start(bf16[8,4,128,64]{2,3,1,0:T(8,128)(2,1)} %fusion.1), calls=%async_computation | async-start | bytes 1048576 | tf_op jit(solution)/shard_map/all_to_all | solution.py:196
  30.7 38.3 %copy-start = (bf16[1,4,8,128,128]{4,3,2,1,0:T(8,128)(2,1)}, bf16[1,4,8,128,128]{4,3,2,1,0:T(8,128)(2,1)S(1)}, u32[]{:S(2)}) copy-start(bf16[1,4,8,128,128]{4,3,2,1,0:T(8,128)(2,1)S(1)} %copy.21) | copy-start | bytes 3145732
  31.9 24.8 %collective-permute-start.2 = (bf16[4,512,128]{2,1,0:T(8,128)(2,1)}, bf16[4,512,128]{2,1,0:T(8,128)(2,1)}, u32[]{:S(2)}, u32[]{:S(2)}) collective-permute-start(bf16[4,512,128]{2,1,0:T(8,128)(2,1)} %get-tuple-element.36), channel_id=1, source_target_pairs={{0,32},{32,64},{64,96},{96,128},{128,160},{160,192},{192,224},{224... | collective-permute-start | bytes 1572872 | tf_op jit(solution)/shard_map/ppermute | solution.py:22
  36.1 22.4 %collective-permute-start.4 = (bf16[4,512,128]{2,1,0:T(8,128)(2,1)}, bf16[4,512,128]{2,1,0:T(8,128)(2,1)}, u32[]{:S(2)}, u32[]{:S(2)}) collective-permute-start(bf16[4,512,128]{2,1,0:T(8,128)(2,1)} %get-tuple-element.37), channel_id=1, source_target_pairs={{32,0},{64,32},{96,64},{128,96},{160,128},{192,160},{224,192},{256... | collective-permute-start | bytes 1572872 | tf_op jit(solution)/shard_map/ppermute | solution.py:22
  47.3 50.9 %collective-permute-start = (bf16[4,512,128]{2,1,0:T(8,128)(2,1)}, bf16[4,512,128]{2,1,0:T(8,128)(2,1)S(1)}, u32[]{:S(2)}, u32[]{:S(2)}) collective-permute-start(bf16[4,512,128]{2,1,0:T(8,128)(2,1)} %get-tuple-element.37), channel_id=1, source_target_pairs={{0,32},{32,64},{64,96},{96,128},{128,160},{160,192},{192,224},{224... | collective-permute-start | bytes 1572872 | tf_op jit(solution)/shard_map/ppermute | solution.py:22
  49.2 49.0 %collective-permute-start.1 = (bf16[4,512,128]{2,1,0:T(8,128)(2,1)}, bf16[4,512,128]{2,1,0:T(8,128)(2,1)S(1)}, u32[]{:S(2)}, u32[]{:S(2)}) collective-permute-start(bf16[4,512,128]{2,1,0:T(8,128)(2,1)} %get-tuple-element.36), channel_id=1, source_target_pairs={{32,0},{64,32},{96,64},{128,96},{160,128},{192,160},{224,192},{256... | collective-permute-start | bytes 1572872 | tf_op jit(solution)/shard_map/ppermute | solution.py:22
  56.7 41.6 %collective-permute-start.3 = (bf16[4,512,128]{2,1,0:T(8,128)(2,1)}, bf16[4,512,128]{2,1,0:T(8,128)(2,1)S(1)}, u32[]{:S(2)}, u32[]{:S(2)}) collective-permute-start(bf16[4,512,128]{2,1,0:T(8,128)(2,1)} %collective-permute-done.2.rest_2_), channel_id=1, source_target_pairs={{0,32},{32,64},{64,96},{96,128},{128,160},{160,192},{192,224},{224... | collective-permute-start | bytes 1572872 | tf_op jit(solution)/shard_map/ppermute | solution.py:22
  58.6 39.7 %collective-permute-start.5 = (bf16[4,512,128]{2,1,0:T(8,128)(2,1)}, bf16[4,512,128]{2,1,0:T(8,128)(2,1)}, u32[]{:S(2)}, u32[]{:S(2)}) collective-permute-start(bf16[4,512,128]{2,1,0:T(8,128)(2,1)} %collective-permute-done.4.rest_4_), channel_id=1, source_target_pairs={{32,0},{64,32},{96,64},{128,96},{160,128},{192,160},{224,192},{256... | collective-permute-start | bytes 1572872 | tf_op jit(solution)/shard_map/ppermute | solution.py:22
  98.2 0.8 copy-start.2
  98.2 1.0 copy-start.3
  98.2 1.1 copy-start.4

commit v9 on v8

--- a/solution.py
+++ b/solution.py
@@ -75,15 +75,14 @@
         pad = jnp.zeros((tq, LANES - HD), jnp.bfloat16)
         qx = [jnp.concatenate([q_ref[h], pad], axis=1) for h in range(heads)]
         qs = jnp.tile(qs_ref[...], (1, TK // LANES))
-        ones = jnp.ones((TK, LANES), jnp.bfloat16)
-        two = 2 * LANES
+        v_lanes = lax.broadcasted_iota(jnp.int32, (TK, LANES), 1) >= HD
         if has_state:
             carry = tuple((m_in[h], acc_in[h]) for h in range(heads))
         else:
             carry = tuple(
                 (
                     jnp.full((tq, LANES), neg_big, jnp.float32),
-                    jnp.zeros((tq, two), jnp.float32),
+                    jnp.zeros((tq, LANES), jnp.float32),
                 )
                 for h in range(heads)
             )
@@ -106,10 +105,8 @@
                     p_w = jnp.exp(s - jnp.tile(m_new, (1, TK // LANES)))
                     alpha = jnp.exp(m - m_new)
                     pb = p_w.astype(jnp.bfloat16)
-                    rhs = jnp.concatenate([kvt, ones], axis=1)
-                    acc = jnp.tile(alpha, (1, 2)) * acc + jnp.dot(
-                        pb, rhs, preferred_element_type=jnp.float32
-                    )
+                    rhs = jnp.where(v_lanes, kvt, jnp.ones_like(kvt))
+                    acc = alpha * acc + jnp.dot(pb, rhs, preferred_element_type=jnp.float32)
                     new.append((m_new, acc))
                 return tuple(new)
 
@@ -117,7 +114,7 @@
         if finalize:
             for h in range(heads):
                 m, acc = carry[h]
-                outs[0][h] = (acc[:, HD:LANES] / acc[:, LANES + HD :]).astype(outs[0].dtype)
+                outs[0][h] = (acc[:, HD:] / acc[:, :HD]).astype(outs[0].dtype)
         else:
             for h in range(heads):
                 m, acc = carry[h]
@@ -143,12 +140,8 @@
         in_specs.append(pl.BlockSpec((heads, rows, LANES), lambda i, *_: (0, 0, 0)))
         in_specs.append(pl.BlockSpec((1, rows), lambda i, *_: (0, 0)))
         args += [kv, ks]
-    state_specs = [
-        pl.BlockSpec((heads, TQ, w), lambda i, *_: (0, i, 0)) for w in (LANES, 2 * LANES)
-    ]
-    state_shapes = [
-        jax.ShapeDtypeStruct((heads, qlen, w), jnp.float32) for w in (LANES, 2 * LANES)
-    ]
+    state_specs = [pl.BlockSpec((heads, TQ, LANES), lambda i, *_: (0, i, 0)) for _ in range(2)]
+    state_shapes = [jax.ShapeDtypeStruct((heads, qlen, LANES), jnp.float32) for _ in range(2)]
     if has_state:
         in_specs += state_specs
         args += list(state)

time: 126 us -> 125 us (level)
  the two profiles are of different devices: /device:TPU:56 before, /device:TPU:8 now
where the time goes in v9:
time: 125 us; the launch traced here: 123 us
  Pallas kernels  38.1 us (30%)
  starting transfers between devices  36.8 us (29%)
  blocking collectives  14.8 us (12%)
  waiting for transfers between devices  12.3 us (10%)
  local copies, waits for them, and re-layouts  11.9 us (10%)
  other arithmetic  9.2 us (7%)
    pallas_call x2, Pallas kernels, attend(): pl.pallas_call(kernel, out_shape=out_shape, grid_spec=pltpu.PrefetchScala...  38.1 us
    ppermute x6, starting transfers between devices, shifted(): return lax.ppermute(block, axis, route)  29 us
    all_to_all x1, blocking collectives, local(): lax.all_to_all(out_src, 'head', split_axis=1, concat_axis=0, tiled=True)  14.8 us
    all_to_all x1, waiting for transfers between devices, local(): kv = lax.all_to_all(kv_src, 'head', split_axis=0, concat_axis=2, tiled=True)  11.2 us
    all_to_all x1, starting transfers between devices, local(): kv = lax.all_to_all(kv_src, 'head', split_axis=0, concat_axis=2, tiled=True)  4.3 us
    select_n x7, other arithmetic, tables(): jnp.where(k_valid, scene_of(k_pos, scene_end), -1).astype(jnp.int32)  3.94 us
    unnamed x17, local copies, waits for them, and re-layouts  3.71 us
    all_to_all x1, starting transfers between devices, local(): q_h = lax.all_to_all(q_rot, 'head', split_axis=0, concat_axis=2, tiled=True)  3.49 us
  transfers between devices with their start and end apart: 8, of which 2 were waited for; matrix products, arithmetic and copies ran while one was open for 10% of the time, Pallas kernels for 20%

profile of v9, /device:TPU:8, one launch (start us, length us, event | category | flops | bytes accessed | tf_op | source)
XLA Modules:
  0.0 123.5 jit_solution(9585363519672917772)
XLA Ops:
  0.0 0.7 convert_element_type.63
  0.8 1.3 %copy.17 = bf16[128,2048]{0,1:T(8,128)(2,1)S(1)} copy(bf16[128,2048]{1,0:T(8,128)(2,1)} %param.7) | data formatting | bytes 1048576 | tf_op args[0]
  3.1 1.0 copy.20
  4.6 0.6 copy-done.1
  5.2 1.1 maximum_bitcast_fusion
  6.3 4.3 %all-to-all-start.1 = ((bf16[8,4,128,128]{2,3,1,0:T(8,128)(2,1)}), bf16[8,4,128,128]{2,3,1,0:T(8,128)(2,1)S(1)}, u32[]{:S(2)}, u32[]{:S(2)}) async-start(bf16[8,4,128,128]{2,3,1,0:T(8,128)(2,1)} %maximum_bitcast_fusion), calls=%async_computation.1 | async-start | bytes 2097152 | tf_op jit(solution)/shard_map/all_to_all | solution.py:187
  11.9 0.9 fusion.1
  12.8 0.6 gather_fusion.1
  13.5 0.6 gather_fusion
  14.6 0.6 and_select_fusion.3.rest_7_
  15.3 11.2 %all-to-all-done.1 = bf16[8,4,128,128]{2,3,1,0:T(8,128)(2,1)S(1)} async-done(((bf16[8,4,128,128]{2,3,1,0:T(8,128)(2,1)}), bf16[8,4,128,128]{2,3,1,0:T(8,128)(2,1)S(1)}, u32[]{:S(2)}, u32[]{:S(2)}) %all-to-all-start.1) | async-done | bytes 1048608 | tf_op jit(solution)/shard_map/all_to_all | solution.py:187
  26.5 3.5 %all-to-all-start = ((bf16[8,4,128,64]{2,3,1,0:T(8,128)(2,1)}), bf16[8,4,128,64]{2,3,1,0:T(8,128)(2,1)S(1)}, u32[]{:S(2)}, u32[]{:S(2)}) async-start(bf16[8,4,128,64]{2,3,1,0:T(8,128)(2,1)} %fusion.1), calls=%async_computation | async-start | bytes 1048576 | tf_op jit(solution)/shard_map/all_to_all | solution.py:189
  30.0 0.7 copy.21
  30.7 1.0 fusion.15
  31.7 4.3 %collective-permute-start.2 = (bf16[4,512,128]{2,1,0:T(8,128)(2,1)S(1)}, bf16[4,512,128]{2,1,0:T(8,128)(2,1)S(1)}, u32[]{:S(2)}, u32[]{:S(2)}) collective-permute-start(bf16[4,512,128]{2,1,0:T(8,128)(2,1)S(1)} %get-tuple-element.36), channel_id=1, source_target_pairs={{0,32},{32,64},{64,96},{96,128},{128,160},{160,192},{192,224},{224... | collective-permute-start | bytes 1572872 | tf_op jit(solution)/shard_map/ppermute | solution.py:22
  36.0 8.5 %collective-permute-start.4 = (bf16[4,512,128]{2,1,0:T(8,128)(2,1)}, bf16[4,512,128]{2,1,0:T(8,128)(2,1)S(1)}, u32[]{:S(2)}, u32[]{:S(2)}) collective-permute-start(bf16[4,512,128]{2,1,0:T(8,128)(2,1)} %get-tuple-element.37), channel_id=1, source_target_pairs={{32,0},{64,32},{96,64},{128,96},{160,128},{192,160},{224,192},{256... | collective-permute-start | bytes 1572872 | tf_op jit(solution)/shard_map/ppermute | solution.py:22
  44.5 0.7 pad_add_fusion.2
  46.2 1.9 %collective-permute-start = (bf16[4,512,128]{2,1,0:T(8,128)(2,1)}, bf16[4,512,128]{2,1,0:T(8,128)(2,1)}, u32[]{:S(2)}, u32[]{:S(2)}) collective-permute-start(bf16[4,512,128]{2,1,0:T(8,128)(2,1)} %get-tuple-element.37), channel_id=1, source_target_pairs={{0,32},{32,64},{64,96},{96,128},{128,160},{160,192},{192,224},{224... | collective-permute-start | bytes 1572872 | tf_op jit(solution)/shard_map/ppermute | solution.py:22
  48.2 6.0 %collective-permute-start.1 = (bf16[4,512,128]{2,1,0:T(8,128)(2,1)S(1)}, bf16[4,512,128]{2,1,0:T(8,128)(2,1)}, u32[]{:S(2)}, u32[]{:S(2)}) collective-permute-start(bf16[4,512,128]{2,1,0:T(8,128)(2,1)S(1)} %get-tuple-element.36), channel_id=1, source_target_pairs={{32,0},{64,32},{96,64},{128,96},{160,128},{192,160},{224,192},{256... | collective-permute-start | bytes 1572872 | tf_op jit(solution)/shard_map/ppermute | solution.py:22
  54.2 1.1 collective-permute-done.2.rest_2_
  55.3 1.9 %collective-permute-start.3 = (bf16[4,512,128]{2,1,0:T(8,128)(2,1)S(1)}, bf16[4,512,128]{2,1,0:T(8,128)(2,1)}, u32[]{:S(2)}, u32[]{:S(2)}) collective-permute-start(bf16[4,512,128]{2,1,0:T(8,128)(2,1)S(1)} %collective-permute-done.2.rest_2_), channel_id=1, source_target_pairs={{0,32},{32,64},{64,96},{96,128},{128,160},{160,192},{192,224},{224... | collective-permute-start | bytes 1572872 | tf_op jit(solution)/shard_map/ppermute | solution.py:22
  57.3 6.4 %collective-permute-start.5 = (bf16[4,512,128]{2,1,0:T(8,128)(2,1)S(1)}, bf16[4,512,128]{2,1,0:T(8,128)(2,1)}, u32[]{:S(2)}, u32[]{:S(2)}) collective-permute-start(bf16[4,512,128]{2,1,0:T(8,128)(2,1)S(1)} %collective-permute-done.4.rest_4_), channel_id=1, source_target_pairs={{32,0},{64,32},{96,64},{128,96},{160,128},{192,160},{224,192},{256... | collective-permute-start | bytes 1572872 | tf_op jit(solution)/shard_map/ppermute | solution.py:22
  63.7 0.7 pad_add_fusion
  64.3 0.6 and_select_fusion.6.rest_1_
  64.9 0.6 and_select_fusion.rest_1_
  65.5 1.3 %copy.18 = bf16[1,4,8,128,64]{4,3,2,1,0:T(8,128)(2,1)} copy(bf16[1,4,8,128,64]{3,4,1,2,0:T(8,128)(2,1)S(1)} %bitcast.53) | data formatting | bytes 1048576 | tf_op jit(solution)/shard_map/all_to_all | solution.py:189
  66.9 1.0 broadcast_in_dim.25.qs_ref
  67.9 24.2 %shard_map.55 = (f32[4,1024,128]{2,1,0:T(8,128)}, f32[4,1024,128]{2,1,0:T(8,128)}) custom-call(s32[12]{0:T(128)} %get-tuple-element.55.lo_ref, s32[12]{0:T(128)} %get-tuple-element.56.hi_ref, bf16[4,1024,64]{2,1,0:T(8,128)(2,1)} %bitcast.47, s32[1024,128]{1,0:T(8,128)} %broadcast_in_dim.25.qs_ref, bf16[4,1024,128]{2,1,0:T(8,128)(2,1)} %bitcast.46, ...), custom_call_target="tpu_custom_call" | custom-call | tf_op jit(solution)/shard_map/pallas_call | solution.py:154
  92.1 13.9 %shard_map.56 = bf16[4,1024,64]{2,1,0:T(8,128)(2,1)} custom-call(s32[16]{0:T(128)} %get-tuple-element.57.lo_ref, s32[16]{0:T(128)} %get-tuple-element.58.hi_ref, bf16[4,1024,64]{2,1,0:T(8,128)(2,1)} %bitcast.48, s32[1024,128]{1,0:T(8,128)} %broadcast_in_dim.25.qs_ref, bf16[4,512,128]{2,1,0:T(8,128)(2,1)} %collective-permute-done.rest_0_, ...), custom_call_target="tpu_custom_call" | custom-call | tf_op jit(solution)/shard_map/pallas_call | solution.py:154
  106.0 1.6 %copy.22 = bf16[4,8,128,64]{2,3,0,1:T(8,128)(2,1)S(1)} copy(bf16[4,8,128,64]{3,2,1,0:T(8,128)(2,1)} %bitcast.50) | data formatting | bytes 1048576 | tf_op jit(solution)/shard_map/reshape | solution.py:252
  107.6 14.8 %all_to_all.45 = bf16[4,8,128,64]{2,3,0,1:T(8,128)(2,1)S(1)} all-to-all(bf16[4,8,128,64]{2,3,0,1:T(8,128)(2,1)S(1)} %copy.22), channel_id=1, replica_groups=mesh['seq'=16,'head'=8,'dp'=4] {'head'}, dimensions={1} | all-to-all | bytes 1048576 | tf_op jit(solution)/shard_map/all_to_all | solution.py:253
  122.5 1.0 copy.23
  (49 shorter events, 4.5 us)
Async XLA Ops:
  0.0 2.2 %copy-start.2 = (bf16[128,2048]{1,0:T(8,128)(2,1)S(1)}, bf16[128,2048]{1,0:T(8,128)(2,1)}, u32[]{:S(2)}) copy-start(bf16[128,2048]{1,0:T(8,128)(2,1)} %param.8) | copy-start | bytes 1572868
  2.1 1.0 copy-start.3
  4.1 1.0 copy-start.1
  5.2 5.4 %copy-start.6 = (s32[32]{0:T(128)S(1)}, s32[32]{0:T(128)}, u32[]{:S(2)}) copy-start(s32[32]{0:T(128)} %param.11) | copy-start | bytes 388
  6.3 20.2 %all-to-all-start.1 = ((bf16[8,4,128,128]{2,3,1,0:T(8,128)(2,1)}), bf16[8,4,128,128]{2,3,1,0:T(8,128)(2,1)S(1)}, u32[]{:S(2)}, u32[]{:S(2)}) async-start(bf16[8,4,128,128]{2,3,1,0:T(8,128)(2,1)} %maximum_bitcast_fusion), calls=%async_computation.1 | async-start | bytes 2097152 | tf_op jit(solution)/shard_map/all_to_all | solution.py:187
  26.5 39.0 %all-to-all-start = ((bf16[8,4,128,64]{2,3,1,0:T(8,128)(2,1)}), bf16[8,4,128,64]{2,3,1,0:T(8,128)(2,1)S(1)}, u32[]{:S(2)}, u32[]{:S(2)}) async-start(bf16[8,4,128,64]{2,3,1,0:T(8,128)(2,1)} %fusion.1), calls=%async_computation | async-start | bytes 1048576 | tf_op jit(solution)/shard_map/all_to_all | solution.py:189
  30.7 37.2 %copy-start = (bf16[1,4,8,128,128]{4,3,2,1,0:T(8,128)(2,1)}, bf16[1,4,8,128,128]{4,3,2,1,0:T(8,128)(2,1)S(1)}, u32[]{:S(2)}) copy-start(bf16[1,4,8,128,128]{4,3,2,1,0:T(8,128)(2,1)S(1)} %copy.21) | copy-start | bytes 3145732
  31.7 23.6 %collective-permute-start.2 = (bf16[4,512,128]{2,1,0:T(8,128)(2,1)S(1)}, bf16[4,512,128]{2,1,0:T(8,128)(2,1)S(1)}, u32[]{:S(2)}, u32[]{:S(2)}) collective-permute-start(bf16[4,512,128]{2,1,0:T(8,128)(2,1)S(1)} %get-tuple-element.36), channel_id=1, source_target_pairs={{0,32},{32,64},{64,96},{96,128},{128,160},{160,192},{192,224},{224... | collective-permute-start | bytes 1572872 | tf_op jit(solution)/shard_map/ppermute | solution.py:22
  36.0 21.2 %collective-permute-start.4 = (bf16[4,512,128]{2,1,0:T(8,128)(2,1)}, bf16[4,512,128]{2,1,0:T(8,128)(2,1)S(1)}, u32[]{:S(2)}, u32[]{:S(2)}) collective-permute-start(bf16[4,512,128]{2,1,0:T(8,128)(2,1)} %get-tuple-element.37), channel_id=1, source_target_pairs={{32,0},{64,32},{96,64},{128,96},{160,128},{192,160},{224,192},{256... | collective-permute-start | bytes 1572872 | tf_op jit(solution)/shard_map/ppermute | solution.py:22
  46.2 45.9 %collective-permute-start = (bf16[4,512,128]{2,1,0:T(8,128)(2,1)}, bf16[4,512,128]{2,1,0:T(8,128)(2,1)}, u32[]{:S(2)}, u32[]{:S(2)}) collective-permute-start(bf16[4,512,128]{2,1,0:T(8,128)(2,1)} %get-tuple-element.37), channel_id=1, source_target_pairs={{0,32},{32,64},{64,96},{96,128},{128,160},{160,192},{192,224},{224... | collective-permute-start | bytes 1572872 | tf_op jit(solution)/shard_map/ppermute | solution.py:22
  48.2 43.9 %collective-permute-start.1 = (bf16[4,512,128]{2,1,0:T(8,128)(2,1)S(1)}, bf16[4,512,128]{2,1,0:T(8,128)(2,1)}, u32[]{:S(2)}, u32[]{:S(2)}) collective-permute-start(bf16[4,512,128]{2,1,0:T(8,128)(2,1)S(1)} %get-tuple-element.36), channel_id=1, source_target_pairs={{32,0},{64,32},{96,64},{128,96},{160,128},{192,160},{224,192},{256... | collective-permute-start | bytes 1572872 | tf_op jit(solution)/shard_map/ppermute | solution.py:22
  55.3 12.5 %copy-start.4 = (bf16[4,512,128]{2,1,0:T(8,128)(2,1)}, bf16[4,512,128]{2,1,0:T(8,128)(2,1)S(1)}, u32[]{:S(2)}) copy-start(bf16[4,512,128]{2,1,0:T(8,128)(2,1)S(1)} %collective-permute-done.2.rest_2_) | copy-start | bytes 1572868
  55.3 36.8 %collective-permute-start.3 = (bf16[4,512,128]{2,1,0:T(8,128)(2,1)S(1)}, bf16[4,512,128]{2,1,0:T(8,128)(2,1)}, u32[]{:S(2)}, u32[]{:S(2)}) collective-permute-start(bf16[4,512,128]{2,1,0:T(8,128)(2,1)S(1)} %collective-permute-done.2.rest_2_), channel_id=1, source_target_pairs={{0,32},{32,64},{64,96},{96,128},{128,160},{160,192},{192,224},{224... | collective-permute-start | bytes 1572872 | tf_op jit(solution)/shard_map/ppermute | solution.py:22
  57.3 10.6 %copy-start.5 = (bf16[4,512,128]{2,1,0:T(8,128)(2,1)}, bf16[4,512,128]{2,1,0:T(8,128)(2,1)S(1)}, u32[]{:S(2)}) copy-start(bf16[4,512,128]{2,1,0:T(8,128)(2,1)S(1)} %collective-permute-done.4.rest_4_) | copy-start | bytes 1572868
  57.3 34.9 %collective-permute-start.5 = (bf16[4,512,128]{2,1,0:T(8,128)(2,1)S(1)}, bf16[4,512,128]{2,1,0:T(8,128)(2,1)}, u32[]{:S(2)}, u32[]{:S(2)}) collective-permute-start(bf16[4,512,128]{2,1,0:T(8,128)(2,1)S(1)} %collective-permute-done.4.rest_4_), channel_id=1, source_target_pairs={{32,0},{64,32},{96,64},{128,96},{160,128},{192,160},{224,192},{256... | collective-permute-start | bytes 1572872 | tf_op jit(solution)/shard_map/ppermute | solution.py:22

commit v10 on v9

--- a/solution.py
+++ b/solution.py
@@ -74,7 +74,7 @@
         tq = q_ref.shape[1]
         pad = jnp.zeros((tq, LANES - HD), jnp.bfloat16)
         qx = [jnp.concatenate([q_ref[h], pad], axis=1) for h in range(heads)]
-        qs = jnp.tile(qs_ref[...], (1, TK // LANES))
+        qs = jnp.broadcast_to(qs_ref[...], (tq, TK))
         v_lanes = lax.broadcasted_iota(jnp.int32, (TK, LANES), 1) >= HD
         if has_state:
             carry = tuple((m_in[h], acc_in[h]) for h in range(heads))
@@ -132,7 +132,7 @@
     kernel = make_kernel(piece_rows, heads, nq, has_state, finalize, tk)
     in_specs = [
         pl.BlockSpec((heads, TQ, HD), lambda i, *_: (0, i, 0)),
-        pl.BlockSpec((TQ, LANES), lambda i, *_: (i, 0)),
+        pl.BlockSpec((TQ, 1), lambda i, *_: (i, 0)),
     ]
     args = [q_h, q_scene]
     for kv, ks in pieces:
@@ -237,7 +237,7 @@
             prepared,
         )
 
-    q_scene_col = jnp.broadcast_to(q_scene.astype(jnp.int32)[:, None], (group_len, LANES))
+    q_scene_col = q_scene.astype(jnp.int32).reshape(group_len, 1)
     if far_pieces:
         first = [(kv, 0), (below_hi, -far), (above_lo, group_len)]
         second = [(below_lo, -group_len), (above_hi, group_len + far)] + far_pieces

time: 125 us -> 128 us (1.024)
  the two profiles are of different devices: /device:TPU:8 before, /device:TPU:40 now
where the time goes in v10:
time: 128 us; the launch traced here: 127 us
  Pallas kernels  40.5 us (32%)
  starting transfers between devices  37.7 us (29%)
  blocking collectives  14.9 us (12%)
  waiting for transfers between devices  12.4 us (10%)
  local copies, waits for them, and re-layouts  12 us (9%)
  other arithmetic  9.07 us (7%)
    pallas_call x2, Pallas kernels, attend(): pl.pallas_call(kernel, out_shape=out_shape, grid_spec=pltpu.PrefetchScala...  40.5 us
    ppermute x6, starting transfers between devices, shifted(): return lax.ppermute(block, axis, route)  29.9 us
    all_to_all x1, blocking collectives, local(): lax.all_to_all(out_src, 'head', split_axis=1, concat_axis=0, tiled=True)  14.9 us
    all_to_all x1, waiting for transfers between devices, local(): kv = lax.all_to_all(kv_src, 'head', split_axis=0, concat_axis=2, tiled=True)  11.2 us
    all_to_all x1, starting transfers between devices, local(): kv = lax.all_to_all(kv_src, 'head', split_axis=0, concat_axis=2, tiled=True)  4.3 us
    select_n x7, other arithmetic, tables(): jnp.where(k_valid, scene_of(k_pos, scene_end), -1).astype(jnp.int32)  3.92 us
    unnamed x17, local copies, waits for them, and re-layouts  3.71 us
    all_to_all x1, starting transfers between devices, local(): q_h = lax.all_to_all(q_rot, 'head', split_axis=0, concat_axis=2, tiled=True)  3.49 us
  transfers between devices with their start and end apart: 8, of which 2 were waited for; matrix products, arithmetic and copies ran while one was open for 10% of the time, Pallas kernels for 18%

profile of v10, /device:TPU:40, one launch (start us, length us, event | category | flops | bytes accessed | tf_op | source)
XLA Modules:
  0.0 126.7 jit_solution(9034566377995928066)
XLA Ops:
  0.0 0.7 convert_element_type.63
  0.8 1.3 %copy.19 = bf16[128,2048]{0,1:T(8,128)(2,1)S(1)} copy(bf16[128,2048]{1,0:T(8,128)(2,1)} %param.7) | data formatting | bytes 1048576 | tf_op args[0]
  3.1 1.0 copy.22
  4.6 0.6 copy-done.1
  5.2 1.1 maximum_bitcast_fusion
  6.3 4.3 %all-to-all-start.1 = ((bf16[8,4,128,128]{2,3,1,0:T(8,128)(2,1)}), bf16[8,4,128,128]{2,3,1,0:T(8,128)(2,1)S(1)}, u32[]{:S(2)}, u32[]{:S(2)}) async-start(bf16[8,4,128,128]{2,3,1,0:T(8,128)(2,1)} %maximum_bitcast_fusion), calls=%async_computation.1 | async-start | bytes 2097152 | tf_op jit(solution)/shard_map/all_to_all | solution.py:187
  11.9 0.9 fusion.1
  12.8 0.6 gather_fusion.1
  13.5 0.6 gather_fusion
  15.3 11.2 %all-to-all-done.1 = bf16[8,4,128,128]{2,3,1,0:T(8,128)(2,1)S(1)} async-done(((bf16[8,4,128,128]{2,3,1,0:T(8,128)(2,1)}), bf16[8,4,128,128]{2,3,1,0:T(8,128)(2,1)S(1)}, u32[]{:S(2)}, u32[]{:S(2)}) %all-to-all-start.1) | async-done | bytes 1048608 | tf_op jit(solution)/shard_map/all_to_all | solution.py:187
  26.5 3.5 %all-to-all-start = ((bf16[8,4,128,64]{2,3,1,0:T(8,128)(2,1)}), bf16[8,4,128,64]{2,3,1,0:T(8,128)(2,1)S(1)}, u32[]{:S(2)}, u32[]{:S(2)}) async-start(bf16[8,4,128,64]{2,3,1,0:T(8,128)(2,1)} %fusion.1), calls=%async_computation | async-start | bytes 1048576 | tf_op jit(solution)/shard_map/all_to_all | solution.py:189
  30.0 0.7 copy.23
  30.7 1.0 fusion.15
  31.7 4.3 %collective-permute-start.2 = (bf16[4,512,128]{2,1,0:T(8,128)(2,1)S(1)}, bf16[4,512,128]{2,1,0:T(8,128)(2,1)S(1)}, u32[]{:S(2)}, u32[]{:S(2)}) collective-permute-start(bf16[4,512,128]{2,1,0:T(8,128)(2,1)S(1)} %get-tuple-element.36), channel_id=1, source_target_pairs={{0,32},{32,64},{64,96},{96,128},{128,160},{160,192},{192,224},{224... | collective-permute-start | bytes 1572872 | tf_op jit(solution)/shard_map/ppermute | solution.py:22
  36.0 9.4 %collective-permute-start.4 = (bf16[4,512,128]{2,1,0:T(8,128)(2,1)}, bf16[4,512,128]{2,1,0:T(8,128)(2,1)S(1)}, u32[]{:S(2)}, u32[]{:S(2)}) collective-permute-start(bf16[4,512,128]{2,1,0:T(8,128)(2,1)} %get-tuple-element.37), channel_id=1, source_target_pairs={{32,0},{64,32},{96,64},{128,96},{160,128},{192,160},{224,192},{256... | collective-permute-start | bytes 1572872 | tf_op jit(solution)/shard_map/ppermute | solution.py:22
  45.4 0.6 pad_add_fusion.2
  46.0 0.6 and_select_fusion.4.rest_5_
  46.6 0.5 and_select_fusion.5.rest_3_
  47.1 1.9 %collective-permute-start = (bf16[4,512,128]{2,1,0:T(8,128)(2,1)}, bf16[4,512,128]{2,1,0:T(8,128)(2,1)}, u32[]{:S(2)}, u32[]{:S(2)}) collective-permute-start(bf16[4,512,128]{2,1,0:T(8,128)(2,1)} %get-tuple-element.37), channel_id=1, source_target_pairs={{0,32},{32,64},{64,96},{96,128},{128,160},{160,192},{192,224},{224... | collective-permute-start | bytes 1572872 | tf_op jit(solution)/shard_map/ppermute | solution.py:22
  49.1 6.0 %collective-permute-start.1 = (bf16[4,512,128]{2,1,0:T(8,128)(2,1)S(1)}, bf16[4,512,128]{2,1,0:T(8,128)(2,1)}, u32[]{:S(2)}, u32[]{:S(2)}) collective-permute-start(bf16[4,512,128]{2,1,0:T(8,128)(2,1)S(1)} %get-tuple-element.36), channel_id=1, source_target_pairs={{32,0},{64,32},{96,64},{128,96},{160,128},{192,160},{224,192},{256... | collective-permute-start | bytes 1572872 | tf_op jit(solution)/shard_map/ppermute | solution.py:22
  55.1 1.1 collective-permute-done.2.rest_2_
  56.2 1.9 %collective-permute-start.3 = (bf16[4,512,128]{2,1,0:T(8,128)(2,1)S(1)}, bf16[4,512,128]{2,1,0:T(8,128)(2,1)}, u32[]{:S(2)}, u32[]{:S(2)}) collective-permute-start(bf16[4,512,128]{2,1,0:T(8,128)(2,1)S(1)} %collective-permute-done.2.rest_2_), channel_id=1, source_target_pairs={{0,32},{32,64},{64,96},{96,128},{128,160},{160,192},{192,224},{224... | collective-permute-start | bytes 1572872 | tf_op jit(solution)/shard_map/ppermute | solution.py:22
  58.2 6.4 %collective-permute-start.5 = (bf16[4,512,128]{2,1,0:T(8,128)(2,1)S(1)}, bf16[4,512,128]{2,1,0:T(8,128)(2,1)}, u32[]{:S(2)}, u32[]{:S(2)}) collective-permute-start(bf16[4,512,128]{2,1,0:T(8,128)(2,1)S(1)} %collective-permute-done.4.rest_4_), channel_id=1, source_target_pairs={{32,0},{64,32},{96,64},{128,96},{160,128},{192,160},{224,192},{256... | collective-permute-start | bytes 1572872 | tf_op jit(solution)/shard_map/ppermute | solution.py:22
  64.6 0.6 pad_add_fusion
  65.2 1.1 copy.25.qs_ref
  66.8 0.6 and_select_fusion.rest_1_
  67.4 1.3 %copy.20 = bf16[1,4,8,128,64]{4,3,2,1,0:T(8,128)(2,1)} copy(bf16[1,4,8,128,64]{3,4,1,2,0:T(8,128)(2,1)S(1)} %bitcast.54) | data formatting | bytes 1048576 | tf_op jit(solution)/shard_map/all_to_all | solution.py:189
  68.8 22.8 %shard_map.55 = (f32[4,1024,128]{2,1,0:T(8,128)}, f32[4,1024,128]{2,1,0:T(8,128)}) custom-call(s32[12]{0:T(128)} %get-tuple-element.55.lo_ref, s32[12]{0:T(128)} %get-tuple-element.56.hi_ref, bf16[4,1024,64]{2,1,0:T(8,128)(2,1)} %bitcast.48, s32[1024,1]{1,0:T(8,128)} %copy.25.qs_ref, bf16[4,1024,128]{2,1,0:T(8,128)(2,1)} %bitcast.47, ...), custom_call_target="tpu_custom_call" | custom-call | tf_op jit(solution)/shard_map/pallas_call | solution.py:154
  91.6 17.7 %shard_map.56 = bf16[4,1024,64]{2,1,0:T(8,128)(2,1)} custom-call(s32[16]{0:T(128)} %get-tuple-element.57.lo_ref, s32[16]{0:T(128)} %get-tuple-element.58.hi_ref, bf16[4,1024,64]{2,1,0:T(8,128)(2,1)} %bitcast.49, s32[1024,1]{1,0:T(8,128)} %copy.25.qs_ref, bf16[4,512,128]{2,1,0:T(8,128)(2,1)} %collective-permute-done.rest_0_, ...), custom_call_target="tpu_custom_call" | custom-call | tf_op jit(solution)/shard_map/pallas_call | solution.py:154
  109.3 1.6 %copy.26 = bf16[4,8,128,64]{2,3,0,1:T(8,128)(2,1)S(1)} copy(bf16[4,8,128,64]{3,2,1,0:T(8,128)(2,1)} %bitcast.51) | data formatting | bytes 1048576 | tf_op jit(solution)/shard_map/reshape | solution.py:252
  110.9 14.9 %all_to_all.45 = bf16[4,8,128,64]{2,3,0,1:T(8,128)(2,1)S(1)} all-to-all(bf16[4,8,128,64]{2,3,0,1:T(8,128)(2,1)S(1)} %copy.26), channel_id=1, replica_groups=mesh['seq'=16,'head'=8,'dp'=4] {'head'}, dimensions={1} | all-to-all | bytes 1048576 | tf_op jit(solution)/shard_map/all_to_all | solution.py:253
  125.7 1.0 copy.27
  (49 shorter events, 4.5 us)
Async XLA Ops:
  0.0 2.2 %copy-start.2 = (bf16[128,2048]{1,0:T(8,128)(2,1)S(1)}, bf16[128,2048]{1,0:T(8,128)(2,1)}, u32[]{:S(2)}) copy-start(bf16[128,2048]{1,0:T(8,128)(2,1)} %param.8) | copy-start | bytes 1572868
  2.1 1.0 copy-start.3
  4.1 1.0 copy-start.1
  5.2 5.4 %copy-start.6 = (s32[32]{0:T(128)S(1)}, s32[32]{0:T(128)}, u32[]{:S(2)}) copy-start(s32[32]{0:T(128)} %param.11) | copy-start | bytes 388
  6.3 20.2 %all-to-all-start.1 = ((bf16[8,4,128,128]{2,3,1,0:T(8,128)(2,1)}), bf16[8,4,128,128]{2,3,1,0:T(8,128)(2,1)S(1)}, u32[]{:S(2)}, u32[]{:S(2)}) async-start(bf16[8,4,128,128]{2,3,1,0:T(8,128)(2,1)} %maximum_bitcast_fusion), calls=%async_computation.1 | async-start | bytes 2097152 | tf_op jit(solution)/shard_map/all_to_all | solution.py:187
  26.5 40.9 %all-to-all-start = ((bf16[8,4,128,64]{2,3,1,0:T(8,128)(2,1)}), bf16[8,4,128,64]{2,3,1,0:T(8,128)(2,1)S(1)}, u32[]{:S(2)}, u32[]{:S(2)}) async-start(bf16[8,4,128,64]{2,3,1,0:T(8,128)(2,1)} %fusion.1), calls=%async_computation | async-start | bytes 1048576 | tf_op jit(solution)/shard_map/all_to_all | solution.py:189
  30.7 38.1 %copy-start = (bf16[1,4,8,128,128]{4,3,2,1,0:T(8,128)(2,1)}, bf16[1,4,8,128,128]{4,3,2,1,0:T(8,128)(2,1)S(1)}, u32[]{:S(2)}) copy-start(bf16[1,4,8,128,128]{4,3,2,1,0:T(8,128)(2,1)S(1)} %copy.23) | copy-start | bytes 3145732
  31.7 24.5 %collective-permute-start.2 = (bf16[4,512,128]{2,1,0:T(8,128)(2,1)S(1)}, bf16[4,512,128]{2,1,0:T(8,128)(2,1)S(1)}, u32[]{:S(2)}, u32[]{:S(2)}) collective-permute-start(bf16[4,512,128]{2,1,0:T(8,128)(2,1)S(1)} %get-tuple-element.36), channel_id=1, source_target_pairs={{0,32},{32,64},{64,96},{96,128},{128,160},{160,192},{192,224},{224... | collective-permute-start | bytes 1572872 | tf_op jit(solution)/shard_map/ppermute | solution.py:22
  36.0 22.1 %collective-permute-start.4 = (bf16[4,512,128]{2,1,0:T(8,128)(2,1)}, bf16[4,512,128]{2,1,0:T(8,128)(2,1)S(1)}, u32[]{:S(2)}, u32[]{:S(2)}) collective-permute-start(bf16[4,512,128]{2,1,0:T(8,128)(2,1)} %get-tuple-element.37), channel_id=1, source_target_pairs={{32,0},{64,32},{96,64},{128,96},{160,128},{192,160},{224,192},{256... | collective-permute-start | bytes 1572872 | tf_op jit(solution)/shard_map/ppermute | solution.py:22
  47.1 44.4 %collective-permute-start = (bf16[4,512,128]{2,1,0:T(8,128)(2,1)}, bf16[4,512,128]{2,1,0:T(8,128)(2,1)}, u32[]{:S(2)}, u32[]{:S(2)}) collective-permute-start(bf16[4,512,128]{2,1,0:T(8,128)(2,1)} %get-tuple-element.37), channel_id=1, source_target_pairs={{0,32},{32,64},{64,96},{96,128},{128,160},{160,192},{192,224},{224... | collective-permute-start | bytes 1572872 | tf_op jit(solution)/shard_map/ppermute | solution.py:22
  49.1 42.5 %collective-permute-start.1 = (bf16[4,512,128]{2,1,0:T(8,128)(2,1)S(1)}, bf16[4,512,128]{2,1,0:T(8,128)(2,1)}, u32[]{:S(2)}, u32[]{:S(2)}) collective-permute-start(bf16[4,512,128]{2,1,0:T(8,128)(2,1)S(1)} %get-tuple-element.36), channel_id=1, source_target_pairs={{32,0},{64,32},{96,64},{128,96},{160,128},{192,160},{224,192},{256... | collective-permute-start | bytes 1572872 | tf_op jit(solution)/shard_map/ppermute | solution.py:22
  56.2 12.5 %copy-start.4 = (bf16[4,512,128]{2,1,0:T(8,128)(2,1)}, bf16[4,512,128]{2,1,0:T(8,128)(2,1)S(1)}, u32[]{:S(2)}) copy-start(bf16[4,512,128]{2,1,0:T(8,128)(2,1)S(1)} %collective-permute-done.2.rest_2_) | copy-start | bytes 1572868
  56.2 35.3 %collective-permute-start.3 = (bf16[4,512,128]{2,1,0:T(8,128)(2,1)S(1)}, bf16[4,512,128]{2,1,0:T(8,128)(2,1)}, u32[]{:S(2)}, u32[]{:S(2)}) collective-permute-start(bf16[4,512,128]{2,1,0:T(8,128)(2,1)S(1)} %collective-permute-done.2.rest_2_), channel_id=1, source_target_pairs={{0,32},{32,64},{64,96},{96,128},{128,160},{160,192},{192,224},{224... | collective-permute-start | bytes 1572872 | tf_op jit(solution)/shard_map/ppermute | solution.py:22
  58.1 10.6 %copy-start.5 = (bf16[4,512,128]{2,1,0:T(8,128)(2,1)}, bf16[4,512,128]{2,1,0:T(8,128)(2,1)S(1)}, u32[]{:S(2)}) copy-start(bf16[4,512,128]{2,1,0:T(8,128)(2,1)S(1)} %collective-permute-done.4.rest_4_) | copy-start | bytes 1572868
  58.2 33.4 %collective-permute-start.5 = (bf16[4,512,128]{2,1,0:T(8,128)(2,1)S(1)}, bf16[4,512,128]{2,1,0:T(8,128)(2,1)}, u32[]{:S(2)}, u32[]{:S(2)}) collective-permute-start(bf16[4,512,128]{2,1,0:T(8,128)(2,1)S(1)} %collective-permute-done.4.rest_4_), channel_id=1, source_target_pairs={{32,0},{64,32},{96,64},{128,96},{160,128},{192,160},{224,192},{256... | collective-permute-start | bytes 1572872 | tf_op jit(solution)/shard_map/ppermute | solution.py:22
